TPU v7x, 32 devices: a whole 2x2x4 slice. The times are simulated.
32 devices in a mesh: ens: 8 (over z, y), col: 4 (over x, core).
Axes of the slice: x: 2, y: 2, z: 4, core: 2. Of those that a mesh axis runs over, the one named last changes fastest.
Arguments:
- state: float32 [256, 3, 8, 4096], P('ens', None, None, 'col'), may hold values from -4 to 4
- noise: float32 [256, 3, 8, 4096], P('ens', None, None, 'col'), may hold values from -1 to 1
- parents: int32 [256], replicated, may hold values from 0 to 255, as said below
Outputs:
- forecast: float32 [256, 3, 8, 4096], P('ens', None, None, 'col')
Inputs may be any that keep to these rules, and one draw needn't show every extreme that they name: Children are in aligned blocks of 32, parents likewise. For any block of children and any block of parents, at most 8 of those children have their parent in that block; in every block of children each block of parents that is used supplies exactly 8, and these 8 children have exactly 4 distinct parents, each the parent of two of them.
All inputs are finite; a program needn't handle non-finite values.
Results may differ from a plain program's by a relative error of at most 0.0003.
Values sent between devices are 32-bit elements; how exact they have to be, the bound alone decides.
No kernel may reach another device: no remote copies, remote signals or barrier semaphores. Data moves between devices by JAX's collectives and lax.ppermute only.
A program may use at most 128 MiB of HBM per device.

v0:
```python
import jax
import jax.numpy as jnp
from jax import lax
from jax.sharding import PartitionSpec as P

STEPS = 4


time_step = 0.3
coriolis = 0.2
gravity = 1.0


def extended(x, sides, width):
    for axis, dim in sides:
        count, length = (lax.axis_size(axis), x.shape[dim])
        up = [(i, (i + 1) % count) for i in range(count)]
        down = [(j, i) for i, j in up]
        last = lax.slice_in_dim(x, length - width, length, axis=dim)
        initial = lax.slice_in_dim(x, 0, width, axis=dim)
        before = lax.ppermute(last, axis, up)
        after = lax.ppermute(initial, axis, down)
        x = jnp.concatenate([before, x, after], axis=dim)
    return x


def diff_x(values):
    return 0.5 * (values[..., 2:] - values[..., :-2])


def diff_y(values):
    middle = values[..., 1:-1]
    return 0.5 * (jnp.roll(middle, -1, axis=-2) - jnp.roll(middle, 1, axis=-2))


def neighbour_mean(values):
    middle = values[..., 1:-1]
    return 0.25 * (
        values[..., 2:]
        + values[..., :-2]
        + jnp.roll(middle, -1, axis=-2)
        + jnp.roll(middle, 1, axis=-2)
    )


def advance(fields):
    surface = fields[:, 0]
    zonal = fields[:, 1]
    meridional = fields[:, 2]
    water_depth = 1.0 + surface
    centre_zonal = zonal[..., 1:-1]
    centre_merid = meridional[..., 1:-1]
    new_surface = neighbour_mean(surface) - time_step * (
        diff_x(water_depth * zonal) + diff_y(water_depth * meridional)
    )
    new_zonal = neighbour_mean(zonal) - time_step * (
        centre_zonal * diff_x(zonal)
        + centre_merid * diff_y(zonal)
        - coriolis * centre_merid
        + gravity * diff_x(surface)
    )
    new_merid = neighbour_mean(meridional) - time_step * (
        centre_zonal * diff_x(meridional)
        + centre_merid * diff_y(meridional)
        + coriolis * centre_zonal
        + gravity * diff_y(surface)
    )
    return jnp.stack([new_surface, new_zonal, new_merid], axis=1)


def shards(state, noise, parents):
    dev_count = lax.axis_size("ens")
    my_index = lax.axis_index("ens")
    per_dev = state.shape[0]
    slot_cap = max(2, 2 * ((per_dev + dev_count - 1) // dev_count))
    ancestor_blocks = parents.reshape(dev_count, per_dev)
    owner_of = ancestor_blocks // per_dev
    local_row = ancestor_blocks % per_dev
    device_ids = jnp.arange(dev_count, dtype=jnp.int32)
    onehot = (owner_of[:, :, None] == device_ids[None, None, :]).astype(jnp.int32)
    rank_of = jnp.sum(jnp.cumsum(onehot, axis=1) * onehot, axis=2) - 1
    slot_ids = jnp.arange(slot_cap, dtype=jnp.int32)
    is_match = (owner_of[:, None, :] == my_index) & (rank_of[:, None, :] == slot_ids[None, :, None])
    send_index = jnp.sum(is_match.astype(jnp.int32) * local_row[:, None, :], axis=2).reshape(-1)
    my_owner = lax.dynamic_index_in_dim(owner_of, my_index, 0, keepdims=False)
    my_rank = lax.dynamic_index_in_dim(rank_of, my_index, 0, keepdims=False)
    position = my_owner * slot_cap + my_rank
    outgoing = jnp.take(state, send_index, axis=0)
    incoming = lax.all_to_all(outgoing, "ens", split_axis=0, concat_axis=0, tiled=True)
    fields = jnp.take(incoming, position, axis=0) + noise
    for repeat in range(STEPS):
        fields = advance(extended(fields, (("col", 3),), 1))
    return fields


def solution(mesh):
    placed = (P("ens", None, None, "col"), P("ens", None, None, "col"), P())
    return jax.shard_map(
        shards, mesh=mesh, in_specs=placed, out_specs=P("ens", None, None, "col"), check_vma=False
    )
```

profile of v0, /device:TPU:0, one launch (start us, length us, event | category | flops | bytes accessed | tf_op | source)
XLA Modules:
  0.0 272.5 jit_solution(7964644737265246596)
XLA Ops:
  2.2 3.6 %gather_fusion = f32[64,3,8,1024]{3,2,1,0:T(8,128)} fusion(f32[32,3,8,1024]{3,2,1,0:T(8,128)S(1)} %copy-done, s32[1024]{0:T(1024)S(1)} %pad_clamp_fusion.1), kind=kCustom, calls=%fused_computation | custom fusion | bytes 12583168 | tf_op jit(solution)/shard_map/jit(_take)/gather | solution.py:88
  5.9 6.8 %broadcast_select_fusion = f32[64,3,8,1024]{3,2,1,0:T(8,128)} fusion(f32[64,3,8,1024]{3,2,1,0:T(8,128)} %gather_fusion, pred[64]{0:T(512)(128)(4,1)S(1)} %compare_and_fusion), kind=kLoop, calls=%fused_computation.7 | loop fusion | flops 1572864 | bytes 12582976 | tf_op jit(solution)/shard_map/jit(_take)/select_n | solution.py:88
  12.7 7.3 %all-to-all-start = ((f32[64,3,8,1024]{3,2,1,0:T(8,128)}), f32[64,3,8,1024]{3,2,1,0:T(8,128)}, u32[]{:S(2)}, u32[]{:S(2)}) async-start(f32[64,3,8,1024]{3,2,1,0:T(8,128)} %broadcast_select_fusion), calls=%async_computation | async-start | bytes 12582912 | tf_op jit(solution)/shard_map/all_to_all | solution.py:89
  20.0 138.2 %all-to-all-done = f32[64,3,8,1024]{3,2,1,0:T(8,128)} async-done(((f32[64,3,8,1024]{3,2,1,0:T(8,128)}), f32[64,3,8,1024]{3,2,1,0:T(8,128)}, u32[]{:S(2)}, u32[]{:S(2)}) %all-to-all-start) | async-done | bytes 6291488 | tf_op jit(solution)/shard_map/all_to_all | solution.py:89
  158.2 3.5 %gather_fusion.1 = f32[32,3,8,1024]{3,2,1,0:T(8,128)S(1)} fusion(f32[64,3,8,1024]{3,2,1,0:T(8,128)} %all-to-all-done, s32[1024]{0:T(1024)S(1)} %pad_clamp_fusion), kind=kCustom, calls=%fused_computation.1 | custom fusion | bytes 6291584 | tf_op jit(solution)/shard_map/jit(_take)/gather | solution.py:90
  161.7 2.7 select_add_fusion
  165.7 6.9 %collective-permute-done.1 = f32[32,3,8,1]{3,2,1,0:T(8,128)S(1)} collective-permute-done((f32[32,3,8,1]{3,2,1,0:T(8,128)S(1)}, f32[32,3,8,1]{3,2,1,0:T(8,128)S(1)}, u32[]{:S(2)}, u32[]{:S(2)}) %collective-permute-start.1) | collective-permute-done | bytes 3104 | tf_op jit(solution)/shard_map/ppermute | solution.py:22
  173.4 2.9 %collective-permute-done = f32[32,3,8,1]{3,2,1,0:T(8,128)} collective-permute-done((f32[32,3,8,1]{3,2,1,0:T(8,128)S(1)}, f32[32,3,8,1]{3,2,1,0:T(8,128)}, u32[]{:S(2)}, u32[]{:S(2)}) %collective-permute-start) | collective-permute-done | bytes 3104 | tf_op jit(solution)/shard_map/ppermute | solution.py:21
  176.2 3.8 %concatenate.134 = f32[32,3,8,1026]{3,2,1,0:T(8,128)S(1)} concatenate(f32[32,3,8,1]{3,2,1,0:T(8,128)} %collective-permute-done, f32[32,3,8,1024]{3,2,1,0:T(8,128)} %copy-done.3, f32[32,3,8,1]{3,2,1,0:T(8,128)} %copy-done.4), dimensions={3} | concatenate | bytes 6303744 | tf_op jit(solution)/shard_map/concatenate | solution.py:23
  186.8 1.4 subtract_bitcast_fusion.6
  189.3 2.0 pad_maximum_fusion
  193.3 7.2 %collective-permute-done.3 = f32[32,3,8,1]{3,2,0,1:T(8,128)S(1)} collective-permute-done((f32[32,3,8,1]{3,2,0,1:T(8,128)S(1)}, f32[32,3,8,1]{3,2,0,1:T(8,128)S(1)}, u32[]{:S(2)}, u32[]{:S(2)}) %collective-permute-start.3) | collective-permute-done | bytes 3104 | tf_op jit(solution)/shard_map/ppermute | solution.py:22
  201.3 2.8 %collective-permute-done.2 = f32[32,3,8,1]{3,2,0,1:T(8,128)} collective-permute-done((f32[32,3,8,1]{3,2,0,1:T(8,128)S(1)}, f32[32,3,8,1]{3,2,0,1:T(8,128)}, u32[]{:S(2)}, u32[]{:S(2)}) %collective-permute-start.2) | collective-permute-done | bytes 3104 | tf_op jit(solution)/shard_map/ppermute | solution.py:21
  204.1 3.8 %concatenate.143 = f32[32,3,8,1026]{3,2,0,1:T(8,128)S(1)} concatenate(f32[32,3,8,1]{3,2,0,1:T(8,128)} %collective-permute-done.2, f32[32,3,8,1024]{3,2,0,1:T(8,128)} %pad_maximum_fusion, f32[32,3,8,1]{3,2,0,1:T(8,128)} %copy-done.5), dimensions={3} | concatenate | bytes 6303744 | tf_op jit(solution)/shard_map/concatenate | solution.py:23
  214.6 1.4 subtract_bitcast_fusion.4
  217.2 2.0 pad_maximum_fusion.1
  221.6 6.2 %collective-permute-done.5 = f32[32,3,8,1]{3,2,0,1:T(8,128)S(1)} collective-permute-done((f32[32,3,8,1]{3,2,0,1:T(8,128)S(1)}, f32[32,3,8,1]{3,2,0,1:T(8,128)S(1)}, u32[]{:S(2)}, u32[]{:S(2)}) %collective-permute-start.5) | collective-permute-done | bytes 3104 | tf_op jit(solution)/shard_map/ppermute | solution.py:22
  228.6 3.0 %collective-permute-done.4 = f32[32,3,8,1]{3,2,0,1:T(8,128)} collective-permute-done((f32[32,3,8,1]{3,2,0,1:T(8,128)S(1)}, f32[32,3,8,1]{3,2,0,1:T(8,128)}, u32[]{:S(2)}, u32[]{:S(2)}) %collective-permute-start.4) | collective-permute-done | bytes 3104 | tf_op jit(solution)/shard_map/ppermute | solution.py:21
  231.5 3.8 %concatenate.152 = f32[32,3,8,1026]{3,2,0,1:T(8,128)S(1)} concatenate(f32[32,3,8,1]{3,2,0,1:T(8,128)} %collective-permute-done.4, f32[32,3,8,1024]{3,2,0,1:T(8,128)} %pad_maximum_fusion.1, f32[32,3,8,1]{3,2,0,1:T(8,128)} %copy-done.6), dimensions={3} | concatenate | bytes 6303744 | tf_op jit(solution)/shard_map/concatenate | solution.py:23
  245.2 1.5 collective-permute-start.6
  246.7 5.4 %collective-permute-done.7 = f32[32,3,8,1]{3,2,0,1:T(8,128)S(1)} collective-permute-done((f32[32,3,8,1]{3,2,0,1:T(8,128)S(1)}, f32[32,3,8,1]{3,2,0,1:T(8,128)S(1)}, u32[]{:S(2)}, u32[]{:S(2)}) %collective-permute-start.7) | collective-permute-done | bytes 3104 | tf_op jit(solution)/shard_map/ppermute | solution.py:22
  252.8 3.0 %collective-permute-done.6 = f32[32,3,8,1]{3,2,0,1:T(8,128)} collective-permute-done((f32[32,3,8,1]{3,2,0,1:T(8,128)S(1)}, f32[32,3,8,1]{3,2,0,1:T(8,128)}, u32[]{:S(2)}, u32[]{:S(2)}) %collective-permute-start.6) | collective-permute-done | bytes 3104 | tf_op jit(solution)/shard_map/ppermute | solution.py:21
  255.9 3.8 %concatenate.161 = f32[32,3,8,1026]{3,2,0,1:T(8,128)S(1)} concatenate(f32[32,3,8,1]{3,2,0,1:T(8,128)} %collective-permute-done.6, f32[32,3,8,1024]{3,2,0,1:T(8,128)} %copy-done.2, f32[32,3,8,1]{3,2,0,1:T(8,128)} %copy-done.7), dimensions={3} | concatenate | bytes 6303744 | tf_op jit(solution)/shard_map/concatenate | solution.py:23
  269.3 1.9 copy.42
  (94 shorter events, 46.8 us)
Async XLA Ops:
  0.0 2.2 copy-start
  12.7 145.5 %all-to-all-start = ((f32[64,3,8,1024]{3,2,1,0:T(8,128)}), f32[64,3,8,1024]{3,2,1,0:T(8,128)}, u32[]{:S(2)}, u32[]{:S(2)}) async-start(f32[64,3,8,1024]{3,2,1,0:T(8,128)} %broadcast_select_fusion), calls=%async_computation | async-start | bytes 12582912 | tf_op jit(solution)/shard_map/all_to_all | solution.py:89
  164.4 8.2 %copy-start.3 = (f32[32,3,8,1024]{3,2,1,0:T(8,128)}, f32[32,3,8,1024]{3,2,1,0:T(8,128)S(1)}, u32[]{:S(2)}) copy-start(f32[32,3,8,1024]{3,2,1,0:T(8,128)S(1)} %select_add_fusion) | copy-start | bytes 9437188
  164.6 8.0 %collective-permute-start.1 = (f32[32,3,8,1]{3,2,1,0:T(8,128)S(1)}, f32[32,3,8,1]{3,2,1,0:T(8,128)S(1)}, u32[]{:S(2)}, u32[]{:S(2)}) collective-permute-start(f32[32,3,8,1]{3,2,1,0:T(8,128)S(1)} %get-tuple-element.35), channel_id=1, source_target_pairs={{1,0},{2,1},{3,2},{0,3},{5,4},{6,5},{7,6},{4,7},{9,8},{10,9},{11,1... | collective-permute-start | bytes 9224 | tf_op jit(solution)/shard_map/ppermute | solution.py:22
  164.7 11.6 %collective-permute-start = (f32[32,3,8,1]{3,2,1,0:T(8,128)S(1)}, f32[32,3,8,1]{3,2,1,0:T(8,128)}, u32[]{:S(2)}, u32[]{:S(2)}) collective-permute-start(f32[32,3,8,1]{3,2,1,0:T(8,128)S(1)} %get-tuple-element.36), channel_id=1, source_target_pairs={{0,1},{1,2},{2,3},{3,0},{4,5},{5,6},{6,7},{7,4},{8,9},{9,10},{10,1... | collective-permute-start | bytes 9224 | tf_op jit(solution)/shard_map/ppermute | solution.py:21
  172.6 0.8 copy-start.4
  192.6 7.9 %collective-permute-start.3 = (f32[32,3,8,1]{3,2,0,1:T(8,128)S(1)}, f32[32,3,8,1]{3,2,0,1:T(8,128)S(1)}, u32[]{:S(2)}, u32[]{:S(2)}) collective-permute-start(f32[32,3,8,1]{3,2,0,1:T(8,128)S(1)} %get-tuple-element.33), channel_id=1, source_target_pairs={{1,0},{2,1},{3,2},{0,3},{5,4},{6,5},{7,6},{4,7},{9,8},{10,9},{11,1... | collective-permute-start | bytes 9224 | tf_op jit(solution)/shard_map/ppermute | solution.py:22
  192.7 11.4 %collective-permute-start.2 = (f32[32,3,8,1]{3,2,0,1:T(8,128)S(1)}, f32[32,3,8,1]{3,2,0,1:T(8,128)}, u32[]{:S(2)}, u32[]{:S(2)}) collective-permute-start(f32[32,3,8,1]{3,2,0,1:T(8,128)S(1)} %get-tuple-element.34), channel_id=1, source_target_pairs={{0,1},{1,2},{2,3},{3,0},{4,5},{5,6},{6,7},{7,4},{8,9},{9,10},{10,1... | collective-permute-start | bytes 9224 | tf_op jit(solution)/shard_map/ppermute | solution.py:21
  200.5 0.8 copy-start.5
  220.4 7.4 %collective-permute-start.5 = (f32[32,3,8,1]{3,2,0,1:T(8,128)S(1)}, f32[32,3,8,1]{3,2,0,1:T(8,128)S(1)}, u32[]{:S(2)}, u32[]{:S(2)}) collective-permute-start(f32[32,3,8,1]{3,2,0,1:T(8,128)S(1)} %get-tuple-element.31), channel_id=1, source_target_pairs={{1,0},{2,1},{3,2},{0,3},{5,4},{6,5},{7,6},{4,7},{9,8},{10,9},{11,1... | collective-permute-start | bytes 9224 | tf_op jit(solution)/shard_map/ppermute | solution.py:22
  220.5 11.0 %collective-permute-start.4 = (f32[32,3,8,1]{3,2,0,1:T(8,128)S(1)}, f32[32,3,8,1]{3,2,0,1:T(8,128)}, u32[]{:S(2)}, u32[]{:S(2)}) collective-permute-start(f32[32,3,8,1]{3,2,0,1:T(8,128)S(1)} %get-tuple-element.32), channel_id=1, source_target_pairs={{0,1},{1,2},{2,3},{3,0},{4,5},{5,6},{6,7},{7,4},{8,9},{9,10},{10,1... | collective-permute-start | bytes 9224 | tf_op jit(solution)/shard_map/ppermute | solution.py:21
  227.8 0.8 copy-start.6
  244.9 7.2 %copy-start.2 = (f32[32,3,8,1024]{3,2,0,1:T(8,128)}, f32[32,3,8,1024]{3,2,0,1:T(8,128)S(1)}, u32[]{:S(2)}) copy-start(f32[32,3,8,1024]{3,2,0,1:T(8,128)S(1)} %pad_maximum_fusion.2) | copy-start | bytes 9437188
  245.1 7.0 %collective-permute-start.7 = (f32[32,3,8,1]{3,2,0,1:T(8,128)S(1)}, f32[32,3,8,1]{3,2,0,1:T(8,128)S(1)}, u32[]{:S(2)}, u32[]{:S(2)}) collective-permute-start(f32[32,3,8,1]{3,2,0,1:T(8,128)S(1)} %get-tuple-element.29), channel_id=1, source_target_pairs={{1,0},{2,1},{3,2},{0,3},{5,4},{6,5},{7,6},{4,7},{9,8},{10,9},{11,1... | collective-permute-start | bytes 9224 | tf_op jit(solution)/shard_map/ppermute | solution.py:22
  245.2 10.7 %collective-permute-start.6 = (f32[32,3,8,1]{3,2,0,1:T(8,128)S(1)}, f32[32,3,8,1]{3,2,0,1:T(8,128)}, u32[]{:S(2)}, u32[]{:S(2)}) collective-permute-start(f32[32,3,8,1]{3,2,0,1:T(8,128)S(1)} %get-tuple-element.30), channel_id=1, source_target_pairs={{0,1},{1,2},{2,3},{3,0},{4,5},{5,6},{6,7},{7,4},{8,9},{9,10},{10,1... | collective-permute-start | bytes 9224 | tf_op jit(solution)/shard_map/ppermute | solution.py:21
  252.1 0.8 copy-start.7
  269.2 3.0 %copy-start.1 = (f32[32,3,8,1024]{3,2,1,0:T(8,128)S(1)}, f32[32,3,8,1024]{3,2,1,0:T(8,128)}, u32[]{:S(2)}) copy-start(f32[32,3,8,1024]{3,2,1,0:T(8,128)} %param.3) | copy-start | bytes 9437188
where the time goes:
time: 278 us; the launch traced here: 273 us
  waiting for transfers between devices  175 us (63%)
  local copies, waits for them, and re-layouts  53.4 us (19%)
  other arithmetic  31.2 us (11%)
  starting transfers between devices  11.8 us (4%)
    all_to_all x1, waiting for transfers between devices, shards(): lax.all_to_all(outgoing, 'ens', split_axis=0, concat_axis=0, tiled=True)  138 us
    ppermute x4, waiting for transfers between devices, extended(): after = lax.ppermute(initial, axis, down)  25.7 us
    another operation x16, other arithmetic, advance(): return jnp.stack([new_surface, new_zonal, new_merid], axis=1)  19.9 us
    concatenate x4, local copies, waits for them, and re-layouts, extended(): x = jnp.concatenate([before, x, after], axis=dim)  15.4 us
    slice x24, local copies, waits for them, and re-layouts, neighbour_mean(): jnp.roll(middle, -1, axis=-2)  14.8 us
    ppermute x4, waiting for transfers between devices, extended(): before = lax.ppermute(last, axis, up)  11.7 us
    all_to_all x1, starting transfers between devices, shards(): lax.all_to_all(outgoing, 'ens', split_axis=0, concat_axis=0, tiled=True)  7.28 us
    select_n x2, other arithmetic, shards(): outgoing = jnp.take(state, send_index, axis=0)  6.81 us
  transfers between devices with their start and end apart: 9, of which 9 were waited for; matrix products, arithmetic and copies ran while one was open for 0% of the time, Pallas kernels for 0%

commit v1 on v0

v1 whole, which is shorter than its diff:
```python
import jax
import jax.numpy as jnp
from jax import lax
from jax.experimental import pallas as pl
from jax.experimental.pallas import tpu as pltpu
from jax.sharding import PartitionSpec as P

STEPS = 4
LANES = 128

time_step = 0.3
coriolis = 0.2
gravity = 1.0


def routing(parents, count, per_dev, dist, me):
    blocks = parents.reshape(count, per_dev)
    owner = blocks // per_dev
    local = blocks % per_dev
    ids = jnp.arange(per_dev, dtype=jnp.int32)
    same = blocks[:, :, None] == blocks[:, None, :]
    earlier = ids[None, :] < ids[:, None]
    first = jnp.logical_not(jnp.any(same & earlier[None], axis=2))
    below = (
        (owner[:, :, None] == owner[:, None, :])
        & (blocks[:, None, :] < blocks[:, :, None])
        & first[:, None, :]
    )
    slot = jnp.sum(below.astype(jnp.int32), axis=2)
    slots = jnp.arange(dist, dtype=jnp.int32)
    pick = (owner == me)[:, None, :] & first[:, None, :] & (slot[:, None, :] == slots[None, :, None])
    send_index = jnp.sum(pick.astype(jnp.int32) * local[:, None, :], axis=2).reshape(-1)
    my_owner = lax.dynamic_index_in_dim(owner, me, 0, keepdims=False)
    my_slot = lax.dynamic_index_in_dim(slot, me, 0, keepdims=False)
    return send_index, my_owner * dist + my_slot


def advance(e, u, v):
    width = e.shape[-1]
    rows = e.shape[-2]

    def xp(a):
        return pltpu.roll(a, width - 1, 1)

    def xm(a):
        return pltpu.roll(a, 1, 1)

    def yp(a):
        return pltpu.roll(a, rows - 1, 0)

    def ym(a):
        return pltpu.roll(a, 1, 0)

    depth = 1.0 + e
    hu = depth * u
    hv = depth * v
    e_xp, e_xm, e_yp, e_ym = xp(e), xm(e), yp(e), ym(e)
    u_xp, u_xm, u_yp, u_ym = xp(u), xm(u), yp(u), ym(u)
    v_xp, v_xm, v_yp, v_ym = xp(v), xm(v), yp(v), ym(v)
    mean_e = 0.25 * (e_xp + e_xm + e_yp + e_ym)
    mean_u = 0.25 * (u_xp + u_xm + u_yp + u_ym)
    mean_v = 0.25 * (v_xp + v_xm + v_yp + v_ym)
    dx_hu = 0.5 * (xp(hu) - xm(hu))
    dy_hv = 0.5 * (yp(hv) - ym(hv))
    dx_e = 0.5 * (e_xp - e_xm)
    dy_e = 0.5 * (e_yp - e_ym)
    dx_u = 0.5 * (u_xp - u_xm)
    dy_u = 0.5 * (u_yp - u_ym)
    dx_v = 0.5 * (v_xp - v_xm)
    dy_v = 0.5 * (v_yp - v_ym)
    new_e = mean_e - time_step * (dx_hu + dy_hv)
    new_u = mean_u - time_step * (u * dx_u + v * dy_u - coriolis * v + gravity * dx_e)
    new_v = mean_v - time_step * (u * dx_v + v * dy_v + coriolis * u + gravity * dy_e)
    return new_e, new_u, new_v


def forecast_kernel(pos_ref, inc_ref, noise_ref, halo_ref, out_ref):
    cols = out_ref.shape[-1]
    fields = []
    for f in range(3):
        body = inc_ref[0, f] + noise_ref[0, f]
        fields.append(jnp.concatenate([body, halo_ref[0, f]], axis=-1))
    e, u, v = fields
    for _ in range(STEPS):
        e, u, v = advance(e, u, v)
    out_ref[0, 0] = e[:, :cols]
    out_ref[0, 1] = u[:, :cols]
    out_ref[0, 2] = v[:, :cols]


def forecast(position, incoming, noise, halo):
    per_dev, nf, rows, cols = noise.shape
    grid_spec = pltpu.PrefetchScalarGridSpec(
        num_scalar_prefetch=1,
        grid=(per_dev,),
        in_specs=[
            pl.BlockSpec((1, nf, rows, cols), lambda i, pos: (pos[i], 0, 0, 0)),
            pl.BlockSpec((1, nf, rows, cols), lambda i, pos: (i, 0, 0, 0)),
            pl.BlockSpec((1, nf, rows, LANES), lambda i, pos: (i, 0, 0, 0)),
        ],
        out_specs=pl.BlockSpec((1, nf, rows, cols), lambda i, pos: (i, 0, 0, 0)),
    )
    return pl.pallas_call(
        forecast_kernel,
        grid_spec=grid_spec,
        out_shape=jax.ShapeDtypeStruct(noise.shape, noise.dtype),
    )(position, incoming, noise, halo)


def shards(state, noise, parents):
    count = lax.axis_size("ens")
    me = lax.axis_index("ens")
    per_dev = state.shape[0]
    dist = max(1, -(-per_dev // count))
    send_index, position = routing(parents, count, per_dev, dist, me)
    outgoing = jnp.take(state, send_index, axis=0)
    incoming = lax.all_to_all(outgoing, "ens", split_axis=0, concat_axis=0, tiled=True)

    width = STEPS
    left_edge = jnp.take(incoming[..., :width], position, axis=0) + noise[..., :width]
    right_edge = jnp.take(incoming[..., -width:], position, axis=0) + noise[..., -width:]
    ring = lax.axis_size("col")
    from_left = lax.ppermute(right_edge, "col", [(i, (i + 1) % ring) for i in range(ring)])
    from_right = lax.ppermute(left_edge, "col", [(i, (i - 1) % ring) for i in range(ring)])
    gap = jnp.zeros(from_left.shape[:-1] + (LANES - 2 * width,), from_left.dtype)
    halo = jnp.concatenate([from_right, gap, from_left], axis=-1)
    return forecast(position, incoming, noise, halo)


def solution(mesh):
    placed = (P("ens", None, None, "col"), P("ens", None, None, "col"), P())
    return jax.shard_map(
        shards, mesh=mesh, in_specs=placed, out_specs=P("ens", None, None, "col"), check_vma=False
    )
```

time: 278 us -> 136 us (0.49); the launches traced: 273 us -> 135 us
  waiting for transfers between devices: 175 us -> 81.6 us
  local copies, waits for them, and re-layouts: 53.4 us -> 9.65 us
  Pallas kernels: 0 us -> 28.2 us
  other arithmetic: 31.2 us -> 7.37 us
  starting transfers between devices: 11.8 us -> 7.83 us
    all_to_all x1, waiting for transfers between devices: 138 us -> 70.8 us  [shards(): lax.all_to_all(outgoing, 'ens', split_axis=0, concat_axis=0, tiled=True)]
    pallas_call x0 -> x1, Pallas kernels: none -> 28.2 us  [forecast(): pl.pallas_call(forecast_kernel, grid_spec=grid_spec, out_shape=jax.ShapeD...]
    ppermute x8 -> x2, waiting for transfers between devices: 37.3 us -> 10.9 us  [the longest x1 7.95 us: shards(): lax.ppermute(left_edge, 'col', [(i, (i - 1) % ring) for i in range(ring)])]
    another operation x17 -> x0, other arithmetic: 20.6 us -> none  [the longest x16 19.9 us: advance(): return jnp.stack([new_surface, new_zonal, new_merid], axis=1)]
    slice x36 -> x1, local copies, waits for them, and re-layouts: 22.6 us -> 2.11 us  [shards(): incoming[..., :width]]
    concatenate x4 -> x1, local copies, waits for them, and re-layouts: 15.4 us -> 0.08 us  [shards(): halo = jnp.concatenate([from_right, gap, from_left], axis=-1)]
    unnamed x16 -> x4, local copies, waits for them, and re-layouts: 4.2 us -> 0.01 us
    ppermute x8 -> x2, starting transfers between devices: 4.55 us -> 0.55 us  [the longest x1 0.5 us: shards(): lax.ppermute(right_edge, 'col', [(i, (i + 1) % ring) for i in range(ring)])]
  transfers between devices with their start and end apart: 9 -> 3, of which waited for: 9 -> 3; matrix products, arithmetic and copies ran while one was open for 0% -> 0% of each run, Pallas kernels for 0% -> 0%
where the time goes in v1:
time: 136 us; the launch traced here: 135 us
  waiting for transfers between devices  81.6 us (60%)
  Pallas kernels  28.2 us (21%)
  local copies, waits for them, and re-layouts  9.65 us (7%)
  starting transfers between devices  7.83 us (6%)
  other arithmetic  7.37 us (5%)
    all_to_all x1, waiting for transfers between devices, shards(): lax.all_to_all(outgoing, 'ens', split_axis=0, concat_axis=0, tiled=True)  70.8 us
    pallas_call x1, Pallas kernels, forecast(): pl.pallas_call(forecast_kernel, grid_spec=grid_spec, out_shape=jax.ShapeD...  28.2 us
    ppermute x1, waiting for transfers between devices, shards(): lax.ppermute(left_edge, 'col', [(i, (i - 1) % ring) for i in range(ring)])  7.95 us
    all_to_all x1, starting transfers between devices, shards(): lax.all_to_all(outgoing, 'ens', split_axis=0, concat_axis=0, tiled=True)  7.28 us
    select_n x2, other arithmetic, shards(): outgoing = jnp.take(state, send_index, axis=0)  4.14 us
    ppermute x1, waiting for transfers between devices, shards(): lax.ppermute(right_edge, 'col', [(i, (i + 1) % ring) for i in range(ring)])  2.92 us
  transfers between devices with their start and end apart: 3, of which 3 were waited for; matrix products, arithmetic and copies ran while one was open for 0% of the time, Pallas kernels for 0%

profile of v1, /device:TPU:0, one launch (start us, length us, event | category | flops | bytes accessed | tf_op | source)
XLA Modules:
  0.0 134.8 jit_solution(11422766794325480917)
XLA Ops:
  0.0 0.0 copy-start
  0.0 0.9 reshape.159
  0.9 0.3 and_reduce_fusion
  1.3 0.3 convert_reduce_fusion
  1.6 0.2 select_reduce_fusion
  1.7 0.1 copy.4
  1.8 0.1 reshape.161
  1.9 0.1 reshape.160
  2.0 0.0 copy-done
  2.0 2.4 %gather_fusion = f32[32,3,8,1024]{3,2,1,0:T(8,128)} fusion(f32[32,3,8,1024]{3,2,1,0:T(8,128)S(1)} %copy-done, s32[1024]{0:T(1024)S(1)} %pad_clamp_fusion.1), kind=kCustom, calls=%fused_computation.2 | custom fusion | bytes 6291584 | tf_op jit(solution)/shard_map/jit(_take)/gather | solution.py:116
  4.5 4.1 %broadcast_select_fusion = f32[32,3,8,1024]{3,2,1,0:T(8,128)} fusion(f32[32,3,8,1024]{3,2,1,0:T(8,128)} %gather_fusion, pred[32]{0:T(512)(128)(4,1)S(1)} %compare_and_fusion.2), kind=kLoop, calls=%fused_computation.3 | loop fusion | flops 786432 | bytes 6291488 | tf_op jit(solution)/shard_map/jit(_take)/select_n | solution.py:116
  8.6 7.3 %all-to-all-start = ((f32[32,3,8,1024]{3,2,1,0:T(8,128)}), f32[32,3,8,1024]{3,2,1,0:T(8,128)}, u32[]{:S(2)}, u32[]{:S(2)}) async-start(f32[32,3,8,1024]{3,2,1,0:T(8,128)} %broadcast_select_fusion), calls=%async_computation | async-start | bytes 6291456 | tf_op jit(solution)/shard_map/all_to_all | solution.py:117
  15.9 70.8 %all-to-all-done.inc_ref = f32[32,3,8,1024]{3,2,1,0:T(8,128)} async-done(((f32[32,3,8,1024]{3,2,1,0:T(8,128)}), f32[32,3,8,1024]{3,2,1,0:T(8,128)}, u32[]{:S(2)}, u32[]{:S(2)}) %all-to-all-start) | async-done | bytes 3145760 | tf_op jit(solution)/shard_map/all_to_all | solution.py:117
  86.7 2.1 %fusion.4 = (f32[32,3,8,4]{3,2,1,0:T(8,128)}, f32[32,3,8,4]{3,2,1,0:T(8,128)}) fusion(f32[32,3,8,1024]{3,2,1,0:T(8,128)} %all-to-all-done.inc_ref), kind=kLoop, calls=%fused_computation.31 | loop fusion | bytes 49152 | tf_op jit(solution)/shard_map/slice | solution.py:120
  88.8 1.6 %gather_fusion.1 = f32[32,3,8,4]{3,2,1,0:T(8,128)S(1)} fusion(f32[32,3,8,4]{3,2,1,0:T(8,128)} %get-tuple-element.12, s32[1024]{0:T(1024)S(1)} %pad_clamp_fusion), kind=kCustom, calls=%fused_computation.clone | custom fusion | bytes 24704 | tf_op jit(solution)/shard_map/jit(_take)/gather | solution.py:120
  90.4 2.3 %gather_fusion.2 = f32[32,3,8,4]{3,2,1,0:T(8,128)} fusion(f32[32,3,8,4]{3,2,1,0:T(8,128)} %get-tuple-element.13, s32[1024]{0:T(1024)S(1)} %pad_clamp_fusion), kind=kCustom, calls=%fused_computation.1.clone | custom fusion | bytes 24704 | tf_op jit(solution)/shard_map/jit(_take)/gather | solution.py:121
  92.7 1.4 %select_add_fusion.1 = (f32[32,3,8,4]{3,2,1,0:T(8,128)S(1)}, f32[32,3,8,4]{3,2,1,0:T(8,128)S(1)}) fusion(f32[32,3,8,4]{3,2,1,0:T(8,128)S(1)} %gather_fusion.1, f32[32,3,8,1024]{3,2,1,0:T(8,128)} %noise_ref.1, pred[32]{0:T(512)(128)(4,1)S(1)} %get-tuple-element.6, f32[32,3,8,4]{3,2,1,0:T(8,128)} %gather_fusion.2), kind=kLoop, calls=%fused_computation.6 | loop fusion | flops 12288 | bytes 73760 | tf_op jit(solution)/shard_map/add | solution.py:120
  94.1 0.1 collective-permute-start
  94.2 0.5 collective-permute-start.1
  94.7 0.1 pad.1.clone
  94.8 8.0 %collective-permute-done = f32[32,3,8,4]{3,2,1,0:T(8,128)S(1)} collective-permute-done((f32[32,3,8,4]{3,2,1,0:T(8,128)S(1)}, f32[32,3,8,4]{3,2,1,0:T(8,128)S(1)}, u32[]{:S(2)}, u32[]{:S(2)}) %collective-permute-start) | collective-permute-done | bytes 12320 | tf_op jit(solution)/shard_map/ppermute | solution.py:124
  102.7 2.9 %collective-permute-done.1 = f32[32,3,8,4]{3,2,1,0:T(8,128)S(1)} collective-permute-done((f32[32,3,8,4]{3,2,1,0:T(8,128)S(1)}, f32[32,3,8,4]{3,2,1,0:T(8,128)S(1)}, u32[]{:S(2)}, u32[]{:S(2)}) %collective-permute-start.1) | collective-permute-done | bytes 12320 | tf_op jit(solution)/shard_map/ppermute | solution.py:123
  105.7 0.9 pad_maximum_fusion.halo_ref
  106.6 28.2 %shard_map.37 = f32[32,3,8,1024]{3,2,1,0:T(8,128)} custom-call(s32[32]{0:T(128)} %copy-done.1, f32[32,3,8,1024]{3,2,1,0:T(8,128)} %all-to-all-done.inc_ref, f32[32,3,8,1024]{3,2,1,0:T(8,128)} %noise_ref.1, f32[32,3,8,128]{3,2,1,0:T(8,128)} %pad_maximum_fusion.halo_ref), custom_call_target="tpu_custom_call" | custom-call | tf_op jit(solution)/shard_map/pallas_call | solution.py:103
  (12 shorter events, 0.1 us)
Async XLA Ops:
  0.0 2.0 %copy-start = (f32[32,3,8,1024]{3,2,1,0:T(8,128)S(1)}, f32[32,3,8,1024]{3,2,1,0:T(8,128)}, u32[]{:S(2)}) copy-start(f32[32,3,8,1024]{3,2,1,0:T(8,128)} %param.5) | copy-start | bytes 9437188
  8.6 78.1 %all-to-all-start = ((f32[32,3,8,1024]{3,2,1,0:T(8,128)}), f32[32,3,8,1024]{3,2,1,0:T(8,128)}, u32[]{:S(2)}, u32[]{:S(2)}) async-start(f32[32,3,8,1024]{3,2,1,0:T(8,128)} %broadcast_select_fusion), calls=%async_computation | async-start | bytes 6291456 | tf_op jit(solution)/shard_map/all_to_all | solution.py:117
  15.9 90.7 %copy-start.1 = (s32[32]{0:T(128)}, s32[32]{0:T(128)S(1)}, u32[]{:S(2)}) copy-start(s32[32]{0:T(128)S(1)} %get-tuple-element.7.pos_ref) | copy-start | bytes 388
  94.1 8.6 %collective-permute-start = (f32[32,3,8,4]{3,2,1,0:T(8,128)S(1)}, f32[32,3,8,4]{3,2,1,0:T(8,128)S(1)}, u32[]{:S(2)}, u32[]{:S(2)}) collective-permute-start(f32[32,3,8,4]{3,2,1,0:T(8,128)S(1)} %get-tuple-element.10), channel_id=1, source_target_pairs={{0,3},{1,0},{2,1},{3,2},{4,7},{5,4},{6,5},{7,6},{8,11},{9,8},{10,9... | collective-permute-start | bytes 36872 | tf_op jit(solution)/shard_map/ppermute | solution.py:124
  94.2 11.4 %collective-permute-start.1 = (f32[32,3,8,4]{3,2,1,0:T(8,128)S(1)}, f32[32,3,8,4]{3,2,1,0:T(8,128)S(1)}, u32[]{:S(2)}, u32[]{:S(2)}) collective-permute-start(f32[32,3,8,4]{3,2,1,0:T(8,128)S(1)} %get-tuple-element.11), channel_id=1, source_target_pairs={{0,1},{1,2},{2,3},{3,0},{4,5},{5,6},{6,7},{7,4},{8,9},{9,10},{10,1... | collective-permute-start | bytes 36872 | tf_op jit(solution)/shard_map/ppermute | solution.py:123

commit v2 on v1

v2 whole, which is shorter than its diff:
```python
import jax
import jax.numpy as jnp
from jax import lax
from jax.experimental import pallas as pl
from jax.experimental.pallas import tpu as pltpu
from jax.sharding import PartitionSpec as P

STEPS = 4
LANES = 128
BLOCK = 4

time_step = 0.3
coriolis = 0.2
gravity = 1.0


def routing(parents, count, per_dev, dist, me):
    blocks = parents.reshape(count, per_dev)
    owner = blocks // per_dev
    local = blocks % per_dev
    ids = jnp.arange(per_dev, dtype=jnp.int32)
    same = blocks[:, :, None] == blocks[:, None, :]
    earlier = ids[None, :] < ids[:, None]
    first = jnp.logical_not(jnp.any(same & earlier[None], axis=2))
    below = (
        (owner[:, :, None] == owner[:, None, :])
        & (blocks[:, None, :] < blocks[:, :, None])
        & first[:, None, :]
    )
    slot = jnp.sum(below.astype(jnp.int32), axis=2)
    slots = jnp.arange(dist, dtype=jnp.int32)
    pick = (owner == me)[:, None, :] & first[:, None, :] & (slot[:, None, :] == slots[None, :, None])
    send_index = jnp.sum(pick.astype(jnp.int32) * local[:, None, :], axis=2).reshape(-1)
    my_owner = lax.dynamic_index_in_dim(owner, me, 0, keepdims=False)
    my_slot = lax.dynamic_index_in_dim(slot, me, 0, keepdims=False)
    return send_index, my_owner * dist + my_slot


def sweep(src, dst, ncol):
    rows = src.shape[-2]
    lane = lax.broadcasted_iota(jnp.int32, (rows, LANES), 1)
    first_lane = lane == 0
    last_lane = lane == LANES - 1

    def load(j):
        window = pl.ds((j % ncol) * LANES, LANES)
        e = src[0, :, window]
        u = src[1, :, window]
        v = src[2, :, window]
        depth = 1.0 + e
        return e, u, v, depth

    def ahead(vals):
        e, u, v, depth = vals
        return tuple(pltpu.roll(a, LANES - 1, 1) for a in (e, u, v, depth * u))

    def behind(vals):
        e, u, v, depth = vals
        return tuple(pltpu.roll(a, 1, 1) for a in (e, u, v, depth * u))

    def yp(a):
        return pltpu.roll(a, rows - 1, 0)

    def ym(a):
        return pltpu.roll(a, 1, 0)

    here = load(0)
    prev_behind = behind(load(ncol - 1)) if ncol > 1 else behind(here)
    here_behind = behind(here)
    here_ahead = ahead(here)
    for j in range(ncol):
        if ncol > 1:
            nxt = load(j + 1)
            nxt_ahead = ahead(nxt)
            nxt_behind = behind(nxt)
        else:
            nxt, nxt_ahead, nxt_behind = here, here_ahead, here_behind
        xp = [jnp.where(last_lane, a, b) for a, b in zip(nxt_ahead, here_ahead)]
        xm = [jnp.where(first_lane, a, b) for a, b in zip(prev_behind, here_behind)]
        e, u, v, depth = here
        e_xp, u_xp, v_xp, hu_xp = xp
        e_xm, u_xm, v_xm, hu_xm = xm
        hv = depth * v
        e_yp, e_ym = yp(e), ym(e)
        u_yp, u_ym = yp(u), ym(u)
        v_yp, v_ym = yp(v), ym(v)
        hv_yp, hv_ym = yp(hv), ym(hv)
        half_step = 0.5 * time_step
        new_e = 0.25 * (e_xp + e_xm + e_yp + e_ym) - half_step * ((hu_xp - hu_xm) + (hv_yp - hv_ym))
        new_u = (
            0.25 * (u_xp + u_xm + u_yp + u_ym)
            - half_step * (u * (u_xp - u_xm) + v * (u_yp - u_ym) + gravity * (e_xp - e_xm))
            + (time_step * coriolis) * v
        )
        new_v = (
            0.25 * (v_xp + v_xm + v_yp + v_ym)
            - half_step * (u * (v_xp - v_xm) + v * (v_yp - v_ym) + gravity * (e_yp - e_ym))
            - (time_step * coriolis) * u
        )
        window = pl.ds(j * LANES, LANES)
        dst[0, :, window] = new_e
        dst[1, :, window] = new_u
        dst[2, :, window] = new_v
        prev_behind = here_behind
        here, here_behind, here_ahead = nxt, nxt_behind, nxt_ahead


def run_steps(src, out, first, second, ncol):
    chain = [src] + [first if s % 2 == 0 else second for s in range(STEPS - 1)] + [out]
    for s in range(STEPS):
        sweep(chain[s], chain[s + 1], ncol)


def main_kernel(ch_ref, out_ref, first, second):
    ncol = ch_ref.shape[-1] // LANES

    def particle(i, carry):
        run_steps(ch_ref.at[i], out_ref.at[i], first, second, ncol)
        return carry

    lax.fori_loop(0, ch_ref.shape[0], particle, 0)


def main_forecast(children):
    per_dev, nf, rows, cols = children.shape
    block = BLOCK if per_dev % BLOCK == 0 else 1
    spec = pl.BlockSpec((block, nf, rows, cols), lambda i: (i, 0, 0, 0))
    return pl.pallas_call(
        main_kernel,
        grid=(per_dev // block,),
        in_specs=[spec],
        out_specs=spec,
        out_shape=jax.ShapeDtypeStruct(children.shape, children.dtype),
        scratch_shapes=[pltpu.VMEM((nf, rows, cols), jnp.float32)] * 2,
    )(children)


def edge_kernel(lblk, rblk, from_left, from_right, body_ref, out_ref, packed, first, second, result):
    side = pl.program_id(0)
    rows = lblk.shape[-2]
    lane = lax.broadcasted_iota(jnp.int32, (rows, LANES), 1)
    half = LANES // 2
    width = STEPS

    @pl.when(side == 0)
    def _():
        def particle(i, carry):
            for f in range(3):
                left = jnp.where(lane >= LANES - width, from_left[i, f], lblk[i, f])
                right = jnp.where(lane < width, from_right[i, f], rblk[i, f])
                right = pltpu.roll(right, half, 1)
                keep_left = (lane < 2 * width) | (lane >= LANES - width)
                packed[f] = jnp.where(keep_left, left, right)
            run_steps(packed, result.at[i], first, second, 1)
            return carry

        lax.fori_loop(0, lblk.shape[0], particle, 0)
        out_ref[...] = jnp.where(lane < width, result[...], body_ref[...])

    @pl.when(side == 1)
    def _():
        def particle(i, carry):
            for f in range(3):
                out_ref[i, f] = jnp.where(
                    lane >= LANES - width, pltpu.roll(result[i, f], half, 1), body_ref[i, f]
                )
            return carry

        lax.fori_loop(0, lblk.shape[0], particle, 0)


def edge_fix(lblk, rblk, from_left, from_right, body):
    per_dev, nf, rows, cols = body.shape
    ncol = cols // LANES
    whole = pl.BlockSpec((per_dev, nf, rows, LANES), lambda s: (0, 0, 0, 0))
    edge = pl.BlockSpec((per_dev, nf, rows, LANES), lambda s: (0, 0, 0, s * (ncol - 1)))
    return pl.pallas_call(
        edge_kernel,
        grid=(2,),
        in_specs=[whole, whole, whole, whole, edge],
        out_specs=edge,
        out_shape=jax.ShapeDtypeStruct(body.shape, body.dtype),
        scratch_shapes=[
            pltpu.VMEM((nf, rows, LANES), jnp.float32),
            pltpu.VMEM((nf, rows, LANES), jnp.float32),
            pltpu.VMEM((nf, rows, LANES), jnp.float32),
            pltpu.VMEM((per_dev, nf, rows, LANES), jnp.float32),
        ],
        input_output_aliases={4: 0},
    )(lblk, rblk, from_left, from_right, body)


def shards(state, noise, parents):
    count = lax.axis_size("ens")
    me = lax.axis_index("ens")
    per_dev = state.shape[0]
    dist = max(1, -(-per_dev // count))
    send_index, position = routing(parents, count, per_dev, dist, me)
    outgoing = jnp.take(state, send_index, axis=0, mode="clip")
    incoming = lax.all_to_all(outgoing, "ens", split_axis=0, concat_axis=0, tiled=True)
    children = jnp.take(incoming, position, axis=0, mode="clip") + noise

    lblk = children[..., :LANES]
    rblk = children[..., -LANES:]
    ring = lax.axis_size("col")
    from_left = lax.ppermute(rblk, "col", [(i, (i + 1) % ring) for i in range(ring)])
    from_right = lax.ppermute(lblk, "col", [(i, (i - 1) % ring) for i in range(ring)])
    body = main_forecast(children)
    return edge_fix(lblk, rblk, from_left, from_right, body)


def solution(mesh):
    placed = (P("ens", None, None, "col"), P("ens", None, None, "col"), P())
    return jax.shard_map(
        shards, mesh=mesh, in_specs=placed, out_specs=P("ens", None, None, "col"), check_vma=False
    )
```

time: 136 us -> 133 us (0.978)
  waiting for transfers between devices: 81.6 us -> 70.8 us
  Pallas kernels: 28.2 us -> 37.7 us
  other arithmetic: 7.37 us -> 4.64 us
    ppermute x2, waiting for transfers between devices: 10.9 us -> 0.01 us  [the longest x1 0.01 us: shards(): lax.ppermute(rblk, 'col', [(i, (i + 1) % ring) for i in range(ring)])]
    pallas_call x1 -> x2, Pallas kernels: 28.2 us -> 37.7 us  [the longest x1 20.9 us: main_forecast(): pl.pallas_call(main_kernel, grid=(per_dev // block,), in_specs=[spec], ou...]
    select_n x3 -> x0, other arithmetic: 4.15 us -> none  [the longest x2 4.14 us: shards(): outgoing = jnp.take(state, send_index, axis=0)]
    add x1 -> x2, other arithmetic: 1.45 us -> 3.81 us  [the longest x1 3.8 us: shards(): children = jnp.take(incoming, position, axis=0, mode='clip') + noise]
    unnamed x4 -> x6, local copies, waits for them, and re-layouts: 0.01 us -> 1.66 us
    gather x3 -> x2, local copies, waits for them, and re-layouts: 6.29 us -> 6.71 us  [the longest x1 4.3 us: shards(): children = jnp.take(incoming, position, axis=0, mode='clip') + noise]
  transfers between devices with their start and end apart: 3 -> 3, of which waited for: 3 -> 1; matrix products, arithmetic and copies ran while one was open for 0% -> 0% of each run, Pallas kernels for 0% -> 16%
where the time goes in v2:
time: 133 us
  waiting for transfers between devices  70.8 us (53%)
  Pallas kernels  37.7 us (28%)
  local copies, waits for them, and re-layouts  10.3 us (8%)
  starting transfers between devices  9.03 us (7%)
  other arithmetic  4.64 us (3%)
    all_to_all x1, waiting for transfers between devices, shards(): lax.all_to_all(outgoing, 'ens', split_axis=0, concat_axis=0, tiled=True)  70.8 us
    pallas_call x1, Pallas kernels, main_forecast(): pl.pallas_call(main_kernel, grid=(per_dev // block,), in_specs=[spec], ou...  20.9 us
    pallas_call x1, Pallas kernels, edge_fix(): pl.pallas_call(edge_kernel, grid=(2,), in_specs=[whole, whole, whole, who...  16.9 us
    all_to_all x1, starting transfers between devices, shards(): lax.all_to_all(outgoing, 'ens', split_axis=0, concat_axis=0, tiled=True)  7.28 us
    gather x1, local copies, waits for them, and re-layouts, shards(): children = jnp.take(incoming, position, axis=0, mode='clip') + noise  4.3 us
    add x1, other arithmetic, shards(): children = jnp.take(incoming, position, axis=0, mode='clip') + noise  3.8 us
  transfers between devices with their start and end apart: 3, of which 1 were waited for; matrix products, arithmetic and copies ran while one was open for 0% of the time, Pallas kernels for 16%

profile of v2, /device:TPU:0, one launch (start us, length us, event | category | flops | bytes accessed | tf_op | source)
XLA Modules:
  0.0 132.5 jit_solution(13781225574844231314)
XLA Ops:
  0.0 0.0 copy-start
  0.0 0.9 reshape.137
  0.9 0.3 and_reduce_fusion
  1.3 0.3 convert_reduce_fusion
  1.6 0.2 select_reduce_fusion
  1.7 0.1 copy.5
  1.8 0.1 reshape.140
  1.9 0.0 copy-done
  1.9 2.4 %gather_fusion = f32[32,3,8,1024]{3,2,1,0:T(8,128)} fusion(f32[32,3,8,1024]{3,2,1,0:T(8,128)S(1)} %copy-done, s32[1024]{0:T(1024)S(1)} %pad_clamp_fusion.1), kind=kCustom, calls=%fused_computation | custom fusion | bytes 6291584 | tf_op jit(solution)/shard_map/jit(_take)/gather | solution.py:199
  4.3 7.3 %all-to-all-start = ((f32[32,3,8,1024]{3,2,1,0:T(8,128)}), f32[32,3,8,1024]{3,2,1,0:T(8,128)}, u32[]{:S(2)}, u32[]{:S(2)}) async-start(f32[32,3,8,1024]{3,2,1,0:T(8,128)} %gather_fusion), calls=%async_computation | async-start | bytes 6291456 | tf_op jit(solution)/shard_map/all_to_all | solution.py:200
  11.7 70.8 %all-to-all-done = f32[32,3,8,1024]{3,2,1,0:T(8,128)} async-done(((f32[32,3,8,1024]{3,2,1,0:T(8,128)}), f32[32,3,8,1024]{3,2,1,0:T(8,128)}, u32[]{:S(2)}, u32[]{:S(2)}) %all-to-all-start) | async-done | bytes 3145760 | tf_op jit(solution)/shard_map/all_to_all | solution.py:200
  82.4 4.3 %gather_fusion.1 = f32[32,3,8,1024]{3,2,1,0:T(8,128)} fusion(f32[32,3,8,1024]{3,2,1,0:T(8,128)} %all-to-all-done, s32[1024]{0:T(1024)S(1)} %pad_clamp_fusion), kind=kCustom, calls=%fused_computation.1 | custom fusion | bytes 6291584 | tf_op jit(solution)/shard_map/jit(_take)/gather | solution.py:201
  86.7 3.8 %add.47.ch_ref = f32[32,3,8,1024]{3,2,1,0:T(8,128)S(1)} add(f32[32,3,8,1024]{3,2,1,0:T(8,128)} %gather_fusion.1, f32[32,3,8,1024]{3,2,1,0:T(8,128)} %param.4) | non-fusion elementwise | flops 786432 | bytes 9437184 | tf_op jit(solution)/shard_map/add | solution.py:201
  90.6 0.0 copy-start.1
  90.6 1.7 %copy-done.1 = f32[32,3,8,1024]{3,2,1,0:T(8,128)} copy-done((f32[32,3,8,1024]{3,2,1,0:T(8,128)}, f32[32,3,8,1024]{3,2,1,0:T(8,128)S(1)}, u32[]{:S(2)}) %copy-start.1) | copy-done | bytes 3145752
  92.2 0.8 fusion.3
  93.0 0.0 copy-start.2
  93.0 0.0 collective-permute-start
  93.0 1.7 %collective-permute-start.1 = (f32[32,3,8,128]{3,2,1,0:T(8,128)}, f32[32,3,8,128]{3,2,1,0:T(8,128)}, u32[]{:S(2)}, u32[]{:S(2)}) collective-permute-start(f32[32,3,8,128]{3,2,1,0:T(8,128)} %get-tuple-element.8.lblk), channel_id=1, source_target_pairs={{0,3},{1,0},{2,1},{3,2},{4,7},{5,4},{6,5},{7,6},{8,11},{9,8},{10,9... | collective-permute-start | bytes 1179656 | tf_op jit(solution)/shard_map/ppermute | solution.py:207
  94.8 20.9 %shard_map.37.body_ref = f32[32,3,8,1024]{3,2,1,0:T(8,128)} custom-call(f32[32,3,8,1024]{3,2,1,0:T(8,128)} %copy-done.1), custom_call_target="tpu_custom_call" | custom-call | tf_op jit(solution)/shard_map/pallas_call | solution.py:128
  115.6 0.0 copy-done.2
  115.7 0.0 collective-permute-done.from_left
  115.7 0.0 collective-permute-done.1.from_right
  115.7 16.9 %shard_map.38 = f32[32,3,8,1024]{3,2,1,0:T(8,128)} custom-call(f32[32,3,8,128]{3,2,1,0:T(8,128)} %get-tuple-element.8.lblk, f32[32,3,8,128]{3,2,1,0:T(8,128)} %copy-done.2, f32[32,3,8,128]{3,2,1,0:T(8,128)} %collective-permute-done.from_left, f32[32,3,8,128]{3,2,1,0:T(8,128)} %collective-permute-done.1.from_right, ...), custom_call_target="tpu_custom_call", output_to_operand_aliasing={{}: (4, {})} | custom-call | tf_op jit(solution)/shard_map/pallas_call | solution.py:177
  (6 shorter events, 0.1 us)
Async XLA Ops:
  0.0 1.9 %copy-start = (f32[32,3,8,1024]{3,2,1,0:T(8,128)S(1)}, f32[32,3,8,1024]{3,2,1,0:T(8,128)}, u32[]{:S(2)}) copy-start(f32[32,3,8,1024]{3,2,1,0:T(8,128)} %param.3) | copy-start | bytes 9437188
  4.3 78.1 %all-to-all-start = ((f32[32,3,8,1024]{3,2,1,0:T(8,128)}), f32[32,3,8,1024]{3,2,1,0:T(8,128)}, u32[]{:S(2)}, u32[]{:S(2)}) async-start(f32[32,3,8,1024]{3,2,1,0:T(8,128)} %gather_fusion), calls=%async_computation | async-start | bytes 6291456 | tf_op jit(solution)/shard_map/all_to_all | solution.py:200
  90.6 1.7 %copy-start.1 = (f32[32,3,8,1024]{3,2,1,0:T(8,128)}, f32[32,3,8,1024]{3,2,1,0:T(8,128)S(1)}, u32[]{:S(2)}) copy-start(f32[32,3,8,1024]{3,2,1,0:T(8,128)S(1)} %add.47.ch_ref) | copy-start | bytes 9437188
  93.0 22.6 %copy-start.2 = (f32[32,3,8,128]{3,2,1,0:T(8,128)}, f32[32,3,8,128]{3,2,1,0:T(8,128)S(1)}, u32[]{:S(2)}) copy-start(f32[32,3,8,128]{3,2,1,0:T(8,128)S(1)} %get-tuple-element.7.rblk) | copy-start | bytes 1179652
  93.0 22.6 %collective-permute-start = (f32[32,3,8,128]{3,2,1,0:T(8,128)S(1)}, f32[32,3,8,128]{3,2,1,0:T(8,128)}, u32[]{:S(2)}, u32[]{:S(2)}) collective-permute-start(f32[32,3,8,128]{3,2,1,0:T(8,128)S(1)} %get-tuple-element.7.rblk), channel_id=1, source_target_pairs={{0,1},{1,2},{2,3},{3,0},{4,5},{5,6},{6,7},{7,4},{8,9},{9,10},{10,1... | collective-permute-start | bytes 1179656 | tf_op jit(solution)/shard_map/ppermute | solution.py:206
  93.0 22.6 %collective-permute-start.1 = (f32[32,3,8,128]{3,2,1,0:T(8,128)}, f32[32,3,8,128]{3,2,1,0:T(8,128)}, u32[]{:S(2)}, u32[]{:S(2)}) collective-permute-start(f32[32,3,8,128]{3,2,1,0:T(8,128)} %get-tuple-element.8.lblk), channel_id=1, source_target_pairs={{0,3},{1,0},{2,1},{3,2},{4,7},{5,4},{6,5},{7,6},{8,11},{9,8},{10,9... | collective-permute-start | bytes 1179656 | tf_op jit(solution)/shard_map/ppermute | solution.py:207

commit v3 on v2

--- a/solution.py
+++ b/solution.py
@@ -7,7 +7,8 @@
 
 STEPS = 4
 LANES = 128
-BLOCK = 4
+PAIR = 2
+EDGE_GROUP = 8
 
 time_step = 0.3
 coriolis = 0.2
@@ -36,7 +37,7 @@
     return send_index, my_owner * dist + my_slot
 
 
-def sweep(src, dst, ncol):
+def sweep(src, dst, ncol, extra=None):
     rows = src.shape[-2]
     lane = lax.broadcasted_iota(jnp.int32, (rows, LANES), 1)
     first_lane = lane == 0
@@ -47,6 +48,10 @@
         e = src[0, :, window]
         u = src[1, :, window]
         v = src[2, :, window]
+        if extra is not None:
+            e = e + extra[0, :, window]
+            u = u + extra[1, :, window]
+            v = v + extra[2, :, window]
         depth = 1.0 + e
         return e, u, v, depth
 
@@ -105,56 +110,75 @@
         here, here_behind, here_ahead = nxt, nxt_behind, nxt_ahead
 
 
-def run_steps(src, out, first, second, ncol):
-    chain = [src] + [first if s % 2 == 0 else second for s in range(STEPS - 1)] + [out]
+def run_steps(chains, extras, ncol):
     for s in range(STEPS):
-        sweep(chain[s], chain[s + 1], ncol)
-
-
-def main_kernel(ch_ref, out_ref, first, second):
-    ncol = ch_ref.shape[-1] // LANES
-
-    def particle(i, carry):
-        run_steps(ch_ref.at[i], out_ref.at[i], first, second, ncol)
-        return carry
-
-    lax.fori_loop(0, ch_ref.shape[0], particle, 0)
-
-
-def main_forecast(children):
-    per_dev, nf, rows, cols = children.shape
-    block = BLOCK if per_dev % BLOCK == 0 else 1
-    spec = pl.BlockSpec((block, nf, rows, cols), lambda i: (i, 0, 0, 0))
+        for chain, extra in zip(chains, extras):
+            sweep(chain[s], chain[s + 1], ncol, extra if s == 0 else None)
+
+
+def chain_of(src, out, first, second):
+    return [src] + [first if s % 2 == 0 else second for s in range(STEPS - 1)] + [out]
+
+
+def main_kernel(pos_ref, *refs):
+    incs = refs[:-4]
+    noise_ref, out_ref, first, second = refs[-4:]
+    ncol = noise_ref.shape[-1] // LANES
+    chains = [chain_of(incs[k].at[0], out_ref.at[k], first.at[k], second.at[k]) for k in range(len(incs))]
+    extras = [noise_ref.at[k] for k in range(len(incs))]
+    run_steps(chains, extras, ncol)
+
+
+def main_forecast(position, incoming, noise):
+    per_dev, nf, rows, cols = noise.shape
+    group = PAIR if per_dev % PAIR == 0 else 1
+
+    def row_map(k):
+        return lambda i, pos: (pos[i * group + k], 0, 0, 0)
+
+    in_specs = [pl.BlockSpec((1, nf, rows, cols), row_map(k)) for k in range(group)]
+    spec = pl.BlockSpec((group, nf, rows, cols), lambda i, pos: (i, 0, 0, 0))
+    grid_spec = pltpu.PrefetchScalarGridSpec(
+        num_scalar_prefetch=1,
+        grid=(per_dev // group,),
+        in_specs=in_specs + [spec],
+        out_specs=spec,
+        scratch_shapes=[pltpu.VMEM((group, nf, rows, cols), jnp.float32)] * 2,
+    )
     return pl.pallas_call(
         main_kernel,
-        grid=(per_dev // block,),
-        in_specs=[spec],
-        out_specs=spec,
-        out_shape=jax.ShapeDtypeStruct(children.shape, children.dtype),
-        scratch_shapes=[pltpu.VMEM((nf, rows, cols), jnp.float32)] * 2,
-    )(children)
+        grid_spec=grid_spec,
+        out_shape=jax.ShapeDtypeStruct(noise.shape, noise.dtype),
+    )(position, *([incoming] * group), noise)
 
 
 def edge_kernel(lblk, rblk, from_left, from_right, body_ref, out_ref, packed, first, second, result):
     side = pl.program_id(0)
     rows = lblk.shape[-2]
+    group = packed.shape[0]
     lane = lax.broadcasted_iota(jnp.int32, (rows, LANES), 1)
     half = LANES // 2
     width = STEPS
 
     @pl.when(side == 0)
     def _():
-        def particle(i, carry):
-            for f in range(3):
-                left = jnp.where(lane >= LANES - width, from_left[i, f], lblk[i, f])
-                right = jnp.where(lane < width, from_right[i, f], rblk[i, f])
-                right = pltpu.roll(right, half, 1)
-                keep_left = (lane < 2 * width) | (lane >= LANES - width)
-                packed[f] = jnp.where(keep_left, left, right)
-            run_steps(packed, result.at[i], first, second, 1)
+        def block(g, carry):
+            base = g * group
+            for k in range(group):
+                i = base + k
+                for f in range(3):
+                    left = jnp.where(lane >= LANES - width, from_left[i, f], lblk[i, f])
+                    right = jnp.where(lane < width, from_right[i, f], rblk[i, f])
+                    right = pltpu.roll(right, half, 1)
+                    keep_left = (lane < 2 * width) | (lane >= LANES - width)
+                    packed[k, f] = jnp.where(keep_left, left, right)
+            chains = [
+                chain_of(packed.at[k], result.at[base + k], first.at[k], second.at[k]) for k in range(group)
+            ]
+            run_steps(chains, [None] * group, 1)
             return carry
 
-        lax.fori_loop(0, lblk.shape[0], particle, 0)
+        lax.fori_loop(0, lblk.shape[0] // group, block, 0)
         out_ref[...] = jnp.where(lane < width, result[...], body_ref[...])
 
     @pl.when(side == 1)
@@ -172,6 +196,7 @@
 def edge_fix(lblk, rblk, from_left, from_right, body):
     per_dev, nf, rows, cols = body.shape
     ncol = cols // LANES
+    group = EDGE_GROUP if per_dev % EDGE_GROUP == 0 else 1
     whole = pl.BlockSpec((per_dev, nf, rows, LANES), lambda s: (0, 0, 0, 0))
     edge = pl.BlockSpec((per_dev, nf, rows, LANES), lambda s: (0, 0, 0, s * (ncol - 1)))
     return pl.pallas_call(
@@ -181,9 +206,9 @@
         out_specs=edge,
         out_shape=jax.ShapeDtypeStruct(body.shape, body.dtype),
         scratch_shapes=[
-            pltpu.VMEM((nf, rows, LANES), jnp.float32),
-            pltpu.VMEM((nf, rows, LANES), jnp.float32),
-            pltpu.VMEM((nf, rows, LANES), jnp.float32),
+            pltpu.VMEM((group, nf, rows, LANES), jnp.float32),
+            pltpu.VMEM((group, nf, rows, LANES), jnp.float32),
+            pltpu.VMEM((group, nf, rows, LANES), jnp.float32),
             pltpu.VMEM((per_dev, nf, rows, LANES), jnp.float32),
         ],
         input_output_aliases={4: 0},
@@ -198,14 +223,12 @@
     send_index, position = routing(parents, count, per_dev, dist, me)
     outgoing = jnp.take(state, send_index, axis=0, mode="clip")
     incoming = lax.all_to_all(outgoing, "ens", split_axis=0, concat_axis=0, tiled=True)
-    children = jnp.take(incoming, position, axis=0, mode="clip") + noise
-
-    lblk = children[..., :LANES]
-    rblk = children[..., -LANES:]
+    lblk = jnp.take(incoming[..., :LANES], position, axis=0, mode="clip") + noise[..., :LANES]
+    rblk = jnp.take(incoming[..., -LANES:], position, axis=0, mode="clip") + noise[..., -LANES:]
     ring = lax.axis_size("col")
     from_left = lax.ppermute(rblk, "col", [(i, (i + 1) % ring) for i in range(ring)])
     from_right = lax.ppermute(lblk, "col", [(i, (i - 1) % ring) for i in range(ring)])
-    body = main_forecast(children)
+    body = main_forecast(position, incoming, noise)
     return edge_fix(lblk, rblk, from_left, from_right, body)
 
 

time: 133 us -> 118 us (0.89)
  Pallas kernels: 37.7 us -> 23.8 us
  other arithmetic: 4.64 us -> 3.03 us
    pallas_call x1, Pallas kernels: 16.9 us -> 6.94 us  [edge_fix(): pl.pallas_call(edge_kernel, grid=(2,), in_specs=[whole, whole, whole, who...]
    pallas_call x1, Pallas kernels: 20.9 us -> 16.9 us  [main_forecast(): pl.pallas_call(main_kernel, grid_spec=grid_spec, out_shape=jax.ShapeDtype...]
    add x1, other arithmetic: 3.8 us -> 2.19 us  [shards(): jnp.take(incoming[..., -LANES:], position, axis=0, mode='clip')]
    gather x1 -> x2, local copies, waits for them, and re-layouts: 4.3 us -> 3.88 us  [the longest x1 2.31 us: shards(): jnp.take(incoming[..., :LANES], position, axis=0, mode='clip')]
  transfers between devices with their start and end apart: 3 -> 3, of which waited for: 1 -> 1; matrix products, arithmetic and copies ran while one was open for 0% -> 0% of each run, Pallas kernels for 16% -> 14%
where the time goes in v3:
time: 118 us; the launch traced here: 117 us
  waiting for transfers between devices  70.8 us (60%)
  Pallas kernels  23.8 us (20%)
  local copies, waits for them, and re-layouts  10.2 us (9%)
  starting transfers between devices  9.03 us (8%)
  other arithmetic  3.03 us (3%)
    all_to_all x1, waiting for transfers between devices, shards(): lax.all_to_all(outgoing, 'ens', split_axis=0, concat_axis=0, tiled=True)  70.8 us
    pallas_call x1, Pallas kernels, main_forecast(): pl.pallas_call(main_kernel, grid_spec=grid_spec, out_shape=jax.ShapeDtype...  16.9 us
    all_to_all x1, starting transfers between devices, shards(): lax.all_to_all(outgoing, 'ens', split_axis=0, concat_axis=0, tiled=True)  7.28 us
    pallas_call x1, Pallas kernels, edge_fix(): pl.pallas_call(edge_kernel, grid=(2,), in_specs=[whole, whole, whole, who...  6.94 us
    gather x1, local copies, waits for them, and re-layouts, shards(): outgoing = jnp.take(state, send_index, axis=0, mode='clip')  2.41 us
  transfers between devices with their start and end apart: 3, of which 1 were waited for; matrix products, arithmetic and copies ran while one was open for 0% of the time, Pallas kernels for 14%

profile of v3, /device:TPU:0, one launch (start us, length us, event | category | flops | bytes accessed | tf_op | source)
XLA Modules:
  0.0 116.9 jit_solution(16203307944311083695)
XLA Ops:
  0.0 0.0 copy-start
  0.0 0.9 reshape.140
  0.9 0.3 and_reduce_fusion
  1.3 0.3 convert_reduce_fusion
  1.6 0.2 select_reduce_fusion
  1.7 0.1 copy.5
  1.8 0.1 reshape.143
  1.9 0.0 copy-done
  1.9 2.4 %gather_fusion = f32[32,3,8,1024]{3,2,1,0:T(8,128)} fusion(f32[32,3,8,1024]{3,2,1,0:T(8,128)S(1)} %copy-done, s32[1024]{0:T(1024)S(1)} %pad_clamp_fusion.1), kind=kCustom, calls=%fused_computation | custom fusion | bytes 6291584 | tf_op jit(solution)/shard_map/jit(_take)/gather | solution.py:224
  4.3 7.3 %all-to-all-start = ((f32[32,3,8,1024]{3,2,1,0:T(8,128)}), f32[32,3,8,1024]{3,2,1,0:T(8,128)}, u32[]{:S(2)}, u32[]{:S(2)}) async-start(f32[32,3,8,1024]{3,2,1,0:T(8,128)} %gather_fusion), calls=%async_computation | async-start | bytes 6291456 | tf_op jit(solution)/shard_map/all_to_all | solution.py:225
  11.6 0.0 copy-start.2
  11.7 70.8 %all-to-all-done.refs_0_.refs_1_ = f32[32,3,8,1024]{3,2,1,0:T(8,128)} async-done(((f32[32,3,8,1024]{3,2,1,0:T(8,128)}), f32[32,3,8,1024]{3,2,1,0:T(8,128)}, u32[]{:S(2)}, u32[]{:S(2)}) %all-to-all-start) | async-done | bytes 3145760 | tf_op jit(solution)/shard_map/all_to_all | solution.py:225
  82.4 2.1 %fusion.3 = (f32[32,3,8,128]{3,2,1,0:T(8,128)}, f32[32,3,8,128]{3,2,1,0:T(8,128)}) fusion(f32[32,3,8,1024]{3,2,1,0:T(8,128)} %all-to-all-done.refs_0_.refs_1_), kind=kLoop, calls=%fused_computation.23 | loop fusion | bytes 1572864 | tf_op jit(solution)/shard_map/slice | solution.py:227
  84.5 1.6 %gather_fusion.2 = f32[32,3,8,128]{3,2,1,0:T(8,128)S(1)} fusion(f32[32,3,8,128]{3,2,1,0:T(8,128)} %get-tuple-element.9, s32[1024]{0:T(1024)S(1)} %pad_clamp_fusion), kind=kCustom, calls=%fused_computation.2 | custom fusion | bytes 786560 | tf_op jit(solution)/shard_map/jit(_take)/gather | solution.py:227
  86.1 2.3 %gather_fusion.1 = f32[32,3,8,128]{3,2,1,0:T(8,128)} fusion(f32[32,3,8,128]{3,2,1,0:T(8,128)} %get-tuple-element.10, s32[1024]{0:T(1024)S(1)} %pad_clamp_fusion), kind=kCustom, calls=%fused_computation.1 | custom fusion | bytes 786560 | tf_op jit(solution)/shard_map/jit(_take)/gather | solution.py:226
  88.4 2.2 %slice_add_fusion = (f32[32,3,8,128]{3,2,1,0:T(8,128)}, f32[32,3,8,128]{3,2,1,0:T(8,128)}) fusion(f32[32,3,8,128]{3,2,1,0:T(8,128)S(1)} %gather_fusion.2, f32[32,3,8,1024]{3,2,1,0:T(8,128)} %refs_2_.1, f32[32,3,8,128]{3,2,1,0:T(8,128)} %gather_fusion.1), kind=kLoop, calls=%fused_computation.3 | loop fusion | flops 196608 | bytes 2359296 | tf_op jit(solution)/shard_map/add | solution.py:227
  90.6 0.0 collective-permute-start
  90.6 1.7 %collective-permute-start.1 = (f32[32,3,8,128]{3,2,1,0:T(8,128)}, f32[32,3,8,128]{3,2,1,0:T(8,128)}, u32[]{:S(2)}, u32[]{:S(2)}) collective-permute-start(f32[32,3,8,128]{3,2,1,0:T(8,128)} %get-tuple-element.8.lblk), channel_id=1, source_target_pairs={{0,3},{1,0},{2,1},{3,2},{4,7},{5,4},{6,5},{7,6},{8,11},{9,8},{10,9... | collective-permute-start | bytes 1179656 | tf_op jit(solution)/shard_map/ppermute | solution.py:230
  92.3 0.0 copy-done.2
  92.3 16.9 %shard_map.37.body_ref = f32[32,3,8,1024]{3,2,1,0:T(8,128)} custom-call(s32[32]{0:T(128)} %copy-done.2, f32[32,3,8,1024]{3,2,1,0:T(8,128)} %all-to-all-done.refs_0_.refs_1_, f32[32,3,8,1024]{3,2,1,0:T(8,128)} %all-to-all-done.refs_0_.refs_1_, f32[32,3,8,1024]{3,2,1,0:T(8,128)} %refs_2_.1), custom_call_target="tpu_custom_call" | custom-call | tf_op jit(solution)/shard_map/pallas_call | solution.py:148
  109.2 0.0 collective-permute-done.from_left
  109.2 0.0 collective-permute-done.1.from_right
  109.2 0.7 copy-done.1
  109.9 6.9 %shard_map.38 = f32[32,3,8,1024]{3,2,1,0:T(8,128)} custom-call(f32[32,3,8,128]{3,2,1,0:T(8,128)} %get-tuple-element.8.lblk, f32[32,3,8,128]{3,2,1,0:T(8,128)} %get-tuple-element.7.rblk, f32[32,3,8,128]{3,2,1,0:T(8,128)} %copy-done.1, f32[32,3,8,128]{3,2,1,0:T(8,128)} %collective-permute-done.1.from_right, ...), custom_call_target="tpu_custom_call", output_to_operand_aliasing={{}: (4, {})} | custom-call | tf_op jit(solution)/shard_map/pallas_call | solution.py:202
  (7 shorter events, 0.1 us)
Async XLA Ops:
  0.0 1.9 %copy-start = (f32[32,3,8,1024]{3,2,1,0:T(8,128)S(1)}, f32[32,3,8,1024]{3,2,1,0:T(8,128)}, u32[]{:S(2)}) copy-start(f32[32,3,8,1024]{3,2,1,0:T(8,128)} %param.3) | copy-start | bytes 9437188
  4.3 78.1 %all-to-all-start = ((f32[32,3,8,1024]{3,2,1,0:T(8,128)}), f32[32,3,8,1024]{3,2,1,0:T(8,128)}, u32[]{:S(2)}, u32[]{:S(2)}) async-start(f32[32,3,8,1024]{3,2,1,0:T(8,128)} %gather_fusion), calls=%async_computation | async-start | bytes 6291456 | tf_op jit(solution)/shard_map/all_to_all | solution.py:225
  11.6 80.7 %copy-start.2 = (s32[32]{0:T(128)}, s32[32]{0:T(128)S(1)}, u32[]{:S(2)}) copy-start(s32[32]{0:T(128)S(1)} %add_bitcast_fusion.pos_ref) | copy-start | bytes 388
  90.6 18.6 %collective-permute-start = (f32[32,3,8,128]{3,2,1,0:T(8,128)}, f32[32,3,8,128]{3,2,1,0:T(8,128)S(1)}, u32[]{:S(2)}, u32[]{:S(2)}) collective-permute-start(f32[32,3,8,128]{3,2,1,0:T(8,128)} %get-tuple-element.7.rblk), channel_id=1, source_target_pairs={{0,1},{1,2},{2,3},{3,0},{4,5},{5,6},{6,7},{7,4},{8,9},{9,10},{10,1... | collective-permute-start | bytes 1179656 | tf_op jit(solution)/shard_map/ppermute | solution.py:229
  90.6 18.6 %collective-permute-start.1 = (f32[32,3,8,128]{3,2,1,0:T(8,128)}, f32[32,3,8,128]{3,2,1,0:T(8,128)}, u32[]{:S(2)}, u32[]{:S(2)}) collective-permute-start(f32[32,3,8,128]{3,2,1,0:T(8,128)} %get-tuple-element.8.lblk), channel_id=1, source_target_pairs={{0,3},{1,0},{2,1},{3,2},{4,7},{5,4},{6,5},{7,6},{8,11},{9,8},{10,9... | collective-permute-start | bytes 1179656 | tf_op jit(solution)/shard_map/ppermute | solution.py:230
  109.2 0.7 copy-start.1

commit v4 on v3

--- a/solution.py
+++ b/solution.py
@@ -8,7 +8,8 @@
 STEPS = 4
 LANES = 128
 PAIR = 2
-EDGE_GROUP = 8
+EDGE_GROUP = 32
+GATHER_GROUP = 8
 
 time_step = 0.3
 coriolis = 0.2
@@ -152,6 +153,42 @@
     )(position, *([incoming] * group), noise)
 
 
+def edges_kernel(pos_ref, *refs):
+    group = (len(refs) - 4) // 2
+    left_rows, right_rows = refs[:group], refs[group:2 * group]
+    noise_left, noise_right, lblk, rblk = refs[2 * group:]
+    for k in range(group):
+        lblk[k] = left_rows[k][0] + noise_left[k]
+        rblk[k] = right_rows[k][0] + noise_right[k]
+
+
+def edge_blocks(position, incoming, noise):
+    per_dev, nf, rows, cols = noise.shape
+    last = cols // LANES - 1
+    group = GATHER_GROUP if per_dev % GATHER_GROUP == 0 else 1
+
+    def row_map(k, col):
+        return lambda i, pos: (pos[i * group + k], 0, 0, col)
+
+    left_specs = [pl.BlockSpec((1, nf, rows, LANES), row_map(k, 0)) for k in range(group)]
+    right_specs = [pl.BlockSpec((1, nf, rows, LANES), row_map(k, last)) for k in range(group)]
+    left = pl.BlockSpec((group, nf, rows, LANES), lambda i, pos: (i, 0, 0, 0))
+    right = pl.BlockSpec((group, nf, rows, LANES), lambda i, pos: (i, 0, 0, last))
+    out = pl.BlockSpec((group, nf, rows, LANES), lambda i, pos: (i, 0, 0, 0))
+    edge_shape = jax.ShapeDtypeStruct((per_dev, nf, rows, LANES), noise.dtype)
+    grid_spec = pltpu.PrefetchScalarGridSpec(
+        num_scalar_prefetch=1,
+        grid=(per_dev // group,),
+        in_specs=left_specs + right_specs + [left, right],
+        out_specs=[out, out],
+    )
+    return pl.pallas_call(
+        edges_kernel,
+        grid_spec=grid_spec,
+        out_shape=[edge_shape, edge_shape],
+    )(position, *([incoming] * (2 * group)), noise, noise)
+
+
 def edge_kernel(lblk, rblk, from_left, from_right, body_ref, out_ref, packed, first, second, result):
     side = pl.program_id(0)
     rows = lblk.shape[-2]
@@ -223,8 +260,7 @@
     send_index, position = routing(parents, count, per_dev, dist, me)
     outgoing = jnp.take(state, send_index, axis=0, mode="clip")
     incoming = lax.all_to_all(outgoing, "ens", split_axis=0, concat_axis=0, tiled=True)
-    lblk = jnp.take(incoming[..., :LANES], position, axis=0, mode="clip") + noise[..., :LANES]
-    rblk = jnp.take(incoming[..., -LANES:], position, axis=0, mode="clip") + noise[..., -LANES:]
+    lblk, rblk = edge_blocks(position, incoming, noise)
     ring = lax.axis_size("col")
     from_left = lax.ppermute(rblk, "col", [(i, (i + 1) % ring) for i in range(ring)])
     from_right = lax.ppermute(lblk, "col", [(i, (i - 1) % ring) for i in range(ring)])

time: 118 us -> 112 us (0.949)
  local copies, waits for them, and re-layouts: 10.2 us -> 4.22 us
  Pallas kernels: 23.8 us -> 27.3 us
  other arithmetic: 3.03 us -> 1.37 us
  starting transfers between devices: 9.03 us -> 7.83 us
    pallas_call x0 -> x1, Pallas kernels: none -> 4.51 us  [edge_blocks(): pl.pallas_call(edges_kernel, grid_spec=grid_spec, out_shape=[edge_shape,...]
    gather x2 -> x0, local copies, waits for them, and re-layouts: 3.88 us -> none  [the longest x1 2.31 us: shards(): jnp.take(incoming[..., :LANES], position, axis=0, mode='clip')]
    add x1 -> x0, other arithmetic: 2.19 us -> none  [shards(): jnp.take(incoming[..., -LANES:], position, axis=0, mode='clip')]
    slice x1 -> x0, local copies, waits for them, and re-layouts: 2.05 us -> none  [shards(): incoming[..., -LANES:]]
    ppermute x1, starting transfers between devices: 1.74 us -> 0.06 us  [shards(): lax.ppermute(lblk, 'col', [(i, (i - 1) % ring) for i in range(ring)])]
  transfers between devices with their start and end apart: 3 -> 3, of which waited for: 1 -> 1; matrix products, arithmetic and copies ran while one was open for 0% -> 0% of each run, Pallas kernels for 14% -> 15%
where the time goes in v4:
time: 112 us; the launch traced here: 111 us
  waiting for transfers between devices  70.3 us (63%)
  Pallas kernels  27.3 us (24%)
  starting transfers between devices  7.83 us (7%)
  local copies, waits for them, and re-layouts  4.22 us (4%)
  other arithmetic  1.37 us (1%)
    all_to_all x1, waiting for transfers between devices, shards(): lax.all_to_all(outgoing, 'ens', split_axis=0, concat_axis=0, tiled=True)  70.3 us
    pallas_call x1, Pallas kernels, main_forecast(): pl.pallas_call(main_kernel, grid_spec=grid_spec, out_shape=jax.ShapeDtype...  16.8 us
    all_to_all x1, starting transfers between devices, shards(): lax.all_to_all(outgoing, 'ens', split_axis=0, concat_axis=0, tiled=True)  7.28 us
    pallas_call x1, Pallas kernels, edge_fix(): pl.pallas_call(edge_kernel, grid=(2,), in_specs=[whole, whole, whole, who...  5.93 us
    pallas_call x1, Pallas kernels, edge_blocks(): pl.pallas_call(edges_kernel, grid_spec=grid_spec, out_shape=[edge_shape,...  4.51 us
    gather x1, local copies, waits for them, and re-layouts, shards(): outgoing = jnp.take(state, send_index, axis=0, mode='clip')  2.41 us
  transfers between devices with their start and end apart: 3, of which 1 were waited for; matrix products, arithmetic and copies ran while one was open for 0% of the time, Pallas kernels for 15%

profile of v4, /device:TPU:0, one launch (start us, length us, event | category | flops | bytes accessed | tf_op | source)
XLA Modules:
  0.0 111.0 jit_solution(17622241586495405390)
XLA Ops:
  0.0 0.0 copy-start
  0.0 0.9 reshape.117
  0.9 0.3 and_reduce_fusion
  1.3 0.3 convert_reduce_fusion
  1.6 0.2 select_reduce_fusion
  1.7 0.1 copy.5
  1.8 0.1 reshape.120
  1.9 0.0 copy-done
  1.9 2.4 %gather_fusion = f32[32,3,8,1024]{3,2,1,0:T(8,128)} fusion(f32[32,3,8,1024]{3,2,1,0:T(8,128)S(1)} %copy-done, s32[1024]{0:T(1024)S(1)} %pad_clamp_fusion), kind=kCustom, calls=%fused_computation | custom fusion | bytes 6291584 | tf_op jit(solution)/shard_map/jit(_take)/gather | solution.py:261
  4.3 7.3 %all-to-all-start = ((f32[32,3,8,1024]{3,2,1,0:T(8,128)}), f32[32,3,8,1024]{3,2,1,0:T(8,128)}, u32[]{:S(2)}, u32[]{:S(2)}) async-start(f32[32,3,8,1024]{3,2,1,0:T(8,128)} %gather_fusion), calls=%async_computation | async-start | bytes 6291456 | tf_op jit(solution)/shard_map/all_to_all | solution.py:262
  11.6 0.5 add_bitcast_fusion.pos_ref
  12.2 70.3 %all-to-all-done.refs_0_.refs_1_.refs_2_.refs_3_.refs_4_.refs_5_.refs_6_.refs_7_.refs_8_.refs_9_.refs_10_.refs_11_.refs_12_.refs_13_.refs_14_.refs_15_ = f32[32,3,8,1024]{3,2,1,0:T(8,128)} async-done(((f32[32,3,8,1024]{3,2,1,0:T(8,128)}), f32[32,3,8,1024]{3,2,1,0:T(8,128)}, u32[]{:S(2)}, u32[]{:S(2)}) %all-to-all-start) | async-done | bytes 3145760 | tf_op jit(solution)/shard_map/all_to_all | solution.py:262
  82.4 4.5 %shard_map.37 = (f32[32,3,8,128]{3,2,1,0:T(8,128)}, f32[32,3,8,128]{3,2,1,0:T(8,128)}) custom-call(s32[32]{0:T(128)} %add_bitcast_fusion.pos_ref, f32[32,3,8,1024]{3,2,1,0:T(8,128)} %all-to-all-done.refs_0_.refs_1_.refs_2_.refs_3_.refs_4_.refs_5_.refs_6_.refs_7_.refs_8_.refs_9_.refs_10_.refs_11_.refs_12_.refs_13_.refs_14_.refs_15_, ...), custom_call_target="tpu_custom_call" | custom-call | tf_op jit(solution)/shard_map/pallas_call | solution.py:185
  87.0 0.1 collective-permute-start.1
  87.0 0.5 collective-permute-start
  87.5 16.8 %shard_map.38.body_ref = f32[32,3,8,1024]{3,2,1,0:T(8,128)} custom-call(s32[32]{0:T(128)} %add_bitcast_fusion.pos_ref, f32[32,3,8,1024]{3,2,1,0:T(8,128)} %all-to-all-done.refs_0_.refs_1_.refs_2_.refs_3_.refs_4_.refs_5_.refs_6_.refs_7_.refs_8_.refs_9_.refs_10_.refs_11_.refs_12_.refs_13_.refs_14_.refs_15_, ...), custom_call_target="tpu_custom_call" | custom-call | tf_op jit(solution)/shard_map/pallas_call | solution.py:149
  104.3 0.0 collective-permute-done.1.from_right
  104.3 0.0 copy-start.1
  104.3 0.0 collective-permute-done.from_left
  104.4 0.7 copy-done.1
  105.1 5.9 %shard_map.39 = f32[32,3,8,1024]{3,2,1,0:T(8,128)} custom-call(f32[32,3,8,128]{3,2,1,0:T(8,128)} %get-tuple-element.7.lblk, f32[32,3,8,128]{3,2,1,0:T(8,128)} %get-tuple-element.8.rblk, f32[32,3,8,128]{3,2,1,0:T(8,128)} %collective-permute-done.from_left, f32[32,3,8,128]{3,2,1,0:T(8,128)} %copy-done.1, ...), custom_call_target="tpu_custom_call", output_to_operand_aliasing={{}: (4, {})} | custom-call | tf_op jit(solution)/shard_map/pallas_call | solution.py:239
  (4 shorter events, 0.0 us)
Async XLA Ops:
  0.0 1.9 %copy-start = (f32[32,3,8,1024]{3,2,1,0:T(8,128)S(1)}, f32[32,3,8,1024]{3,2,1,0:T(8,128)}, u32[]{:S(2)}) copy-start(f32[32,3,8,1024]{3,2,1,0:T(8,128)} %param.3) | copy-start | bytes 9437188
  4.3 78.1 %all-to-all-start = ((f32[32,3,8,1024]{3,2,1,0:T(8,128)}), f32[32,3,8,1024]{3,2,1,0:T(8,128)}, u32[]{:S(2)}, u32[]{:S(2)}) async-start(f32[32,3,8,1024]{3,2,1,0:T(8,128)} %gather_fusion), calls=%async_computation | async-start | bytes 6291456 | tf_op jit(solution)/shard_map/all_to_all | solution.py:262
  87.0 17.4 %collective-permute-start.1 = (f32[32,3,8,128]{3,2,1,0:T(8,128)}, f32[32,3,8,128]{3,2,1,0:T(8,128)S(1)}, u32[]{:S(2)}, u32[]{:S(2)}) collective-permute-start(f32[32,3,8,128]{3,2,1,0:T(8,128)} %get-tuple-element.7.lblk), channel_id=1, source_target_pairs={{0,3},{1,0},{2,1},{3,2},{4,7},{5,4},{6,5},{7,6},{8,11},{9,8},{10,9... | collective-permute-start | bytes 1179656 | tf_op jit(solution)/shard_map/ppermute | solution.py:266
  87.0 17.3 %collective-permute-start = (f32[32,3,8,128]{3,2,1,0:T(8,128)}, f32[32,3,8,128]{3,2,1,0:T(8,128)}, u32[]{:S(2)}, u32[]{:S(2)}) collective-permute-start(f32[32,3,8,128]{3,2,1,0:T(8,128)} %get-tuple-element.8.rblk), channel_id=1, source_target_pairs={{0,1},{1,2},{2,3},{3,0},{4,5},{5,6},{6,7},{7,4},{8,9},{9,10},{10,1... | collective-permute-start | bytes 1179656 | tf_op jit(solution)/shard_map/ppermute | solution.py:265
  104.3 0.7 copy-start.1

commit v5 on v4

--- a/solution.py
+++ b/solution.py
@@ -8,8 +8,8 @@
 STEPS = 4
 LANES = 128
 PAIR = 2
-EDGE_GROUP = 32
-GATHER_GROUP = 8
+EDGE_GROUP = 8
+GATHER_GROUP = 32
 
 time_step = 0.3
 coriolis = 0.2
@@ -38,6 +38,45 @@
     return send_index, my_owner * dist + my_slot
 
 
+def update(e, u, v, depth, xp, xm):
+    rows = e.shape[-2]
+
+    def yp(a):
+        return pltpu.roll(a, rows - 1, 0)
+
+    def ym(a):
+        return pltpu.roll(a, 1, 0)
+
+    e_xp, u_xp, v_xp, hu_xp = xp
+    e_xm, u_xm, v_xm, hu_xm = xm
+    hv = depth * v
+    e_yp, e_ym = yp(e), ym(e)
+    u_yp, u_ym = yp(u), ym(u)
+    v_yp, v_ym = yp(v), ym(v)
+    hv_yp, hv_ym = yp(hv), ym(hv)
+    half_step = 0.5 * time_step
+    new_e = 0.25 * (e_xp + e_xm + e_yp + e_ym) - half_step * ((hu_xp - hu_xm) + (hv_yp - hv_ym))
+    new_u = (
+        0.25 * (u_xp + u_xm + u_yp + u_ym)
+        - half_step * (u * (u_xp - u_xm) + v * (u_yp - u_ym) + gravity * (e_xp - e_xm))
+        + (time_step * coriolis) * v
+    )
+    new_v = (
+        0.25 * (v_xp + v_xm + v_yp + v_ym)
+        - half_step * (u * (v_xp - v_xm) + v * (v_yp - v_ym) + gravity * (e_yp - e_ym))
+        - (time_step * coriolis) * u
+    )
+    return new_e, new_u, new_v
+
+
+def advance_vreg(e, u, v):
+    depth = 1.0 + e
+    hu = depth * u
+    xp = tuple(pltpu.roll(a, LANES - 1, 1) for a in (e, u, v, hu))
+    xm = tuple(pltpu.roll(a, 1, 1) for a in (e, u, v, hu))
+    return update(e, u, v, depth, xp, xm)
+
+
 def sweep(src, dst, ncol, extra=None):
     rows = src.shape[-2]
     lane = lax.broadcasted_iota(jnp.int32, (rows, LANES), 1)
@@ -54,21 +93,15 @@
             u = u + extra[1, :, window]
             v = v + extra[2, :, window]
         depth = 1.0 + e
-        return e, u, v, depth
+        return e, u, v, depth, depth * u
 
     def ahead(vals):
-        e, u, v, depth = vals
-        return tuple(pltpu.roll(a, LANES - 1, 1) for a in (e, u, v, depth * u))
+        e, u, v, depth, hu = vals
+        return tuple(pltpu.roll(a, LANES - 1, 1) for a in (e, u, v, hu))
 
     def behind(vals):
-        e, u, v, depth = vals
-        return tuple(pltpu.roll(a, 1, 1) for a in (e, u, v, depth * u))
-
-    def yp(a):
-        return pltpu.roll(a, rows - 1, 0)
-
-    def ym(a):
-        return pltpu.roll(a, 1, 0)
+        e, u, v, depth, hu = vals
+        return tuple(pltpu.roll(a, 1, 1) for a in (e, u, v, hu))
 
     here = load(0)
     prev_behind = behind(load(ncol - 1)) if ncol > 1 else behind(here)
@@ -83,26 +116,8 @@
             nxt, nxt_ahead, nxt_behind = here, here_ahead, here_behind
         xp = [jnp.where(last_lane, a, b) for a, b in zip(nxt_ahead, here_ahead)]
         xm = [jnp.where(first_lane, a, b) for a, b in zip(prev_behind, here_behind)]
-        e, u, v, depth = here
-        e_xp, u_xp, v_xp, hu_xp = xp
-        e_xm, u_xm, v_xm, hu_xm = xm
-        hv = depth * v
-        e_yp, e_ym = yp(e), ym(e)
-        u_yp, u_ym = yp(u), ym(u)
-        v_yp, v_ym = yp(v), ym(v)
-        hv_yp, hv_ym = yp(hv), ym(hv)
-        half_step = 0.5 * time_step
-        new_e = 0.25 * (e_xp + e_xm + e_yp + e_ym) - half_step * ((hu_xp - hu_xm) + (hv_yp - hv_ym))
-        new_u = (
-            0.25 * (u_xp + u_xm + u_yp + u_ym)
-            - half_step * (u * (u_xp - u_xm) + v * (u_yp - u_ym) + gravity * (e_xp - e_xm))
-            + (time_step * coriolis) * v
-        )
-        new_v = (
-            0.25 * (v_xp + v_xm + v_yp + v_ym)
-            - half_step * (u * (v_xp - v_xm) + v * (v_yp - v_ym) + gravity * (e_yp - e_ym))
-            - (time_step * coriolis) * u
-        )
+        e, u, v, depth, _ = here
+        new_e, new_u, new_v = update(e, u, v, depth, xp, xm)
         window = pl.ds(j * LANES, LANES)
         dst[0, :, window] = new_e
         dst[1, :, window] = new_u
@@ -203,16 +218,19 @@
             base = g * group
             for k in range(group):
                 i = base + k
+                fields = []
                 for f in range(3):
                     left = jnp.where(lane >= LANES - width, from_left[i, f], lblk[i, f])
                     right = jnp.where(lane < width, from_right[i, f], rblk[i, f])
                     right = pltpu.roll(right, half, 1)
                     keep_left = (lane < 2 * width) | (lane >= LANES - width)
-                    packed[k, f] = jnp.where(keep_left, left, right)
-            chains = [
-                chain_of(packed.at[k], result.at[base + k], first.at[k], second.at[k]) for k in range(group)
-            ]
-            run_steps(chains, [None] * group, 1)
+                    fields.append(jnp.where(keep_left, left, right))
+                e, u, v = fields
+                for _ in range(STEPS):
+                    e, u, v = advance_vreg(e, u, v)
+                result[i, 0] = e
+                result[i, 1] = u
+                result[i, 2] = v
             return carry
 
         lax.fori_loop(0, lblk.shape[0] // group, block, 0)

time: 112 us -> 112 us (level)
    pallas_call x1, Pallas kernels: 4.51 us -> 3.18 us  [edge_blocks(): pl.pallas_call(edges_kernel, grid_spec=grid_spec, out_shape=[edge_shape,...]
where the time goes in v5:
time: 112 us; the launch traced here: 111 us
  waiting for transfers between devices  70.3 us (63%)
  Pallas kernels  27 us (24%)
  starting transfers between devices  7.83 us (7%)
  local copies, waits for them, and re-layouts  4.22 us (4%)
  other arithmetic  1.37 us (1%)
    all_to_all x1, waiting for transfers between devices, shards(): lax.all_to_all(outgoing, 'ens', split_axis=0, concat_axis=0, tiled=True)  70.3 us
    pallas_call x1, Pallas kernels, main_forecast(): pl.pallas_call(main_kernel, grid_spec=grid_spec, out_shape=jax.ShapeDtype...  16.9 us
    all_to_all x1, starting transfers between devices, shards(): lax.all_to_all(outgoing, 'ens', split_axis=0, concat_axis=0, tiled=True)  7.28 us
    pallas_call x1, Pallas kernels, edge_fix(): pl.pallas_call(edge_kernel, grid=(2,), in_specs=[whole, whole, whole, who...  6.99 us
    pallas_call x1, Pallas kernels, edge_blocks(): pl.pallas_call(edges_kernel, grid_spec=grid_spec, out_shape=[edge_shape,...  3.18 us
    gather x1, local copies, waits for them, and re-layouts, shards(): outgoing = jnp.take(state, send_index, axis=0, mode='clip')  2.41 us
  transfers between devices with their start and end apart: 3, of which 1 were waited for; matrix products, arithmetic and copies ran while one was open for 0% of the time, Pallas kernels for 15%

profile of v5, /device:TPU:0, one launch (start us, length us, event | category | flops | bytes accessed | tf_op | source)
XLA Modules:
  0.0 110.8 jit_solution(16563469335019541663)
XLA Ops:
  0.0 0.0 copy-start
  0.0 0.9 reshape.117
  0.9 0.3 and_reduce_fusion
  1.3 0.3 convert_reduce_fusion
  1.6 0.2 select_reduce_fusion
  1.7 0.1 copy.5
  1.8 0.1 reshape.120
  1.9 0.0 copy-done
  1.9 2.4 %gather_fusion = f32[32,3,8,1024]{3,2,1,0:T(8,128)} fusion(f32[32,3,8,1024]{3,2,1,0:T(8,128)S(1)} %copy-done, s32[1024]{0:T(1024)S(1)} %pad_clamp_fusion), kind=kCustom, calls=%fused_computation | custom fusion | bytes 6291584 | tf_op jit(solution)/shard_map/jit(_take)/gather | solution.py:279
  4.3 7.3 %all-to-all-start = ((f32[32,3,8,1024]{3,2,1,0:T(8,128)}), f32[32,3,8,1024]{3,2,1,0:T(8,128)}, u32[]{:S(2)}, u32[]{:S(2)}) async-start(f32[32,3,8,1024]{3,2,1,0:T(8,128)} %gather_fusion), calls=%async_computation | async-start | bytes 6291456 | tf_op jit(solution)/shard_map/all_to_all | solution.py:280
  11.6 0.5 add_bitcast_fusion.pos_ref
  12.2 70.3 %all-to-all-done.refs_0_.refs_1_.refs_2_.refs_3_.refs_4_.refs_5_.refs_6_.refs_7_.refs_8_.refs_9_.refs_10_.refs_11_.refs_12_.refs_13_.refs_14_.refs_15_.refs_16_.refs_17_.refs_18_.refs_19_.refs_20_.refs_21_.refs_22_.refs_23_.refs_24_.refs_25_.refs_26_.refs_27_.refs_28_.refs_29_.refs_30_.refs_31_.refs_32_.refs_33_.refs_34_.refs_35_.refs_36_.refs_37_.refs_38_.refs_39_.refs_40_.refs_41_.refs_42_.refs_43_.refs_44_.refs_45_.refs_46_.refs_47_.refs_48_.refs_49_.refs_50_.refs_51_.refs_52_.refs_53_.refs_54_.refs_55_.refs_56_.refs_57_.refs_58_.refs_59_.refs_60_.refs_61_.refs_62_.refs_63_ = f32[32,3,8,1024]{3,2,1,0:T(8,128)} async-done(((f32[32,3,8,1024]{3,2,1,0:T(8,128)}), ...) | async-done | bytes 3145760 | tf_op jit(solution)/shard_map/all_to_all | solution.py:280
  82.4 3.2 %shard_map.37 = (f32[32,3,8,128]{3,2,1,0:T(8,128)}, f32[32,3,8,128]{3,2,1,0:T(8,128)}) custom-call(s32[32]{0:T(128)} %add_bitcast_fusion.pos_ref, ...), custom_call_target="tpu_custom_call" | custom-call | tf_op jit(solution)/shard_map/pallas_call | solution.py:200
  85.6 0.1 collective-permute-start.1
  85.7 0.5 collective-permute-start
  86.2 16.9 %shard_map.38.body_ref = f32[32,3,8,1024]{3,2,1,0:T(8,128)} custom-call(s32[32]{0:T(128)} %add_bitcast_fusion.pos_ref, ...), custom_call_target="tpu_custom_call" | custom-call | tf_op jit(solution)/shard_map/pallas_call | solution.py:164
  103.1 0.0 collective-permute-done.1.from_right
  103.1 0.0 copy-start.1
  103.1 0.0 collective-permute-done.from_left
  103.1 0.7 copy-done.1
  103.8 7.0 %shard_map.39 = f32[32,3,8,1024]{3,2,1,0:T(8,128)} custom-call(f32[32,3,8,128]{3,2,1,0:T(8,128)} %get-tuple-element.7.lblk, f32[32,3,8,128]{3,2,1,0:T(8,128)} %get-tuple-element.8.rblk, f32[32,3,8,128]{3,2,1,0:T(8,128)} %collective-permute-done.from_left, f32[32,3,8,128]{3,2,1,0:T(8,128)} %copy-done.1, ...), custom_call_target="tpu_custom_call", output_to_operand_aliasing={{}: (4, {})} | custom-call | tf_op jit(solution)/shard_map/pallas_call | solution.py:257
  (4 shorter events, 0.0 us)
Async XLA Ops:
  0.0 1.9 %copy-start = (f32[32,3,8,1024]{3,2,1,0:T(8,128)S(1)}, f32[32,3,8,1024]{3,2,1,0:T(8,128)}, u32[]{:S(2)}) copy-start(f32[32,3,8,1024]{3,2,1,0:T(8,128)} %param.3) | copy-start | bytes 9437188
  4.3 78.1 %all-to-all-start = ((f32[32,3,8,1024]{3,2,1,0:T(8,128)}), f32[32,3,8,1024]{3,2,1,0:T(8,128)}, u32[]{:S(2)}, u32[]{:S(2)}) async-start(f32[32,3,8,1024]{3,2,1,0:T(8,128)} %gather_fusion), calls=%async_computation | async-start | bytes 6291456 | tf_op jit(solution)/shard_map/all_to_all | solution.py:280
  85.6 17.4 %collective-permute-start.1 = (f32[32,3,8,128]{3,2,1,0:T(8,128)}, f32[32,3,8,128]{3,2,1,0:T(8,128)S(1)}, u32[]{:S(2)}, u32[]{:S(2)}) collective-permute-start(f32[32,3,8,128]{3,2,1,0:T(8,128)} %get-tuple-element.7.lblk), channel_id=1, source_target_pairs={{0,3},{1,0},{2,1},{3,2},{4,7},{5,4},{6,5},{7,6},{8,11},{9,8},{10,9... | collective-permute-start | bytes 1179656 | tf_op jit(solution)/shard_map/ppermute | solution.py:284
  85.7 17.4 %collective-permute-start = (f32[32,3,8,128]{3,2,1,0:T(8,128)}, f32[32,3,8,128]{3,2,1,0:T(8,128)}, u32[]{:S(2)}, u32[]{:S(2)}) collective-permute-start(f32[32,3,8,128]{3,2,1,0:T(8,128)} %get-tuple-element.8.rblk), channel_id=1, source_target_pairs={{0,1},{1,2},{2,3},{3,0},{4,5},{5,6},{6,7},{7,4},{8,9},{9,10},{10,1... | collective-permute-start | bytes 1179656 | tf_op jit(solution)/shard_map/ppermute | solution.py:283
  103.1 0.7 copy-start.1

commit v6 on v5

--- a/solution.py
+++ b/solution.py
@@ -38,7 +38,7 @@
     return send_index, my_owner * dist + my_slot
 
 
-def update(e, u, v, depth, xp, xm):
+def update(e, u, v, xp, xm):
     rows = e.shape[-2]
 
     def yp(a):
@@ -47,13 +47,15 @@
     def ym(a):
         return pltpu.roll(a, 1, 0)
 
-    e_xp, u_xp, v_xp, hu_xp = xp
-    e_xm, u_xm, v_xm, hu_xm = xm
-    hv = depth * v
+    e_xp, u_xp, v_xp = xp
+    e_xm, u_xm, v_xm = xm
     e_yp, e_ym = yp(e), ym(e)
     u_yp, u_ym = yp(u), ym(u)
     v_yp, v_ym = yp(v), ym(v)
-    hv_yp, hv_ym = yp(hv), ym(hv)
+    hu_xp = (1.0 + e_xp) * u_xp
+    hu_xm = (1.0 + e_xm) * u_xm
+    hv_yp = (1.0 + e_yp) * v_yp
+    hv_ym = (1.0 + e_ym) * v_ym
     half_step = 0.5 * time_step
     new_e = 0.25 * (e_xp + e_xm + e_yp + e_ym) - half_step * ((hu_xp - hu_xm) + (hv_yp - hv_ym))
     new_u = (
@@ -70,11 +72,9 @@
 
 
 def advance_vreg(e, u, v):
-    depth = 1.0 + e
-    hu = depth * u
-    xp = tuple(pltpu.roll(a, LANES - 1, 1) for a in (e, u, v, hu))
-    xm = tuple(pltpu.roll(a, 1, 1) for a in (e, u, v, hu))
-    return update(e, u, v, depth, xp, xm)
+    xp = tuple(pltpu.roll(a, LANES - 1, 1) for a in (e, u, v))
+    xm = tuple(pltpu.roll(a, 1, 1) for a in (e, u, v))
+    return update(e, u, v, xp, xm)
 
 
 def sweep(src, dst, ncol, extra=None):
@@ -92,16 +92,13 @@
             e = e + extra[0, :, window]
             u = u + extra[1, :, window]
             v = v + extra[2, :, window]
-        depth = 1.0 + e
-        return e, u, v, depth, depth * u
+        return e, u, v
 
     def ahead(vals):
-        e, u, v, depth, hu = vals
-        return tuple(pltpu.roll(a, LANES - 1, 1) for a in (e, u, v, hu))
+        return tuple(pltpu.roll(a, LANES - 1, 1) for a in vals)
 
     def behind(vals):
-        e, u, v, depth, hu = vals
-        return tuple(pltpu.roll(a, 1, 1) for a in (e, u, v, hu))
+        return tuple(pltpu.roll(a, 1, 1) for a in vals)
 
     here = load(0)
     prev_behind = behind(load(ncol - 1)) if ncol > 1 else behind(here)
@@ -116,8 +113,8 @@
             nxt, nxt_ahead, nxt_behind = here, here_ahead, here_behind
         xp = [jnp.where(last_lane, a, b) for a, b in zip(nxt_ahead, here_ahead)]
         xm = [jnp.where(first_lane, a, b) for a, b in zip(prev_behind, here_behind)]
-        e, u, v, depth, _ = here
-        new_e, new_u, new_v = update(e, u, v, depth, xp, xm)
+        e, u, v = here
+        new_e, new_u, new_v = update(e, u, v, xp, xm)
         window = pl.ds(j * LANES, LANES)
         dst[0, :, window] = new_e
         dst[1, :, window] = new_u

time: 112 us -> 111 us (level)
  no operation moved by 1% of the time
where the time goes in v6:
time: 111 us; the launch traced here: 110 us
  waiting for transfers between devices  70.3 us (63%)
  Pallas kernels  25.9 us (23%)
  starting transfers between devices  7.83 us (7%)
  local copies, waits for them, and re-layouts  4.22 us (4%)
  other arithmetic  1.37 us (1%)
    all_to_all x1, waiting for transfers between devices, shards(): lax.all_to_all(outgoing, 'ens', split_axis=0, concat_axis=0, tiled=True)  70.3 us
    pallas_call x1, Pallas kernels, main_forecast(): pl.pallas_call(main_kernel, grid_spec=grid_spec, out_shape=jax.ShapeDtype...  15.9 us
    all_to_all x1, starting transfers between devices, shards(): lax.all_to_all(outgoing, 'ens', split_axis=0, concat_axis=0, tiled=True)  7.28 us
    pallas_call x1, Pallas kernels, edge_fix(): pl.pallas_call(edge_kernel, grid=(2,), in_specs=[whole, whole, whole, who...  6.78 us
    pallas_call x1, Pallas kernels, edge_blocks(): pl.pallas_call(edges_kernel, grid_spec=grid_spec, out_shape=[edge_shape,...  3.18 us
    gather x1, local copies, waits for them, and re-layouts, shards(): outgoing = jnp.take(state, send_index, axis=0, mode='clip')  2.41 us
  transfers between devices with their start and end apart: 3, of which 1 were waited for; matrix products, arithmetic and copies ran while one was open for 0% of the time, Pallas kernels for 15%

profile of v6, /device:TPU:0, one launch (start us, length us, event | category | flops | bytes accessed | tf_op | source)
XLA Modules:
  0.0 109.7 jit_solution(3760261269750214538)
XLA Ops:
  0.0 0.0 copy-start
  0.0 0.9 reshape.117
  0.9 0.3 and_reduce_fusion
  1.3 0.3 convert_reduce_fusion
  1.6 0.2 select_reduce_fusion
  1.7 0.1 copy.5
  1.8 0.1 reshape.120
  1.9 0.0 copy-done
  1.9 2.4 %gather_fusion = f32[32,3,8,1024]{3,2,1,0:T(8,128)} fusion(f32[32,3,8,1024]{3,2,1,0:T(8,128)S(1)} %copy-done, s32[1024]{0:T(1024)S(1)} %pad_clamp_fusion), kind=kCustom, calls=%fused_computation | custom fusion | bytes 6291584 | tf_op jit(solution)/shard_map/jit(_take)/gather | solution.py:276
  4.3 7.3 %all-to-all-start = ((f32[32,3,8,1024]{3,2,1,0:T(8,128)}), f32[32,3,8,1024]{3,2,1,0:T(8,128)}, u32[]{:S(2)}, u32[]{:S(2)}) async-start(f32[32,3,8,1024]{3,2,1,0:T(8,128)} %gather_fusion), calls=%async_computation | async-start | bytes 6291456 | tf_op jit(solution)/shard_map/all_to_all | solution.py:277
  11.6 0.5 add_bitcast_fusion.pos_ref
  12.2 70.3 %all-to-all-done.refs_0_.refs_1_.refs_2_.refs_3_.refs_4_.refs_5_.refs_6_.refs_7_.refs_8_.refs_9_.refs_10_.refs_11_.refs_12_.refs_13_.refs_14_.refs_15_.refs_16_.refs_17_.refs_18_.refs_19_.refs_20_.refs_21_.refs_22_.refs_23_.refs_24_.refs_25_.refs_26_.refs_27_.refs_28_.refs_29_.refs_30_.refs_31_.refs_32_.refs_33_.refs_34_.refs_35_.refs_36_.refs_37_.refs_38_.refs_39_.refs_40_.refs_41_.refs_42_.refs_43_.refs_44_.refs_45_.refs_46_.refs_47_.refs_48_.refs_49_.refs_50_.refs_51_.refs_52_.refs_53_.refs_54_.refs_55_.refs_56_.refs_57_.refs_58_.refs_59_.refs_60_.refs_61_.refs_62_.refs_63_ = f32[32,3,8,1024]{3,2,1,0:T(8,128)} async-done(((f32[32,3,8,1024]{3,2,1,0:T(8,128)}), ...) | async-done | bytes 3145760 | tf_op jit(solution)/shard_map/all_to_all | solution.py:277
  82.4 3.2 %shard_map.37 = (f32[32,3,8,128]{3,2,1,0:T(8,128)}, f32[32,3,8,128]{3,2,1,0:T(8,128)}) custom-call(s32[32]{0:T(128)} %add_bitcast_fusion.pos_ref, ...), custom_call_target="tpu_custom_call" | custom-call | tf_op jit(solution)/shard_map/pallas_call | solution.py:197
  85.6 0.1 collective-permute-start.1
  85.7 0.5 collective-permute-start
  86.2 15.9 %shard_map.38.body_ref = f32[32,3,8,1024]{3,2,1,0:T(8,128)} custom-call(s32[32]{0:T(128)} %add_bitcast_fusion.pos_ref, ...), custom_call_target="tpu_custom_call" | custom-call | tf_op jit(solution)/shard_map/pallas_call | solution.py:161
  102.1 0.0 collective-permute-done.1.from_right
  102.1 0.0 copy-start.1
  102.1 0.0 collective-permute-done.from_left
  102.1 0.7 copy-done.1
  102.9 6.8 %shard_map.39 = f32[32,3,8,1024]{3,2,1,0:T(8,128)} custom-call(f32[32,3,8,128]{3,2,1,0:T(8,128)} %get-tuple-element.7.lblk, f32[32,3,8,128]{3,2,1,0:T(8,128)} %get-tuple-element.8.rblk, f32[32,3,8,128]{3,2,1,0:T(8,128)} %collective-permute-done.from_left, f32[32,3,8,128]{3,2,1,0:T(8,128)} %copy-done.1, ...), custom_call_target="tpu_custom_call", output_to_operand_aliasing={{}: (4, {})} | custom-call | tf_op jit(solution)/shard_map/pallas_call | solution.py:254
  (4 shorter events, 0.0 us)
Async XLA Ops:
  0.0 1.9 %copy-start = (f32[32,3,8,1024]{3,2,1,0:T(8,128)S(1)}, f32[32,3,8,1024]{3,2,1,0:T(8,128)}, u32[]{:S(2)}) copy-start(f32[32,3,8,1024]{3,2,1,0:T(8,128)} %param.3) | copy-start | bytes 9437188
  4.3 78.1 %all-to-all-start = ((f32[32,3,8,1024]{3,2,1,0:T(8,128)}), f32[32,3,8,1024]{3,2,1,0:T(8,128)}, u32[]{:S(2)}, u32[]{:S(2)}) async-start(f32[32,3,8,1024]{3,2,1,0:T(8,128)} %gather_fusion), calls=%async_computation | async-start | bytes 6291456 | tf_op jit(solution)/shard_map/all_to_all | solution.py:277
  85.6 16.5 %collective-permute-start.1 = (f32[32,3,8,128]{3,2,1,0:T(8,128)}, f32[32,3,8,128]{3,2,1,0:T(8,128)S(1)}, u32[]{:S(2)}, u32[]{:S(2)}) collective-permute-start(f32[32,3,8,128]{3,2,1,0:T(8,128)} %get-tuple-element.7.lblk), channel_id=1, source_target_pairs={{0,3},{1,0},{2,1},{3,2},{4,7},{5,4},{6,5},{7,6},{8,11},{9,8},{10,9... | collective-permute-start | bytes 1179656 | tf_op jit(solution)/shard_map/ppermute | solution.py:281
  85.7 16.4 %collective-permute-start = (f32[32,3,8,128]{3,2,1,0:T(8,128)}, f32[32,3,8,128]{3,2,1,0:T(8,128)}, u32[]{:S(2)}, u32[]{:S(2)}) collective-permute-start(f32[32,3,8,128]{3,2,1,0:T(8,128)} %get-tuple-element.8.rblk), channel_id=1, source_target_pairs={{0,1},{1,2},{2,3},{3,0},{4,5},{5,6},{6,7},{7,4},{8,9},{9,10},{10,1... | collective-permute-start | bytes 1179656 | tf_op jit(solution)/shard_map/ppermute | solution.py:280
  102.1 0.7 copy-start.1

commit v7 on v1

v7 whole, which is shorter than its diff:
```python
import jax
import jax.numpy as jnp
from jax import lax
from jax.experimental import pallas as pl
from jax.experimental.pallas import tpu as pltpu
from jax.sharding import PartitionSpec as P

STEPS = 4
LANES = 128
PAIR = 2

time_step = 0.3
coriolis = 0.2
gravity = 1.0


def routing(parents, count, per_dev, dist, me):
    blocks = parents.reshape(count, per_dev)
    owner = blocks // per_dev
    local = blocks % per_dev
    ids = jnp.arange(per_dev, dtype=jnp.int32)
    same = blocks[:, :, None] == blocks[:, None, :]
    earlier = ids[None, :] < ids[:, None]
    first = jnp.logical_not(jnp.any(same & earlier[None], axis=2))
    below = (
        (owner[:, :, None] == owner[:, None, :])
        & (blocks[:, None, :] < blocks[:, :, None])
        & first[:, None, :]
    )
    slot = jnp.sum(below.astype(jnp.int32), axis=2)
    slots = jnp.arange(dist, dtype=jnp.int32)
    pick = (owner == me)[:, None, :] & first[:, None, :] & (slot[:, None, :] == slots[None, :, None])
    send_index = jnp.sum(pick.astype(jnp.int32) * local[:, None, :], axis=2).reshape(-1)
    my_owner = lax.dynamic_index_in_dim(owner, me, 0, keepdims=False)
    my_slot = lax.dynamic_index_in_dim(slot, me, 0, keepdims=False)
    return send_index, my_owner * dist + my_slot


def update(e, u, v, xp, xm):
    rows = e.shape[-2]

    def yp(a):
        return pltpu.roll(a, rows - 1, 0)

    def ym(a):
        return pltpu.roll(a, 1, 0)

    e_xp, u_xp, v_xp = xp
    e_xm, u_xm, v_xm = xm
    e_yp, e_ym = yp(e), ym(e)
    u_yp, u_ym = yp(u), ym(u)
    v_yp, v_ym = yp(v), ym(v)
    hu_xp = (1.0 + e_xp) * u_xp
    hu_xm = (1.0 + e_xm) * u_xm
    hv_yp = (1.0 + e_yp) * v_yp
    hv_ym = (1.0 + e_ym) * v_ym
    half_step = 0.5 * time_step
    new_e = 0.25 * (e_xp + e_xm + e_yp + e_ym) - half_step * ((hu_xp - hu_xm) + (hv_yp - hv_ym))
    new_u = (
        0.25 * (u_xp + u_xm + u_yp + u_ym)
        - half_step * (u * (u_xp - u_xm) + v * (u_yp - u_ym) + gravity * (e_xp - e_xm))
        + (time_step * coriolis) * v
    )
    new_v = (
        0.25 * (v_xp + v_xm + v_yp + v_ym)
        - half_step * (u * (v_xp - v_xm) + v * (v_yp - v_ym) + gravity * (e_yp - e_ym))
        - (time_step * coriolis) * u
    )
    return new_e, new_u, new_v


def advance_vreg(e, u, v):
    xp = tuple(pltpu.roll(a, LANES - 1, 1) for a in (e, u, v))
    xm = tuple(pltpu.roll(a, 1, 1) for a in (e, u, v))
    return update(e, u, v, xp, xm)


def sweep(load, store, ncol):
    rows = load(0)[0].shape[-2]
    lane = lax.broadcasted_iota(jnp.int32, (rows, LANES), 1)
    first_lane = lane == 0
    last_lane = lane == LANES - 1

    def fetch(j):
        return load(j % ncol)

    def ahead(vals):
        return tuple(pltpu.roll(a, LANES - 1, 1) for a in vals)

    def behind(vals):
        return tuple(pltpu.roll(a, 1, 1) for a in vals)

    here = fetch(0)
    prev_behind = behind(fetch(ncol - 1))
    here_behind = behind(here)
    here_ahead = ahead(here)
    for j in range(ncol):
        nxt = fetch(j + 1)
        nxt_ahead = ahead(nxt)
        nxt_behind = behind(nxt)
        xp = [jnp.where(last_lane, a, b) for a, b in zip(nxt_ahead, here_ahead)]
        xm = [jnp.where(first_lane, a, b) for a, b in zip(prev_behind, here_behind)]
        e, u, v = here
        store(j, update(e, u, v, xp, xm))
        prev_behind = here_behind
        here, here_behind, here_ahead = nxt, nxt_behind, nxt_ahead


def ref_loader(ref):
    def load(j):
        window = pl.ds(j * LANES, LANES)
        return tuple(ref[f, :, window] for f in range(3))

    return load


def ref_storer(ref, limit):
    def store(j, values):
        if j < limit:
            window = pl.ds(j * LANES, LANES)
            for f in range(3):
                ref[f, :, window] = values[f]

    return store


def child_loader(inc, noise, halo, ncol):
    def load(j):
        if j == ncol:
            return tuple(halo[f] for f in range(3))
        window = pl.ds(j * LANES, LANES)
        return tuple(inc[f, :, window] + noise[f, :, window] for f in range(3))

    return load


def main_kernel(pos_ref, *refs):
    incs = refs[:-5]
    noise_ref, halo_ref, out_ref, first, second = refs[-5:]
    ncol = noise_ref.shape[-1] // LANES
    wide = ncol + 1
    for s in range(STEPS):
        for k in range(len(incs)):
            if s == 0:
                load = child_loader(incs[k].at[0], noise_ref.at[k], halo_ref.at[k], ncol)
            else:
                load = ref_loader((first if s % 2 == 1 else second).at[k])
            if s == STEPS - 1:
                store = ref_storer(out_ref.at[k], ncol)
            else:
                store = ref_storer((first if s % 2 == 0 else second).at[k], wide)
            sweep(load, store, wide)


def main_forecast(position, incoming, noise, halo):
    per_dev, nf, rows, cols = noise.shape
    group = PAIR if per_dev % PAIR == 0 else 1

    def row_map(k):
        return lambda i, pos: (pos[i * group + k], 0, 0, 0)

    in_specs = [pl.BlockSpec((1, nf, rows, cols), row_map(k)) for k in range(group)]
    spec = pl.BlockSpec((group, nf, rows, cols), lambda i, pos: (i, 0, 0, 0))
    halo_spec = pl.BlockSpec((group, nf, rows, LANES), lambda i, pos: (i, 0, 0, 0))
    grid_spec = pltpu.PrefetchScalarGridSpec(
        num_scalar_prefetch=1,
        grid=(per_dev // group,),
        in_specs=in_specs + [spec, halo_spec],
        out_specs=spec,
        scratch_shapes=[pltpu.VMEM((group, nf, rows, cols + LANES), jnp.float32)] * 2,
    )
    return pl.pallas_call(
        main_kernel,
        grid_spec=grid_spec,
        out_shape=jax.ShapeDtypeStruct(noise.shape, noise.dtype),
    )(position, *([incoming] * group), noise, halo)


def halo_block(state, noise, parents, me):
    per_dev, nf, rows, cols = state.shape
    width = STEPS

    def edges(a):
        return jnp.concatenate([a[..., :width], a[..., -width:]], axis=-1).reshape(a.shape[0], -1)

    everyone = lax.all_gather(edges(state), "ens", axis=0, tiled=True)
    mine = lax.dynamic_slice_in_dim(parents, me * per_dev, per_dev)
    child_edges = jnp.take(everyone, mine, axis=0, mode="clip") + edges(noise)
    ring = lax.axis_size("col")
    from_left = lax.ppermute(child_edges, "col", [(i, (i + 1) % ring) for i in range(ring)])
    from_right = lax.ppermute(child_edges, "col", [(i, (i - 1) % ring) for i in range(ring)])
    from_left = from_left.reshape(per_dev, nf, rows, 2 * width)
    from_right = from_right.reshape(per_dev, nf, rows, 2 * width)
    gap = jnp.zeros((per_dev, nf, rows, LANES - 2 * width), state.dtype)
    return jnp.concatenate([from_right[..., :width], gap, from_left[..., width:]], axis=-1)


def shards(state, noise, parents):
    count = lax.axis_size("ens")
    me = lax.axis_index("ens")
    per_dev = state.shape[0]
    dist = max(1, -(-per_dev // count))
    send_index, position = routing(parents, count, per_dev, dist, me)
    outgoing = jnp.take(state, send_index, axis=0, mode="clip")
    incoming = lax.all_to_all(outgoing, "ens", split_axis=0, concat_axis=0, tiled=True)
    halo = halo_block(state, noise, parents, me)
    return main_forecast(position, incoming, noise, halo)


def solution(mesh):
    placed = (P("ens", None, None, "col"), P("ens", None, None, "col"), P())
    return jax.shard_map(
        shards, mesh=mesh, in_specs=placed, out_specs=P("ens", None, None, "col"), check_vma=False
    )
```

time: 136 us -> 137 us (level)
  waiting for transfers between devices: 81.6 us -> 1.24 us
  blocking collectives: 0 us -> 79.3 us
  local copies, waits for them, and re-layouts: 9.65 us -> 24.3 us
  Pallas kernels: 28.2 us -> 16.2 us
  other arithmetic: 7.37 us -> 5.55 us
    all_gather x0 -> x1, blocking collectives: none -> 79.3 us  [halo_block(): everyone = lax.all_gather(edges(state), 'ens', axis=0, tiled=True)]
    all_to_all x1, waiting for transfers between devices: 70.8 us -> 0.01 us  [shards(): lax.all_to_all(outgoing, 'ens', split_axis=0, concat_axis=0, tiled=True)]
    pallas_call x1, Pallas kernels: 28.2 us -> 16.2 us  [main_forecast(): pl.pallas_call(main_kernel, grid_spec=grid_spec, out_shape=jax.ShapeDtype...]
    unnamed x4 -> x10, local copies, waits for them, and re-layouts: 0.01 us -> 9.77 us
    ppermute x2, waiting for transfers between devices: 10.9 us -> 1.24 us  [the longest x1 1.23 us: halo_block(): lax.ppermute(child_edges, 'col', [(i, (i + 1) % ring) for i in range(ring)])]
    select_n x3 -> x0, other arithmetic: 4.15 us -> none  [the longest x2 4.14 us: shards(): outgoing = jnp.take(state, send_index, axis=0)]
    slice x1 -> x4, local copies, waits for them, and re-layouts: 2.11 us -> 6.2 us  [the longest x2 4.05 us: edges(): a[..., :width]]
    concatenate x1 -> x3, other arithmetic: 0.92 us -> 3.62 us  [the longest x1 1.92 us: halo_block(): jnp.concatenate([from_right[..., :width], gap, from_left[..., width:]], a...]
  transfers between devices with their start and end apart: 3 -> 3, of which waited for: 3 -> 1; matrix products, arithmetic and copies ran while one was open for 0% -> 16% of each run, Pallas kernels for 0% -> 0%
where the time goes in v7:
time: 137 us; the launch traced here: 136 us
  blocking collectives  79.3 us (58%)
  local copies, waits for them, and re-layouts  24.3 us (18%)
  Pallas kernels  16.2 us (12%)
  starting transfers between devices  9.16 us (7%)
  other arithmetic  5.55 us (4%)
    all_gather x1, blocking collectives, halo_block(): everyone = lax.all_gather(edges(state), 'ens', axis=0, tiled=True)  79.3 us
    pallas_call x1, Pallas kernels, main_forecast(): pl.pallas_call(main_kernel, grid_spec=grid_spec, out_shape=jax.ShapeDtype...  16.2 us
    unnamed x10, local copies, waits for them, and re-layouts  9.77 us
    all_to_all x1, starting transfers between devices, shards(): lax.all_to_all(outgoing, 'ens', split_axis=0, concat_axis=0, tiled=True)  7.42 us
    gather x1, local copies, waits for them, and re-layouts, shards(): outgoing = jnp.take(state, send_index, axis=0, mode='clip')  4.31 us
    slice x2, local copies, waits for them, and re-layouts, edges(): a[..., :width]  4.05 us
  transfers between devices with their start and end apart: 3, of which 1 were waited for; matrix products, arithmetic and copies ran while one was open for 16% of the time, Pallas kernels for 0%

profile of v7, /device:TPU:0, one launch (start us, length us, event | category | flops | bytes accessed | tf_op | source)
XLA Modules:
  0.0 135.8 jit_solution(10890951581926869096)
XLA Ops:
  0.0 0.8 reshape.129
  1.8 4.3 %gather_fusion = f32[32,3,8,1024]{3,2,1,0:T(8,128)} fusion(f32[32,3,8,1024]{3,2,1,0:T(8,128)} %param.3, s32[1024]{0:T(1024)S(1)} %pad_clamp_fusion.1), kind=kCustom, calls=%fused_computation | custom fusion | bytes 6291584 | tf_op jit(solution)/shard_map/jit(_take)/gather | solution.py:204
  6.1 7.4 %all-to-all-start = ((f32[32,3,8,1024]{3,2,1,0:T(8,128)}), f32[32,3,8,1024]{3,2,1,0:T(8,128)S(1)}, u32[]{:S(2)}, u32[]{:S(2)}) async-start(f32[32,3,8,1024]{3,2,1,0:T(8,128)} %gather_fusion), calls=%async_computation | async-start | bytes 6291456 | tf_op jit(solution)/shard_map/all_to_all | solution.py:205
  13.5 2.0 %fusion.4 = (f32[32,3,8,4]{3,2,1,0:T(8,128)S(1)}, f32[32,3,8,4]{3,2,1,0:T(8,128)}) fusion(f32[32,3,8,1024]{3,2,1,0:T(8,128)} %param.3), kind=kLoop, calls=%fused_computation.24 | loop fusion | bytes 49152 | tf_op jit(solution)/shard_map/slice | solution.py:184
  15.5 1.8 %copy.34 = f32[32,3,8,4]{0,3,2,1:T(4,128)} copy(f32[32,3,8,4]{3,2,1,0:T(8,128)} %get-tuple-element.10) | data formatting | bytes 24576
  17.3 0.8 copy.33
  18.2 0.9 pad_maximum_fusion.1
  19.0 0.7 copy.25
  19.8 2.0 %fusion.3 = (f32[32,3,8,4]{3,2,1,0:T(8,128)S(1)}, f32[32,3,8,4]{3,2,1,0:T(8,128)}) fusion(f32[32,3,8,1024]{3,2,1,0:T(8,128)} %refs_2_.1), kind=kLoop, calls=%fused_computation.23 | loop fusion | bytes 49152 | tf_op jit(solution)/shard_map/slice | solution.py:184
  21.8 1.8 %copy.36 = f32[32,3,8,4]{0,3,2,1:T(4,128)} copy(f32[32,3,8,4]{3,2,1,0:T(8,128)} %get-tuple-element.8) | data formatting | bytes 24576
  23.6 0.8 copy.35
  24.5 0.9 pad_maximum_fusion.2
  25.4 79.3 %all_gather.3 = f32[256,192]{1,0:T(8,128)S(1)} all-gather(f32[32,192]{1,0:T(8,128)} %copy.25), channel_id=1, replica_groups=mesh['ens'=8,'col'=4] {'ens'}, dimensions={0}, use_global_device_ids=true | all-gather | bytes 221184 | tf_op jit(solution)/shard_map/all_gather | solution.py:186
  105.3 0.6 add.43
  105.9 1.7 %collective-permute-start = (f32[32,192]{1,0:T(8,128)}, f32[32,192]{1,0:T(8,128)}, u32[]{:S(2)}, u32[]{:S(2)}) collective-permute-start(f32[32,192]{1,0:T(8,128)} %add.43), channel_id=1, source_target_pairs={{0,3},{1,0},{2,1},{3,2},{4,7},{5,4},{6,5},{7,6},{8,11},{9,8},{10,9... | collective-permute-start | bytes 73736 | tf_op jit(solution)/shard_map/ppermute | solution.py:191
  108.2 1.2 collective-permute-done.1
  109.6 0.6 slice.29
  110.2 1.0 copy.38
  111.2 1.5 %copy.29 = f32[32,192]{0,1:T(8,128)} copy(f32[32,192]{1,0:T(8,128)} %collective-permute-done) | data formatting | bytes 49152 | tf_op jit(solution)/shard_map/ppermute | solution.py:191
  112.7 1.5 %slice.28 = f32[32,3,8,4]{0,3,2,1:T(4,128)} slice(f32[32,3,8,8]{0,3,2,1:T(8,128)} %bitcast.9), slice={[0:32], [0:3], [0:8], [0:4]} | slice | bytes 24576 | tf_op jit(solution)/shard_map/slice | solution.py:195
  114.3 1.7 %copy.37 = f32[32,3,8,4]{3,2,1,0:T(8,128)} copy(f32[32,3,8,4]{0,3,2,1:T(4,128)} %slice.28) | data formatting | bytes 24576
  116.0 1.9 %pad_maximum_fusion.refs_3_ = f32[32,3,8,128]{3,2,1,0:T(8,128)} fusion(f32[32,3,8,4]{3,2,1,0:T(8,128)S(1)} %copy.38, f32[32,3,8,4]{3,2,1,0:T(8,128)} %copy.37, f32[128]{0:T(128)S(1)} %pad.1.clone), kind=kLoop, calls=%fused_computation.2 | loop fusion | flops 196608 | bytes 418304 | tf_op jit(solution)/shard_map/concatenate | solution.py:195
  117.9 1.7 %copy-done = f32[32,3,8,1024]{3,2,1,0:T(8,128)} copy-done((f32[32,3,8,1024]{3,2,1,0:T(8,128)}, f32[32,3,8,1024]{3,2,1,0:T(8,128)S(1)}, u32[]{:S(2)}) %copy-start) | copy-done | bytes 3145752
  119.6 16.2 %shard_map.37 = f32[32,3,8,1024]{3,2,1,0:T(8,128)} custom-call(s32[32]{0:T(128)} %add_bitcast_fusion.pos_ref, f32[32,3,8,1024]{3,2,1,0:T(8,128)} %copy-done, f32[32,3,8,1024]{3,2,1,0:T(8,128)} %copy-done, f32[32,3,8,1024]{3,2,1,0:T(8,128)} %refs_2_.1, f32[32,3,8,128]{3,2,1,0:T(8,128)} %pad_maximum_fusion.refs_3_), custom_call_target="tpu_custom_call" | custom-call | tf_op jit(solution)/shard_map/pallas_call | solution.py:172
  (23 shorter events, 2.4 us)
Async XLA Ops:
  6.1 13.6 %copy-start.1 = (s32[256]{0:T(256)S(1)}, s32[256]{0:T(256)}, u32[]{:S(2)}) copy-start(s32[256]{0:T(256)} %param.5) | copy-start | bytes 3076
  6.1 111.9 %all-to-all-start = ((f32[32,3,8,1024]{3,2,1,0:T(8,128)}), f32[32,3,8,1024]{3,2,1,0:T(8,128)S(1)}, u32[]{:S(2)}, u32[]{:S(2)}) async-start(f32[32,3,8,1024]{3,2,1,0:T(8,128)} %gather_fusion), calls=%async_computation | async-start | bytes 6291456 | tf_op jit(solution)/shard_map/all_to_all | solution.py:205
  105.9 3.6 %collective-permute-start.1 = (f32[32,192]{1,0:T(8,128)}, f32[32,192]{1,0:T(8,128)S(1)}, u32[]{:S(2)}, u32[]{:S(2)}) collective-permute-start(f32[32,192]{1,0:T(8,128)} %add.43), channel_id=1, source_target_pairs={{0,1},{1,2},{2,3},{3,0},{4,5},{5,6},{6,7},{7,4},{8,9},{9,10},{10,1... | collective-permute-start | bytes 73736 | tf_op jit(solution)/shard_map/ppermute | solution.py:190
  105.9 5.3 %collective-permute-start = (f32[32,192]{1,0:T(8,128)}, f32[32,192]{1,0:T(8,128)}, u32[]{:S(2)}, u32[]{:S(2)}) collective-permute-start(f32[32,192]{1,0:T(8,128)} %add.43), channel_id=1, source_target_pairs={{0,3},{1,0},{2,1},{3,2},{4,7},{5,4},{6,5},{7,6},{8,11},{9,8},{10,9... | collective-permute-start | bytes 73736 | tf_op jit(solution)/shard_map/ppermute | solution.py:191
  117.9 1.7 %copy-start = (f32[32,3,8,1024]{3,2,1,0:T(8,128)}, f32[32,3,8,1024]{3,2,1,0:T(8,128)S(1)}, u32[]{:S(2)}) copy-start(f32[32,3,8,1024]{3,2,1,0:T(8,128)S(1)} %all-to-all-done.refs_0_.refs_1_) | copy-start | bytes 9437188

commit v8 on v7

--- a/solution.py
+++ b/solution.py
@@ -176,14 +176,13 @@
     )(position, *([incoming] * group), noise, halo)
 
 
-def halo_block(state, noise, parents, me):
+def edges(a):
+    return jnp.concatenate([a[..., :STEPS], a[..., -STEPS:]], axis=-1).reshape(a.shape[0], -1)
+
+
+def halo_block(everyone, state, noise, parents, me):
     per_dev, nf, rows, cols = state.shape
     width = STEPS
-
-    def edges(a):
-        return jnp.concatenate([a[..., :width], a[..., -width:]], axis=-1).reshape(a.shape[0], -1)
-
-    everyone = lax.all_gather(edges(state), "ens", axis=0, tiled=True)
     mine = lax.dynamic_slice_in_dim(parents, me * per_dev, per_dev)
     child_edges = jnp.take(everyone, mine, axis=0, mode="clip") + edges(noise)
     ring = lax.axis_size("col")
@@ -202,8 +201,10 @@
     dist = max(1, -(-per_dev // count))
     send_index, position = routing(parents, count, per_dev, dist, me)
     outgoing = jnp.take(state, send_index, axis=0, mode="clip")
+    everyone = lax.all_gather(edges(state), "ens", axis=0, tiled=True)
+    everyone, outgoing = lax.optimization_barrier((everyone, outgoing))
     incoming = lax.all_to_all(outgoing, "ens", split_axis=0, concat_axis=0, tiled=True)
-    halo = halo_block(state, noise, parents, me)
+    halo = halo_block(everyone, state, noise, parents, me)
     return main_forecast(position, incoming, noise, halo)
 
 

time: 137 us -> 133 us (0.971)
  waiting for transfers between devices: 1.24 us -> 48.8 us
  blocking collectives: 79.3 us -> 34.5 us
  local copies, waits for them, and re-layouts: 24.3 us -> 20.5 us
  starting transfers between devices: 9.16 us -> 7.41 us
    all_to_all x1, waiting for transfers between devices: 0.01 us -> 47.8 us  [shards(): lax.all_to_all(outgoing, 'ens', split_axis=0, concat_axis=0, tiled=True)]
    all_gather x1, blocking collectives: 79.3 us -> 34.5 us  [shards(): everyone = lax.all_gather(edges(state), 'ens', axis=0, tiled=True)]
    gather x1, local copies, waits for them, and re-layouts: 4.31 us -> 2.41 us  [shards(): outgoing = jnp.take(state, send_index, axis=0, mode='clip')]
    all_to_all x1, starting transfers between devices: 7.42 us -> 5.62 us  [shards(): lax.all_to_all(outgoing, 'ens', split_axis=0, concat_axis=0, tiled=True)]
    ppermute x1, local copies, waits for them, and re-layouts: 1.49 us -> 0.1 us  [halo_block(): lax.ppermute(child_edges, 'col', [(i, (i - 1) % ring) for i in range(ring)])]
    unnamed x10 -> x12, local copies, waits for them, and re-layouts: 9.77 us -> 9.76 us
  transfers between devices with their start and end apart: 3 -> 3, of which waited for: 1 -> 2; matrix products, arithmetic and copies ran while one was open for 16% -> 10% of each run, Pallas kernels for 0% -> 0%
where the time goes in v8:
time: 133 us
  waiting for transfers between devices  48.8 us (37%)
  blocking collectives  34.5 us (26%)
  local copies, waits for them, and re-layouts  20.5 us (15%)
  Pallas kernels  16.2 us (12%)
  starting transfers between devices  7.41 us (6%)
  other arithmetic  4.95 us (4%)
    all_to_all x1, waiting for transfers between devices, shards(): lax.all_to_all(outgoing, 'ens', split_axis=0, concat_axis=0, tiled=True)  47.8 us
    all_gather x1, blocking collectives, shards(): everyone = lax.all_gather(edges(state), 'ens', axis=0, tiled=True)  34.5 us
    pallas_call x1, Pallas kernels, main_forecast(): pl.pallas_call(main_kernel, grid_spec=grid_spec, out_shape=jax.ShapeDtype...  16.2 us
    unnamed x12, local copies, waits for them, and re-layouts  9.76 us
    all_to_all x1, starting transfers between devices, shards(): lax.all_to_all(outgoing, 'ens', split_axis=0, concat_axis=0, tiled=True)  5.62 us
    slice x2, local copies, waits for them, and re-layouts, edges(): a[..., :STEPS]  3.95 us
  transfers between devices with their start and end apart: 3, of which 2 were waited for; matrix products, arithmetic and copies ran while one was open for 10% of the time, Pallas kernels for 0%

profile of v8, /device:TPU:0, one launch (start us, length us, event | category | flops | bytes accessed | tf_op | source)
XLA Modules:
  0.0 132.5 jit_solution(8327241317613532893)
XLA Ops:
  0.0 0.9 reshape.129
  1.9 2.0 %fusion.4 = (f32[32,3,8,4]{3,2,1,0:T(8,128)}, f32[32,3,8,4]{3,2,1,0:T(8,128)S(1)}) fusion(f32[32,3,8,1024]{3,2,1,0:T(8,128)} %param.3), kind=kLoop, calls=%fused_computation.24 | loop fusion | bytes 49152 | tf_op jit(solution)/shard_map/slice | solution.py:180
  3.9 1.8 %copy.33 = f32[32,3,8,4]{0,3,2,1:T(4,128)} copy(f32[32,3,8,4]{3,2,1,0:T(8,128)} %get-tuple-element.13) | data formatting | bytes 24576
  5.7 0.8 copy.34
  6.6 0.9 pad_maximum_fusion.1
  7.5 34.5 %all_gather.3 = f32[256,192]{1,0:T(8,128)} all-gather(f32[32,192]{1,0:T(8,128)S(1)} %copy.24), channel_id=1, replica_groups=mesh['ens'=8,'col'=4] {'ens'}, dimensions={0}, use_global_device_ids=true | all-gather | bytes 221184 | tf_op jit(solution)/shard_map/all_gather | solution.py:204
  42.0 2.4 %gather_fusion = f32[32,3,8,1024]{3,2,1,0:T(8,128)} fusion(f32[32,3,8,1024]{3,2,1,0:T(8,128)S(1)} %copy-done.1, s32[1024]{0:T(1024)S(1)} %pad_clamp_fusion.1), kind=kCustom, calls=%fused_computation | custom fusion | bytes 6291584 | tf_op jit(solution)/shard_map/jit(_take)/gather | solution.py:203
  44.4 5.6 %all-to-all-start = ((f32[32,3,8,1024]{3,2,1,0:T(8,128)}), f32[32,3,8,1024]{3,2,1,0:T(8,128)S(1)}, u32[]{:S(2)}, u32[]{:S(2)}) async-start(f32[32,3,8,1024]{3,2,1,0:T(8,128)} %gather_fusion), calls=%async_computation | async-start | bytes 6291456 | tf_op jit(solution)/shard_map/all_to_all | solution.py:206
  50.1 2.0 %fusion.3 = (f32[32,3,8,4]{3,2,1,0:T(8,128)}, f32[32,3,8,4]{3,2,1,0:T(8,128)S(1)}) fusion(f32[32,3,8,1024]{3,2,1,0:T(8,128)} %refs_2_.1), kind=kLoop, calls=%fused_computation.23 | loop fusion | bytes 49152 | tf_op jit(solution)/shard_map/slice | solution.py:180
  52.1 1.8 %copy.35 = f32[32,3,8,4]{0,3,2,1:T(4,128)} copy(f32[32,3,8,4]{3,2,1,0:T(8,128)} %get-tuple-element.11) | data formatting | bytes 24576
  53.9 0.8 copy.36
  54.8 0.9 pad_maximum_fusion.2
  55.7 1.6 %gather_fusion.1 = f32[32,192]{1,0:T(8,128)S(1)} fusion(f32[256,192]{1,0:T(8,128)} %all_gather.3, s32[1024]{0:T(1024)S(1)} %pad_clamp_fusion), kind=kCustom, calls=%fused_computation.1 | custom fusion | bytes 49280 | tf_op jit(solution)/shard_map/jit(_take)/gather | solution.py:187
  57.3 1.7 %collective-permute-start = (f32[32,192]{1,0:T(8,128)S(1)}, f32[32,192]{1,0:T(8,128)S(1)}, u32[]{:S(2)}, u32[]{:S(2)}) collective-permute-start(f32[32,192]{1,0:T(8,128)S(1)} %add.43), channel_id=1, source_target_pairs={{0,3},{1,0},{2,1},{3,2},{4,7},{5,4},{6,5},{7,6},{8,11},{9,8},{10,9... | collective-permute-start | bytes 73736 | tf_op jit(solution)/shard_map/ppermute | solution.py:190
  59.1 0.5 add_bitcast_fusion.pos_ref
  59.6 1.0 collective-permute-done
  60.8 0.6 slice.28
  61.5 0.6 slice.29
  62.1 1.0 copy.38
  63.2 1.8 %copy.37 = f32[32,3,8,4]{3,2,1,0:T(8,128)} copy(f32[32,3,8,4]{0,3,2,1:T(4,128)} %slice.28) | data formatting | bytes 24576
  64.9 1.9 %pad_maximum_fusion.refs_3_ = f32[32,3,8,128]{3,2,1,0:T(8,128)} fusion(f32[32,3,8,4]{3,2,1,0:T(8,128)S(1)} %copy.38, f32[32,3,8,4]{3,2,1,0:T(8,128)} %copy.37, f32[128]{0:T(128)S(1)} %pad.1.clone), kind=kLoop, calls=%fused_computation.2 | loop fusion | flops 196608 | bytes 418304 | tf_op jit(solution)/shard_map/concatenate | solution.py:194
  66.8 47.8 %all-to-all-done.refs_0_.refs_1_ = f32[32,3,8,1024]{3,2,1,0:T(8,128)S(1)} async-done(((f32[32,3,8,1024]{3,2,1,0:T(8,128)}), f32[32,3,8,1024]{3,2,1,0:T(8,128)S(1)}, u32[]{:S(2)}, u32[]{:S(2)}) %all-to-all-start) | async-done | bytes 3145760 | tf_op jit(solution)/shard_map/all_to_all | solution.py:206
  114.6 1.7 %copy-done = f32[32,3,8,1024]{3,2,1,0:T(8,128)} copy-done((f32[32,3,8,1024]{3,2,1,0:T(8,128)}, f32[32,3,8,1024]{3,2,1,0:T(8,128)S(1)}, u32[]{:S(2)}) %copy-start) | copy-done | bytes 3145752
  116.3 16.2 %shard_map.37 = f32[32,3,8,1024]{3,2,1,0:T(8,128)} custom-call(s32[32]{0:T(128)} %add_bitcast_fusion.pos_ref, f32[32,3,8,1024]{3,2,1,0:T(8,128)} %copy-done, f32[32,3,8,1024]{3,2,1,0:T(8,128)} %copy-done, f32[32,3,8,1024]{3,2,1,0:T(8,128)} %refs_2_.1, f32[32,3,8,128]{3,2,1,0:T(8,128)} %pad_maximum_fusion.refs_3_), custom_call_target="tpu_custom_call" | custom-call | tf_op jit(solution)/shard_map/pallas_call | solution.py:172
  (25 shorter events, 1.6 us)
Async XLA Ops:
  0.0 42.0 %copy-start.1 = (f32[32,3,8,1024]{3,2,1,0:T(8,128)S(1)}, f32[32,3,8,1024]{3,2,1,0:T(8,128)}, u32[]{:S(2)}) copy-start(f32[32,3,8,1024]{3,2,1,0:T(8,128)} %param.3) | copy-start | bytes 9437188
  44.4 5.6 %copy-start.2 = (s32[256]{0:T(256)S(1)}, s32[256]{0:T(256)}, u32[]{:S(2)}) copy-start(s32[256]{0:T(256)} %param.5) | copy-start | bytes 3076
  44.4 70.2 %all-to-all-start = ((f32[32,3,8,1024]{3,2,1,0:T(8,128)}), f32[32,3,8,1024]{3,2,1,0:T(8,128)S(1)}, u32[]{:S(2)}, u32[]{:S(2)}) async-start(f32[32,3,8,1024]{3,2,1,0:T(8,128)} %gather_fusion), calls=%async_computation | async-start | bytes 6291456 | tf_op jit(solution)/shard_map/all_to_all | solution.py:206
  57.3 4.1 %collective-permute-start.1 = (f32[32,192]{1,0:T(8,128)S(1)}, f32[32,192]{1,0:T(8,128)S(1)}, u32[]{:S(2)}, u32[]{:S(2)}) collective-permute-start(f32[32,192]{1,0:T(8,128)S(1)} %add.43), channel_id=1, source_target_pairs={{0,1},{1,2},{2,3},{3,0},{4,5},{5,6},{6,7},{7,4},{8,9},{9,10},{10,1... | collective-permute-start | bytes 73736 | tf_op jit(solution)/shard_map/ppermute | solution.py:189
  57.3 3.3 %collective-permute-start = (f32[32,192]{1,0:T(8,128)S(1)}, f32[32,192]{1,0:T(8,128)S(1)}, u32[]{:S(2)}, u32[]{:S(2)}) collective-permute-start(f32[32,192]{1,0:T(8,128)S(1)} %add.43), channel_id=1, source_target_pairs={{0,3},{1,0},{2,1},{3,2},{4,7},{5,4},{6,5},{7,6},{8,11},{9,8},{10,9... | collective-permute-start | bytes 73736 | tf_op jit(solution)/shard_map/ppermute | solution.py:190
  114.6 1.7 %copy-start = (f32[32,3,8,1024]{3,2,1,0:T(8,128)}, f32[32,3,8,1024]{3,2,1,0:T(8,128)S(1)}, u32[]{:S(2)}) copy-start(f32[32,3,8,1024]{3,2,1,0:T(8,128)S(1)} %all-to-all-done.refs_0_.refs_1_) | copy-start | bytes 9437188

commit v9 on v6

--- a/solution.py
+++ b/solution.py
@@ -7,7 +7,7 @@
 
 STEPS = 4
 LANES = 128
-PAIR = 2
+PAIR = 4
 EDGE_GROUP = 8
 GATHER_GROUP = 32
 

time: 111 us -> 107 us (0.964)
  Pallas kernels: 25.9 us -> 22.1 us
    pallas_call x1, Pallas kernels: 15.9 us -> 12.1 us  [main_forecast(): pl.pallas_call(main_kernel, grid_spec=grid_spec, out_shape=jax.ShapeDtype...]
  transfers between devices with their start and end apart: 3 -> 3, of which waited for: 1 -> 1; matrix products, arithmetic and copies ran while one was open for 0% -> 1% of each run, Pallas kernels for 15% -> 11%
where the time goes in v9:
time: 107 us; the launch traced here: 106 us
  waiting for transfers between devices  70.3 us (66%)
  Pallas kernels  22.1 us (21%)
  starting transfers between devices  7.83 us (7%)
  local copies, waits for them, and re-layouts  4.21 us (4%)
  other arithmetic  1.37 us (1%)
    all_to_all x1, waiting for transfers between devices, shards(): lax.all_to_all(outgoing, 'ens', split_axis=0, concat_axis=0, tiled=True)  70.3 us
    pallas_call x1, Pallas kernels, main_forecast(): pl.pallas_call(main_kernel, grid_spec=grid_spec, out_shape=jax.ShapeDtype...  12.1 us
    all_to_all x1, starting transfers between devices, shards(): lax.all_to_all(outgoing, 'ens', split_axis=0, concat_axis=0, tiled=True)  7.28 us
    pallas_call x1, Pallas kernels, edge_fix(): pl.pallas_call(edge_kernel, grid=(2,), in_specs=[whole, whole, whole, who...  6.78 us
    pallas_call x1, Pallas kernels, edge_blocks(): pl.pallas_call(edges_kernel, grid_spec=grid_spec, out_shape=[edge_shape,...  3.18 us
    gather x1, local copies, waits for them, and re-layouts, shards(): outgoing = jnp.take(state, send_index, axis=0, mode='clip')  2.41 us
  transfers between devices with their start and end apart: 3, of which 1 were waited for; matrix products, arithmetic and copies ran while one was open for 1% of the time, Pallas kernels for 11%

profile of v9, /device:TPU:0, one launch (start us, length us, event | category | flops | bytes accessed | tf_op | source)
XLA Modules:
  0.0 105.8 jit_solution(17232487628235218802)
XLA Ops:
  0.0 0.0 copy-start
  0.0 0.9 reshape.117
  0.9 0.3 and_reduce_fusion
  1.3 0.3 convert_reduce_fusion
  1.6 0.2 select_reduce_fusion
  1.7 0.1 copy.5
  1.8 0.1 reshape.120
  1.9 0.0 copy-done
  1.9 2.4 %gather_fusion = f32[32,3,8,1024]{3,2,1,0:T(8,128)} fusion(f32[32,3,8,1024]{3,2,1,0:T(8,128)S(1)} %copy-done, s32[1024]{0:T(1024)S(1)} %pad_clamp_fusion), kind=kCustom, calls=%fused_computation | custom fusion | bytes 6291584 | tf_op jit(solution)/shard_map/jit(_take)/gather | solution.py:276
  4.3 7.3 %all-to-all-start = ((f32[32,3,8,1024]{3,2,1,0:T(8,128)}), f32[32,3,8,1024]{3,2,1,0:T(8,128)}, u32[]{:S(2)}, u32[]{:S(2)}) async-start(f32[32,3,8,1024]{3,2,1,0:T(8,128)} %gather_fusion), calls=%async_computation | async-start | bytes 6291456 | tf_op jit(solution)/shard_map/all_to_all | solution.py:277
  11.6 0.5 add_bitcast_fusion.pos_ref
  12.2 70.3 %all-to-all-done.refs_0_.refs_1_.refs_2_.refs_3_.refs_4_.refs_5_.refs_6_.refs_7_.refs_8_.refs_9_.refs_10_.refs_11_.refs_12_.refs_13_.refs_14_.refs_15_.refs_16_.refs_17_.refs_18_.refs_19_.refs_20_.refs_21_.refs_22_.refs_23_.refs_24_.refs_25_.refs_26_.refs_27_.refs_28_.refs_29_.refs_30_.refs_31_.refs_32_.refs_33_.refs_34_.refs_35_.refs_36_.refs_37_.refs_38_.refs_39_.refs_40_.refs_41_.refs_42_.refs_43_.refs_44_.refs_45_.refs_46_.refs_47_.refs_48_.refs_49_.refs_50_.refs_51_.refs_52_.refs_53_.refs_54_.refs_55_.refs_56_.refs_57_.refs_58_.refs_59_.refs_60_.refs_61_.refs_62_.refs_63_ = f32[32,3,8,1024]{3,2,1,0:T(8,128)} async-done(((f32[32,3,8,1024]{3,2,1,0:T(8,128)}), ...) | async-done | bytes 3145760 | tf_op jit(solution)/shard_map/all_to_all | solution.py:277
  82.4 3.2 %shard_map.37 = (f32[32,3,8,128]{3,2,1,0:T(8,128)}, f32[32,3,8,128]{3,2,1,0:T(8,128)}) custom-call(s32[32]{0:T(128)} %add_bitcast_fusion.pos_ref, ...), custom_call_target="tpu_custom_call" | custom-call | tf_op jit(solution)/shard_map/pallas_call | solution.py:197
  85.6 0.1 collective-permute-start.1
  85.7 0.5 collective-permute-start
  86.2 12.1 %shard_map.38.body_ref = f32[32,3,8,1024]{3,2,1,0:T(8,128)} custom-call(s32[32]{0:T(128)} %add_bitcast_fusion.pos_ref, ...), custom_call_target="tpu_custom_call" | custom-call | tf_op jit(solution)/shard_map/pallas_call | solution.py:161
  98.3 0.0 collective-permute-done.1.from_right
  98.3 0.0 copy-start.1
  98.3 0.0 collective-permute-done.from_left
  98.3 0.7 copy-done.1
  99.0 6.8 %shard_map.39 = f32[32,3,8,1024]{3,2,1,0:T(8,128)} custom-call(f32[32,3,8,128]{3,2,1,0:T(8,128)} %get-tuple-element.7.lblk, f32[32,3,8,128]{3,2,1,0:T(8,128)} %get-tuple-element.8.rblk, f32[32,3,8,128]{3,2,1,0:T(8,128)} %collective-permute-done.from_left, f32[32,3,8,128]{3,2,1,0:T(8,128)} %copy-done.1, ...), custom_call_target="tpu_custom_call", output_to_operand_aliasing={{}: (4, {})} | custom-call | tf_op jit(solution)/shard_map/pallas_call | solution.py:254
  (4 shorter events, 0.0 us)
Async XLA Ops:
  0.0 1.9 %copy-start = (f32[32,3,8,1024]{3,2,1,0:T(8,128)S(1)}, f32[32,3,8,1024]{3,2,1,0:T(8,128)}, u32[]{:S(2)}) copy-start(f32[32,3,8,1024]{3,2,1,0:T(8,128)} %param.3) | copy-start | bytes 9437188
  4.3 78.1 %all-to-all-start = ((f32[32,3,8,1024]{3,2,1,0:T(8,128)}), f32[32,3,8,1024]{3,2,1,0:T(8,128)}, u32[]{:S(2)}, u32[]{:S(2)}) async-start(f32[32,3,8,1024]{3,2,1,0:T(8,128)} %gather_fusion), calls=%async_computation | async-start | bytes 6291456 | tf_op jit(solution)/shard_map/all_to_all | solution.py:277
  85.6 12.7 %collective-permute-start.1 = (f32[32,3,8,128]{3,2,1,0:T(8,128)}, f32[32,3,8,128]{3,2,1,0:T(8,128)S(1)}, u32[]{:S(2)}, u32[]{:S(2)}) collective-permute-start(f32[32,3,8,128]{3,2,1,0:T(8,128)} %get-tuple-element.7.lblk), channel_id=1, source_target_pairs={{0,3},{1,0},{2,1},{3,2},{4,7},{5,4},{6,5},{7,6},{8,11},{9,8},{10,9... | collective-permute-start | bytes 1179656 | tf_op jit(solution)/shard_map/ppermute | solution.py:281
  85.7 12.6 %collective-permute-start = (f32[32,3,8,128]{3,2,1,0:T(8,128)}, f32[32,3,8,128]{3,2,1,0:T(8,128)}, u32[]{:S(2)}, u32[]{:S(2)}) collective-permute-start(f32[32,3,8,128]{3,2,1,0:T(8,128)} %get-tuple-element.8.rblk), channel_id=1, source_target_pairs={{0,1},{1,2},{2,3},{3,0},{4,5},{5,6},{6,7},{7,4},{8,9},{9,10},{10,1... | collective-permute-start | bytes 1179656 | tf_op jit(solution)/shard_map/ppermute | solution.py:280
  98.3 0.7 copy-start.1

commit v10 on v9

--- a/solution.py
+++ b/solution.py
@@ -166,12 +166,17 @@
 
 
 def edges_kernel(pos_ref, *refs):
-    group = (len(refs) - 4) // 2
+    group = (len(refs) - 3) // 2
     left_rows, right_rows = refs[:group], refs[group:2 * group]
-    noise_left, noise_right, lblk, rblk = refs[2 * group:]
+    noise_left, noise_right, own = refs[2 * group:]
+    rows = own.shape[-2]
+    lane = lax.broadcasted_iota(jnp.int32, (rows, LANES), 1)
+    keep_left = (lane < 2 * STEPS) | (lane >= LANES - STEPS)
     for k in range(group):
-        lblk[k] = left_rows[k][0] + noise_left[k]
-        rblk[k] = right_rows[k][0] + noise_right[k]
+        for f in range(3):
+            left = left_rows[k][0, f] + noise_left[k, f]
+            right = pltpu.roll(right_rows[k][0, f] + noise_right[k, f], LANES // 2, 1)
+            own[k, f] = jnp.where(keep_left, left, right)
 
 
 def edge_blocks(position, incoming, noise):
@@ -187,84 +192,85 @@
     left = pl.BlockSpec((group, nf, rows, LANES), lambda i, pos: (i, 0, 0, 0))
     right = pl.BlockSpec((group, nf, rows, LANES), lambda i, pos: (i, 0, 0, last))
     out = pl.BlockSpec((group, nf, rows, LANES), lambda i, pos: (i, 0, 0, 0))
-    edge_shape = jax.ShapeDtypeStruct((per_dev, nf, rows, LANES), noise.dtype)
     grid_spec = pltpu.PrefetchScalarGridSpec(
         num_scalar_prefetch=1,
         grid=(per_dev // group,),
         in_specs=left_specs + right_specs + [left, right],
-        out_specs=[out, out],
+        out_specs=out,
     )
     return pl.pallas_call(
         edges_kernel,
         grid_spec=grid_spec,
-        out_shape=[edge_shape, edge_shape],
+        out_shape=jax.ShapeDtypeStruct((per_dev, nf, rows, LANES), noise.dtype),
     )(position, *([incoming] * (2 * group)), noise, noise)
 
 
-def edge_kernel(lblk, rblk, from_left, from_right, body_ref, out_ref, packed, first, second, result):
-    side = pl.program_id(0)
-    rows = lblk.shape[-2]
-    group = packed.shape[0]
+def edge_kernel(own, from_left, from_right, body, out, patch, first_buf, last_buf, sems):
+    rows = own.shape[-2]
+    cols = body.shape[-1]
+    group = EDGE_GROUP if own.shape[0] % EDGE_GROUP == 0 else 1
     lane = lax.broadcasted_iota(jnp.int32, (rows, LANES), 1)
-    half = LANES // 2
-    width = STEPS
-
-    @pl.when(side == 0)
-    def _():
-        def block(g, carry):
-            base = g * group
-            for k in range(group):
-                i = base + k
-                fields = []
-                for f in range(3):
-                    left = jnp.where(lane >= LANES - width, from_left[i, f], lblk[i, f])
-                    right = jnp.where(lane < width, from_right[i, f], rblk[i, f])
-                    right = pltpu.roll(right, half, 1)
-                    keep_left = (lane < 2 * width) | (lane >= LANES - width)
-                    fields.append(jnp.where(keep_left, left, right))
-                e, u, v = fields
-                for _ in range(STEPS):
-                    e, u, v = advance_vreg(e, u, v)
-                result[i, 0] = e
-                result[i, 1] = u
-                result[i, 2] = v
-            return carry
-
-        lax.fori_loop(0, lblk.shape[0] // group, block, 0)
-        out_ref[...] = jnp.where(lane < width, result[...], body_ref[...])
-
-    @pl.when(side == 1)
-    def _():
-        def particle(i, carry):
+    halo_lanes = (lane >= LANES - STEPS) | ((lane >= LANES // 2) & (lane < LANES // 2 + STEPS))
+    first_in = pltpu.make_async_copy(body.at[:, :, :, pl.ds(0, LANES)], first_buf, sems.at[0])
+    last_in = pltpu.make_async_copy(body.at[:, :, :, pl.ds(cols - LANES, LANES)], last_buf, sems.at[1])
+    first_in.start()
+    last_in.start()
+
+    def block(g, carry):
+        base = g * group
+        for k in range(group):
+            i = base + k
+            fields = []
             for f in range(3):
-                out_ref[i, f] = jnp.where(
-                    lane >= LANES - width, pltpu.roll(result[i, f], half, 1), body_ref[i, f]
-                )
-            return carry
-
-        lax.fori_loop(0, lblk.shape[0], particle, 0)
-
-
-def edge_fix(lblk, rblk, from_left, from_right, body):
-    per_dev, nf, rows, cols = body.shape
-    ncol = cols // LANES
-    group = EDGE_GROUP if per_dev % EDGE_GROUP == 0 else 1
-    whole = pl.BlockSpec((per_dev, nf, rows, LANES), lambda s: (0, 0, 0, 0))
-    edge = pl.BlockSpec((per_dev, nf, rows, LANES), lambda s: (0, 0, 0, s * (ncol - 1)))
+                received = jnp.where(lane < STEPS, from_right[i, f], from_left[i, f])
+                received = pltpu.roll(received, LANES // 2, 1)
+                fields.append(jnp.where(halo_lanes, received, own[i, f]))
+            e, u, v = fields
+            for _ in range(STEPS):
+                e, u, v = advance_vreg(e, u, v)
+            patch[i, 0] = e
+            patch[i, 1] = u
+            patch[i, 2] = v
+        return carry
+
+    lax.fori_loop(0, own.shape[0] // group, block, 0)
+    first_in.wait()
+    last_in.wait()
+
+    def merge(i, carry):
+        for f in range(3):
+            values = patch[i, f]
+            first_buf[i, f] = jnp.where(lane < STEPS, values, first_buf[i, f])
+            last_buf[i, f] = jnp.where(
+                lane >= LANES - STEPS, pltpu.roll(values, LANES // 2, 1), last_buf[i, f]
+            )
+        return carry
+
+    lax.fori_loop(0, own.shape[0], merge, 0)
+    first_out = pltpu.make_async_copy(first_buf, out.at[:, :, :, pl.ds(0, LANES)], sems.at[0])
+    last_out = pltpu.make_async_copy(last_buf, out.at[:, :, :, pl.ds(cols - LANES, LANES)], sems.at[1])
+    first_out.start()
+    last_out.start()
+    first_out.wait()
+    last_out.wait()
+
+
+def edge_fix(own, from_left, from_right, body):
+    whole = pl.BlockSpec(memory_space=pltpu.VMEM)
+    raw = pl.BlockSpec(memory_space=pl.ANY)
     return pl.pallas_call(
         edge_kernel,
-        grid=(2,),
-        in_specs=[whole, whole, whole, whole, edge],
-        out_specs=edge,
+        in_specs=[whole, whole, whole, raw],
+        out_specs=raw,
         out_shape=jax.ShapeDtypeStruct(body.shape, body.dtype),
         scratch_shapes=[
-            pltpu.VMEM((group, nf, rows, LANES), jnp.float32),
-            pltpu.VMEM((group, nf, rows, LANES), jnp.float32),
-            pltpu.VMEM((group, nf, rows, LANES), jnp.float32),
-            pltpu.VMEM((per_dev, nf, rows, LANES), jnp.float32),
+            pltpu.VMEM(own.shape, jnp.float32),
+            pltpu.VMEM(own.shape, jnp.float32),
+            pltpu.VMEM(own.shape, jnp.float32),
+            pltpu.SemaphoreType.DMA((2,)),
         ],
-        input_output_aliases={4: 0},
-    )(lblk, rblk, from_left, from_right, body)
+        input_output_aliases={3: 0},
+    )(own, from_left, from_right, body)
 
 
 def shards(state, noise, parents):
@@ -275,12 +281,12 @@
     send_index, position = routing(parents, count, per_dev, dist, me)
     outgoing = jnp.take(state, send_index, axis=0, mode="clip")
     incoming = lax.all_to_all(outgoing, "ens", split_axis=0, concat_axis=0, tiled=True)
-    lblk, rblk = edge_blocks(position, incoming, noise)
+    own = edge_blocks(position, incoming, noise)
     ring = lax.axis_size("col")
-    from_left = lax.ppermute(rblk, "col", [(i, (i + 1) % ring) for i in range(ring)])
-    from_right = lax.ppermute(lblk, "col", [(i, (i - 1) % ring) for i in range(ring)])
+    from_left = lax.ppermute(own, "col", [(i, (i + 1) % ring) for i in range(ring)])
+    from_right = lax.ppermute(own, "col", [(i, (i - 1) % ring) for i in range(ring)])
     body = main_forecast(position, incoming, noise)
-    return edge_fix(lblk, rblk, from_left, from_right, body)
+    return edge_fix(own, from_left, from_right, body)
 
 
 def solution(mesh):

time: 107 us -> 107 us (level)
  no operation moved by 1% of the time
where the time goes in v10:
time: 107 us; the launch traced here: 105 us
  waiting for transfers between devices  70.3 us (66%)
  Pallas kernels  21.7 us (20%)
  starting transfers between devices  7.83 us (7%)
  local copies, waits for them, and re-layouts  4.21 us (4%)
  other arithmetic  1.36 us (1%)
    all_to_all x1, waiting for transfers between devices, shards(): lax.all_to_all(outgoing, 'ens', split_axis=0, concat_axis=0, tiled=True)  70.3 us
    pallas_call x1, Pallas kernels, main_forecast(): pl.pallas_call(main_kernel, grid_spec=grid_spec, out_shape=jax.ShapeDtype...  12.1 us
    all_to_all x1, starting transfers between devices, shards(): lax.all_to_all(outgoing, 'ens', split_axis=0, concat_axis=0, tiled=True)  7.28 us
    pallas_call x1, Pallas kernels, edge_fix(): pl.pallas_call(edge_kernel, in_specs=[whole, whole, whole, raw], out_spec...  6.49 us
    pallas_call x1, Pallas kernels, edge_blocks(): pl.pallas_call(edges_kernel, grid_spec=grid_spec, out_shape=jax.ShapeDtyp...  3.13 us
    gather x1, local copies, waits for them, and re-layouts, shards(): outgoing = jnp.take(state, send_index, axis=0, mode='clip')  2.41 us
  transfers between devices with their start and end apart: 3, of which 1 were waited for; matrix products, arithmetic and copies ran while one was open for 1% of the time, Pallas kernels for 11%

profile of v10, /device:TPU:0, one launch (start us, length us, event | category | flops | bytes accessed | tf_op | source)
XLA Modules:
  0.0 105.5 jit_solution(791298269783189758)
XLA Ops:
  0.0 0.0 copy-start
  0.0 0.9 reshape.117
  0.9 0.3 and_reduce_fusion
  1.3 0.3 convert_reduce_fusion
  1.6 0.2 select_reduce_fusion
  1.7 0.1 copy.5
  1.8 0.1 reshape.120
  1.9 0.0 copy-done
  1.9 2.4 %gather_fusion = f32[32,3,8,1024]{3,2,1,0:T(8,128)} fusion(f32[32,3,8,1024]{3,2,1,0:T(8,128)S(1)} %copy-done, s32[1024]{0:T(1024)S(1)} %pad_clamp_fusion), kind=kCustom, calls=%fused_computation | custom fusion | bytes 6291584 | tf_op jit(solution)/shard_map/jit(_take)/gather | solution.py:282
  4.3 7.3 %all-to-all-start = ((f32[32,3,8,1024]{3,2,1,0:T(8,128)}), f32[32,3,8,1024]{3,2,1,0:T(8,128)}, u32[]{:S(2)}, u32[]{:S(2)}) async-start(f32[32,3,8,1024]{3,2,1,0:T(8,128)} %gather_fusion), calls=%async_computation | async-start | bytes 6291456 | tf_op jit(solution)/shard_map/all_to_all | solution.py:283
  11.6 0.5 add_bitcast_fusion.pos_ref
  12.2 70.3 %all-to-all-done.refs_0_.refs_1_.refs_2_.refs_3_.refs_4_.refs_5_.refs_6_.refs_7_.refs_8_.refs_9_.refs_10_.refs_11_.refs_12_.refs_13_.refs_14_.refs_15_.refs_16_.refs_17_.refs_18_.refs_19_.refs_20_.refs_21_.refs_22_.refs_23_.refs_24_.refs_25_.refs_26_.refs_27_.refs_28_.refs_29_.refs_30_.refs_31_.refs_32_.refs_33_.refs_34_.refs_35_.refs_36_.refs_37_.refs_38_.refs_39_.refs_40_.refs_41_.refs_42_.refs_43_.refs_44_.refs_45_.refs_46_.refs_47_.refs_48_.refs_49_.refs_50_.refs_51_.refs_52_.refs_53_.refs_54_.refs_55_.refs_56_.refs_57_.refs_58_.refs_59_.refs_60_.refs_61_.refs_62_.refs_63_ = f32[32,3,8,1024]{3,2,1,0:T(8,128)} async-done(((f32[32,3,8,1024]{3,2,1,0:T(8,128)}), ...) | async-done | bytes 3145760 | tf_op jit(solution)/shard_map/all_to_all | solution.py:283
  82.4 3.1 %shard_map.37.own = f32[32,3,8,128]{3,2,1,0:T(8,128)} custom-call(s32[32]{0:T(128)} %add_bitcast_fusion.pos_ref, ...), custom_call_target="tpu_custom_call" | custom-call | tf_op jit(solution)/shard_map/pallas_call | solution.py:201
  85.6 0.1 collective-permute-start.1
  85.6 0.5 collective-permute-start
  86.1 12.1 %shard_map.38.body = f32[32,3,8,1024]{3,2,1,0:T(8,128)} custom-call(s32[32]{0:T(128)} %add_bitcast_fusion.pos_ref, ...), custom_call_target="tpu_custom_call" | custom-call | tf_op jit(solution)/shard_map/pallas_call | solution.py:161
  98.2 0.0 collective-permute-done.1.from_right
  98.3 0.0 copy-start.1
  98.3 0.0 collective-permute-done.from_left
  98.3 0.7 copy-done.1
  99.0 6.5 %shard_map.39 = f32[32,3,8,1024]{3,2,1,0:T(8,128)} custom-call(f32[32,3,8,128]{3,2,1,0:T(8,128)} %shard_map.37.own, f32[32,3,8,128]{3,2,1,0:T(8,128)} %collective-permute-done.from_left, f32[32,3,8,128]{3,2,1,0:T(8,128)} %copy-done.1, f32[32,3,8,1024]{3,2,1,0:T(8,128)} %shard_map.38.body), custom_call_target="tpu_custom_call", output_to_operand_aliasing={{}: (3, {})} | custom-call | tf_op jit(solution)/shard_map/pallas_call | solution.py:261
  (4 shorter events, 0.0 us)
Async XLA Ops:
  0.0 1.9 %copy-start = (f32[32,3,8,1024]{3,2,1,0:T(8,128)S(1)}, f32[32,3,8,1024]{3,2,1,0:T(8,128)}, u32[]{:S(2)}) copy-start(f32[32,3,8,1024]{3,2,1,0:T(8,128)} %param.3) | copy-start | bytes 9437188
  4.3 78.1 %all-to-all-start = ((f32[32,3,8,1024]{3,2,1,0:T(8,128)}), f32[32,3,8,1024]{3,2,1,0:T(8,128)}, u32[]{:S(2)}, u32[]{:S(2)}) async-start(f32[32,3,8,1024]{3,2,1,0:T(8,128)} %gather_fusion), calls=%async_computation | async-start | bytes 6291456 | tf_op jit(solution)/shard_map/all_to_all | solution.py:283
  85.6 12.7 %collective-permute-start.1 = (f32[32,3,8,128]{3,2,1,0:T(8,128)}, f32[32,3,8,128]{3,2,1,0:T(8,128)S(1)}, u32[]{:S(2)}, u32[]{:S(2)}) collective-permute-start(f32[32,3,8,128]{3,2,1,0:T(8,128)} %shard_map.37.own), channel_id=1, source_target_pairs={{0,3},{1,0},{2,1},{3,2},{4,7},{5,4},{6,5},{7,6},{8,11},{9,8},{10,9... | collective-permute-start | bytes 1179656 | tf_op jit(solution)/shard_map/ppermute | solution.py:287
  85.6 12.6 %collective-permute-start = (f32[32,3,8,128]{3,2,1,0:T(8,128)}, f32[32,3,8,128]{3,2,1,0:T(8,128)}, u32[]{:S(2)}, u32[]{:S(2)}) collective-permute-start(f32[32,3,8,128]{3,2,1,0:T(8,128)} %shard_map.37.own), channel_id=1, source_target_pairs={{0,1},{1,2},{2,3},{3,0},{4,5},{5,6},{6,7},{7,4},{8,9},{9,10},{10,1... | collective-permute-start | bytes 1179656 | tf_op jit(solution)/shard_map/ppermute | solution.py:286
  98.3 0.7 copy-start.1

commit v11 on v10

--- a/solution.py
+++ b/solution.py
@@ -8,7 +8,7 @@
 STEPS = 4
 LANES = 128
 PAIR = 4
-EDGE_GROUP = 8
+EDGE_GROUP = 32
 GATHER_GROUP = 32
 
 time_step = 0.3

time: 107 us -> 110 us (1.028)
  Pallas kernels: 21.7 us -> 25.4 us
    pallas_call x1, Pallas kernels: 6.49 us -> 10.1 us  [edge_fix(): pl.pallas_call(edge_kernel, in_specs=[whole, whole, whole, raw], out_spec...]
  transfers between devices with their start and end apart: 3 -> 3, of which waited for: 1 -> 1; matrix products, arithmetic and copies ran while one was open for 1% -> 0% of each run, Pallas kernels for 11% -> 11%
where the time goes in v11:
time: 110 us; the launch traced here: 109 us
  waiting for transfers between devices  70.3 us (64%)
  Pallas kernels  25.4 us (23%)
  starting transfers between devices  7.83 us (7%)
  local copies, waits for them, and re-layouts  4.21 us (4%)
  other arithmetic  1.36 us (1%)
    all_to_all x1, waiting for transfers between devices, shards(): lax.all_to_all(outgoing, 'ens', split_axis=0, concat_axis=0, tiled=True)  70.3 us
    pallas_call x1, Pallas kernels, main_forecast(): pl.pallas_call(main_kernel, grid_spec=grid_spec, out_shape=jax.ShapeDtype...  12.1 us
    pallas_call x1, Pallas kernels, edge_fix(): pl.pallas_call(edge_kernel, in_specs=[whole, whole, whole, raw], out_spec...  10.1 us
    all_to_all x1, starting transfers between devices, shards(): lax.all_to_all(outgoing, 'ens', split_axis=0, concat_axis=0, tiled=True)  7.28 us
    pallas_call x1, Pallas kernels, edge_blocks(): pl.pallas_call(edges_kernel, grid_spec=grid_spec, out_shape=jax.ShapeDtyp...  3.13 us
    gather x1, local copies, waits for them, and re-layouts, shards(): outgoing = jnp.take(state, send_index, axis=0, mode='clip')  2.41 us
  transfers between devices with their start and end apart: 3, of which 1 were waited for; matrix products, arithmetic and copies ran while one was open for 0% of the time, Pallas kernels for 11%

profile of v11, /device:TPU:0, one launch (start us, length us, event | category | flops | bytes accessed | tf_op | source)
XLA Modules:
  0.0 109.2 jit_solution(15110289985354863996)
XLA Ops:
  0.0 0.0 copy-start
  0.0 0.9 reshape.117
  0.9 0.3 and_reduce_fusion
  1.3 0.3 convert_reduce_fusion
  1.6 0.2 select_reduce_fusion
  1.7 0.1 copy.5
  1.8 0.1 reshape.120
  1.9 0.0 copy-done
  1.9 2.4 %gather_fusion = f32[32,3,8,1024]{3,2,1,0:T(8,128)} fusion(f32[32,3,8,1024]{3,2,1,0:T(8,128)S(1)} %copy-done, s32[1024]{0:T(1024)S(1)} %pad_clamp_fusion), kind=kCustom, calls=%fused_computation | custom fusion | bytes 6291584 | tf_op jit(solution)/shard_map/jit(_take)/gather | solution.py:282
  4.3 7.3 %all-to-all-start = ((f32[32,3,8,1024]{3,2,1,0:T(8,128)}), f32[32,3,8,1024]{3,2,1,0:T(8,128)}, u32[]{:S(2)}, u32[]{:S(2)}) async-start(f32[32,3,8,1024]{3,2,1,0:T(8,128)} %gather_fusion), calls=%async_computation | async-start | bytes 6291456 | tf_op jit(solution)/shard_map/all_to_all | solution.py:283
  11.6 0.5 add_bitcast_fusion.pos_ref
  12.2 70.3 %all-to-all-done.refs_0_.refs_1_.refs_2_.refs_3_.refs_4_.refs_5_.refs_6_.refs_7_.refs_8_.refs_9_.refs_10_.refs_11_.refs_12_.refs_13_.refs_14_.refs_15_.refs_16_.refs_17_.refs_18_.refs_19_.refs_20_.refs_21_.refs_22_.refs_23_.refs_24_.refs_25_.refs_26_.refs_27_.refs_28_.refs_29_.refs_30_.refs_31_.refs_32_.refs_33_.refs_34_.refs_35_.refs_36_.refs_37_.refs_38_.refs_39_.refs_40_.refs_41_.refs_42_.refs_43_.refs_44_.refs_45_.refs_46_.refs_47_.refs_48_.refs_49_.refs_50_.refs_51_.refs_52_.refs_53_.refs_54_.refs_55_.refs_56_.refs_57_.refs_58_.refs_59_.refs_60_.refs_61_.refs_62_.refs_63_ = f32[32,3,8,1024]{3,2,1,0:T(8,128)} async-done(((f32[32,3,8,1024]{3,2,1,0:T(8,128)}), ...) | async-done | bytes 3145760 | tf_op jit(solution)/shard_map/all_to_all | solution.py:283
  82.4 3.1 %shard_map.37.own = f32[32,3,8,128]{3,2,1,0:T(8,128)} custom-call(s32[32]{0:T(128)} %add_bitcast_fusion.pos_ref, ...), custom_call_target="tpu_custom_call" | custom-call | tf_op jit(solution)/shard_map/pallas_call | solution.py:201
  85.6 0.1 collective-permute-start.1
  85.6 0.5 collective-permute-start
  86.1 12.1 %shard_map.38.body = f32[32,3,8,1024]{3,2,1,0:T(8,128)} custom-call(s32[32]{0:T(128)} %add_bitcast_fusion.pos_ref, ...), custom_call_target="tpu_custom_call" | custom-call | tf_op jit(solution)/shard_map/pallas_call | solution.py:161
  98.3 0.0 collective-permute-done.1.from_right
  98.3 0.0 copy-start.1
  98.3 0.0 collective-permute-done.from_left
  98.3 0.7 copy-done.1
  99.0 10.1 %shard_map.39 = f32[32,3,8,1024]{3,2,1,0:T(8,128)} custom-call(f32[32,3,8,128]{3,2,1,0:T(8,128)} %shard_map.37.own, f32[32,3,8,128]{3,2,1,0:T(8,128)} %collective-permute-done.from_left, f32[32,3,8,128]{3,2,1,0:T(8,128)} %copy-done.1, f32[32,3,8,1024]{3,2,1,0:T(8,128)} %shard_map.38.body), custom_call_target="tpu_custom_call", output_to_operand_aliasing={{}: (3, {})} | custom-call | tf_op jit(solution)/shard_map/pallas_call | solution.py:261
  (4 shorter events, 0.0 us)
Async XLA Ops:
  0.0 1.9 %copy-start = (f32[32,3,8,1024]{3,2,1,0:T(8,128)S(1)}, f32[32,3,8,1024]{3,2,1,0:T(8,128)}, u32[]{:S(2)}) copy-start(f32[32,3,8,1024]{3,2,1,0:T(8,128)} %param.3) | copy-start | bytes 9437188
  4.3 78.1 %all-to-all-start = ((f32[32,3,8,1024]{3,2,1,0:T(8,128)}), f32[32,3,8,1024]{3,2,1,0:T(8,128)}, u32[]{:S(2)}, u32[]{:S(2)}) async-start(f32[32,3,8,1024]{3,2,1,0:T(8,128)} %gather_fusion), calls=%async_computation | async-start | bytes 6291456 | tf_op jit(solution)/shard_map/all_to_all | solution.py:283
  85.6 12.7 %collective-permute-start.1 = (f32[32,3,8,128]{3,2,1,0:T(8,128)}, f32[32,3,8,128]{3,2,1,0:T(8,128)S(1)}, u32[]{:S(2)}, u32[]{:S(2)}) collective-permute-start(f32[32,3,8,128]{3,2,1,0:T(8,128)} %shard_map.37.own), channel_id=1, source_target_pairs={{0,3},{1,0},{2,1},{3,2},{4,7},{5,4},{6,5},{7,6},{8,11},{9,8},{10,9... | collective-permute-start | bytes 1179656 | tf_op jit(solution)/shard_map/ppermute | solution.py:287
  85.6 12.6 %collective-permute-start = (f32[32,3,8,128]{3,2,1,0:T(8,128)}, f32[32,3,8,128]{3,2,1,0:T(8,128)}, u32[]{:S(2)}, u32[]{:S(2)}) collective-permute-start(f32[32,3,8,128]{3,2,1,0:T(8,128)} %shard_map.37.own), channel_id=1, source_target_pairs={{0,1},{1,2},{2,3},{3,0},{4,5},{5,6},{6,7},{7,4},{8,9},{9,10},{10,1... | collective-permute-start | bytes 1179656 | tf_op jit(solution)/shard_map/ppermute | solution.py:286
  98.3 0.7 copy-start.1

commit v12 on v10

--- a/solution.py
+++ b/solution.py
@@ -208,45 +208,56 @@
 def edge_kernel(own, from_left, from_right, body, out, patch, first_buf, last_buf, sems):
     rows = own.shape[-2]
     cols = body.shape[-1]
-    group = EDGE_GROUP if own.shape[0] % EDGE_GROUP == 0 else 1
     lane = lax.broadcasted_iota(jnp.int32, (rows, LANES), 1)
-    halo_lanes = (lane >= LANES - STEPS) | ((lane >= LANES // 2) & (lane < LANES // 2 + STEPS))
     first_in = pltpu.make_async_copy(body.at[:, :, :, pl.ds(0, LANES)], first_buf, sems.at[0])
     last_in = pltpu.make_async_copy(body.at[:, :, :, pl.ds(cols - LANES, LANES)], last_buf, sems.at[1])
     first_in.start()
     last_in.start()
 
-    def block(g, carry):
-        base = g * group
-        for k in range(group):
-            i = base + k
-            fields = []
-            for f in range(3):
-                received = jnp.where(lane < STEPS, from_right[i, f], from_left[i, f])
-                received = pltpu.roll(received, LANES // 2, 1)
-                fields.append(jnp.where(halo_lanes, received, own[i, f]))
-            e, u, v = fields
-            for _ in range(STEPS):
-                e, u, v = advance_vreg(e, u, v)
-            patch[i, 0] = e
-            patch[i, 1] = u
-            patch[i, 2] = v
-        return carry
-
-    lax.fori_loop(0, own.shape[0] // group, block, 0)
+    slot = 16
+    per_vreg = LANES // (2 * slot)
+    groups = own.shape[0] // per_vreg
+
+    def span(lo, size):
+        return (lane >= lo) & (lane < lo + size)
+
+    def moved(x, shift):
+        return pltpu.roll(x, shift % LANES, 1)
+
+    for g in range(groups):
+        fields = []
+        for f in range(3):
+            packed = jnp.zeros((rows, LANES), jnp.float32)
+            for k in range(per_vreg):
+                i = g * per_vreg + k
+                b = 2 * k * slot
+                c = b + slot
+                mine = own[i, f]
+                packed = jnp.where(span(b, STEPS), moved(from_left[i, f], b - (LANES // 2 - STEPS)), packed)
+                packed = jnp.where(span(b + STEPS, 2 * STEPS), moved(mine, b + STEPS), packed)
+                packed = jnp.where(span(c, 2 * STEPS), moved(mine, c - LANES // 2 + 2 * STEPS), packed)
+                packed = jnp.where(span(c + 2 * STEPS, STEPS), moved(from_right[i, f], c + 2 * STEPS), packed)
+            fields.append(packed)
+        e, u, v = fields
+        for _ in range(STEPS):
+            e, u, v = advance_vreg(e, u, v)
+        patch[g, 0] = e
+        patch[g, 1] = u
+        patch[g, 2] = v
+
     first_in.wait()
     last_in.wait()
-
-    def merge(i, carry):
-        for f in range(3):
-            values = patch[i, f]
-            first_buf[i, f] = jnp.where(lane < STEPS, values, first_buf[i, f])
-            last_buf[i, f] = jnp.where(
-                lane >= LANES - STEPS, pltpu.roll(values, LANES // 2, 1), last_buf[i, f]
-            )
-        return carry
-
-    lax.fori_loop(0, own.shape[0], merge, 0)
+    for g in range(groups):
+        for k in range(per_vreg):
+            i = g * per_vreg + k
+            b = 2 * k * slot
+            c = b + slot
+            for f in range(3):
+                values = patch[g, f]
+                first_buf[i, f] = jnp.where(lane < STEPS, moved(values, -(b + STEPS)), first_buf[i, f])
+                last_buf[i, f] = jnp.where(
+                    lane >= LANES - STEPS, moved(values, LANES - 2 * STEPS - c), last_buf[i, f]
+                )
     first_out = pltpu.make_async_copy(first_buf, out.at[:, :, :, pl.ds(0, LANES)], sems.at[0])
     last_out = pltpu.make_async_copy(last_buf, out.at[:, :, :, pl.ds(cols - LANES, LANES)], sems.at[1])
     first_out.start()
@@ -264,7 +275,7 @@
         out_specs=raw,
         out_shape=jax.ShapeDtypeStruct(body.shape, body.dtype),
         scratch_shapes=[
-            pltpu.VMEM(own.shape, jnp.float32),
+            pltpu.VMEM((own.shape[0] // 4,) + own.shape[1:], jnp.float32),
             pltpu.VMEM(own.shape, jnp.float32),
             pltpu.VMEM(own.shape, jnp.float32),
             pltpu.SemaphoreType.DMA((2,)),

time: 107 us -> 104 us (0.972)
  Pallas kernels: 21.7 us -> 19.4 us
    pallas_call x1, Pallas kernels: 6.49 us -> 4.18 us  [edge_fix(): pl.pallas_call(edge_kernel, in_specs=[whole, whole, whole, raw], out_spec...]
  transfers between devices with their start and end apart: 3 -> 3, of which waited for: 1 -> 1; matrix products, arithmetic and copies ran while one was open for 1% -> 1% of each run, Pallas kernels for 11% -> 12%
where the time goes in v12:
time: 104 us; the launch traced here: 103 us
  waiting for transfers between devices  70.3 us (68%)
  Pallas kernels  19.4 us (19%)
  starting transfers between devices  7.83 us (8%)
  local copies, waits for them, and re-layouts  4.21 us (4%)
  other arithmetic  1.36 us (1%)
    all_to_all x1, waiting for transfers between devices, shards(): lax.all_to_all(outgoing, 'ens', split_axis=0, concat_axis=0, tiled=True)  70.3 us
    pallas_call x1, Pallas kernels, main_forecast(): pl.pallas_call(main_kernel, grid_spec=grid_spec, out_shape=jax.ShapeDtype...  12.1 us
    all_to_all x1, starting transfers between devices, shards(): lax.all_to_all(outgoing, 'ens', split_axis=0, concat_axis=0, tiled=True)  7.28 us
    pallas_call x1, Pallas kernels, edge_fix(): pl.pallas_call(edge_kernel, in_specs=[whole, whole, whole, raw], out_spec...  4.18 us
    pallas_call x1, Pallas kernels, edge_blocks(): pl.pallas_call(edges_kernel, grid_spec=grid_spec, out_shape=jax.ShapeDtyp...  3.13 us
    gather x1, local copies, waits for them, and re-layouts, shards(): outgoing = jnp.take(state, send_index, axis=0, mode='clip')  2.41 us
  transfers between devices with their start and end apart: 3, of which 1 were waited for; matrix products, arithmetic and copies ran while one was open for 1% of the time, Pallas kernels for 12%

profile of v12, /device:TPU:0, one launch (start us, length us, event | category | flops | bytes accessed | tf_op | source)
XLA Modules:
  0.0 103.2 jit_solution(2811785606619113558)
XLA Ops:
  0.0 0.0 copy-start
  0.0 0.9 reshape.117
  0.9 0.3 and_reduce_fusion
  1.3 0.3 convert_reduce_fusion
  1.6 0.2 select_reduce_fusion
  1.7 0.1 copy.5
  1.8 0.1 reshape.120
  1.9 0.0 copy-done
  1.9 2.4 %gather_fusion = f32[32,3,8,1024]{3,2,1,0:T(8,128)} fusion(f32[32,3,8,1024]{3,2,1,0:T(8,128)S(1)} %copy-done, s32[1024]{0:T(1024)S(1)} %pad_clamp_fusion), kind=kCustom, calls=%fused_computation | custom fusion | bytes 6291584 | tf_op jit(solution)/shard_map/jit(_take)/gather | solution.py:293
  4.3 7.3 %all-to-all-start = ((f32[32,3,8,1024]{3,2,1,0:T(8,128)}), f32[32,3,8,1024]{3,2,1,0:T(8,128)}, u32[]{:S(2)}, u32[]{:S(2)}) async-start(f32[32,3,8,1024]{3,2,1,0:T(8,128)} %gather_fusion), calls=%async_computation | async-start | bytes 6291456 | tf_op jit(solution)/shard_map/all_to_all | solution.py:294
  11.6 0.5 add_bitcast_fusion.pos_ref
  12.2 70.3 %all-to-all-done.refs_0_.refs_1_.refs_2_.refs_3_.refs_4_.refs_5_.refs_6_.refs_7_.refs_8_.refs_9_.refs_10_.refs_11_.refs_12_.refs_13_.refs_14_.refs_15_.refs_16_.refs_17_.refs_18_.refs_19_.refs_20_.refs_21_.refs_22_.refs_23_.refs_24_.refs_25_.refs_26_.refs_27_.refs_28_.refs_29_.refs_30_.refs_31_.refs_32_.refs_33_.refs_34_.refs_35_.refs_36_.refs_37_.refs_38_.refs_39_.refs_40_.refs_41_.refs_42_.refs_43_.refs_44_.refs_45_.refs_46_.refs_47_.refs_48_.refs_49_.refs_50_.refs_51_.refs_52_.refs_53_.refs_54_.refs_55_.refs_56_.refs_57_.refs_58_.refs_59_.refs_60_.refs_61_.refs_62_.refs_63_ = f32[32,3,8,1024]{3,2,1,0:T(8,128)} async-done(((f32[32,3,8,1024]{3,2,1,0:T(8,128)}), ...) | async-done | bytes 3145760 | tf_op jit(solution)/shard_map/all_to_all | solution.py:294
  82.4 3.1 %shard_map.37.own = f32[32,3,8,128]{3,2,1,0:T(8,128)} custom-call(s32[32]{0:T(128)} %add_bitcast_fusion.pos_ref, ...), custom_call_target="tpu_custom_call" | custom-call | tf_op jit(solution)/shard_map/pallas_call | solution.py:201
  85.6 0.1 collective-permute-start.1
  85.6 0.5 collective-permute-start
  86.1 12.1 %shard_map.38.body = f32[32,3,8,1024]{3,2,1,0:T(8,128)} custom-call(s32[32]{0:T(128)} %add_bitcast_fusion.pos_ref, ...), custom_call_target="tpu_custom_call" | custom-call | tf_op jit(solution)/shard_map/pallas_call | solution.py:161
  98.3 0.0 collective-permute-done.1.from_right
  98.3 0.0 copy-start.1
  98.3 0.0 collective-permute-done.from_left
  98.3 0.7 copy-done.1
  99.0 4.2 %shard_map.39 = f32[32,3,8,1024]{3,2,1,0:T(8,128)} custom-call(f32[32,3,8,128]{3,2,1,0:T(8,128)} %shard_map.37.own, f32[32,3,8,128]{3,2,1,0:T(8,128)} %collective-permute-done.from_left, f32[32,3,8,128]{3,2,1,0:T(8,128)} %copy-done.1, f32[32,3,8,1024]{3,2,1,0:T(8,128)} %shard_map.38.body), custom_call_target="tpu_custom_call", output_to_operand_aliasing={{}: (3, {})} | custom-call | tf_op jit(solution)/shard_map/pallas_call | solution.py:272
  (4 shorter events, 0.0 us)
Async XLA Ops:
  0.0 1.9 %copy-start = (f32[32,3,8,1024]{3,2,1,0:T(8,128)S(1)}, f32[32,3,8,1024]{3,2,1,0:T(8,128)}, u32[]{:S(2)}) copy-start(f32[32,3,8,1024]{3,2,1,0:T(8,128)} %param.3) | copy-start | bytes 9437188
  4.3 78.1 %all-to-all-start = ((f32[32,3,8,1024]{3,2,1,0:T(8,128)}), f32[32,3,8,1024]{3,2,1,0:T(8,128)}, u32[]{:S(2)}, u32[]{:S(2)}) async-start(f32[32,3,8,1024]{3,2,1,0:T(8,128)} %gather_fusion), calls=%async_computation | async-start | bytes 6291456 | tf_op jit(solution)/shard_map/all_to_all | solution.py:294
  85.6 12.7 %collective-permute-start.1 = (f32[32,3,8,128]{3,2,1,0:T(8,128)}, f32[32,3,8,128]{3,2,1,0:T(8,128)S(1)}, u32[]{:S(2)}, u32[]{:S(2)}) collective-permute-start(f32[32,3,8,128]{3,2,1,0:T(8,128)} %shard_map.37.own), channel_id=1, source_target_pairs={{0,3},{1,0},{2,1},{3,2},{4,7},{5,4},{6,5},{7,6},{8,11},{9,8},{10,9... | collective-permute-start | bytes 1179656 | tf_op jit(solution)/shard_map/ppermute | solution.py:298
  85.6 12.6 %collective-permute-start = (f32[32,3,8,128]{3,2,1,0:T(8,128)}, f32[32,3,8,128]{3,2,1,0:T(8,128)}, u32[]{:S(2)}, u32[]{:S(2)}) collective-permute-start(f32[32,3,8,128]{3,2,1,0:T(8,128)} %shard_map.37.own), channel_id=1, source_target_pairs={{0,1},{1,2},{2,3},{3,0},{4,5},{5,6},{6,7},{7,4},{8,9},{9,10},{10,1... | collective-permute-start | bytes 1179656 | tf_op jit(solution)/shard_map/ppermute | solution.py:297
  98.3 0.7 copy-start.1

commit v13 on v12

--- a/solution.py
+++ b/solution.py
@@ -165,44 +165,41 @@
     )(position, *([incoming] * group), noise)
 
 
-def edges_kernel(pos_ref, *refs):
-    group = (len(refs) - 3) // 2
-    left_rows, right_rows = refs[:group], refs[group:2 * group]
-    noise_left, noise_right, own = refs[2 * group:]
+def edges_kernel(pos_ref, inc_left, inc_right, noise_left, noise_right, own):
     rows = own.shape[-2]
     lane = lax.broadcasted_iota(jnp.int32, (rows, LANES), 1)
     keep_left = (lane < 2 * STEPS) | (lane >= LANES - STEPS)
-    for k in range(group):
+
+    def particle(k, carry):
+        row = pos_ref[k]
         for f in range(3):
-            left = left_rows[k][0, f] + noise_left[k, f]
-            right = pltpu.roll(right_rows[k][0, f] + noise_right[k, f], LANES // 2, 1)
+            left = inc_left[row, f] + noise_left[k, f]
+            right = pltpu.roll(inc_right[row, f] + noise_right[k, f], LANES // 2, 1)
             own[k, f] = jnp.where(keep_left, left, right)
+        return carry
+
+    lax.fori_loop(0, own.shape[0], particle, 0)
 
 
 def edge_blocks(position, incoming, noise):
     per_dev, nf, rows, cols = noise.shape
     last = cols // LANES - 1
-    group = GATHER_GROUP if per_dev % GATHER_GROUP == 0 else 1
-
-    def row_map(k, col):
-        return lambda i, pos: (pos[i * group + k], 0, 0, col)
-
-    left_specs = [pl.BlockSpec((1, nf, rows, LANES), row_map(k, 0)) for k in range(group)]
-    right_specs = [pl.BlockSpec((1, nf, rows, LANES), row_map(k, last)) for k in range(group)]
-    left = pl.BlockSpec((group, nf, rows, LANES), lambda i, pos: (i, 0, 0, 0))
-    right = pl.BlockSpec((group, nf, rows, LANES), lambda i, pos: (i, 0, 0, last))
-    out = pl.BlockSpec((group, nf, rows, LANES), lambda i, pos: (i, 0, 0, 0))
+    sources = incoming.shape[0]
+    inc_first = pl.BlockSpec((sources, nf, rows, LANES), lambda i, pos: (0, 0, 0, 0))
+    inc_last = pl.BlockSpec((sources, nf, rows, LANES), lambda i, pos: (0, 0, 0, last))
+    first = pl.BlockSpec((per_dev, nf, rows, LANES), lambda i, pos: (0, 0, 0, 0))
+    final = pl.BlockSpec((per_dev, nf, rows, LANES), lambda i, pos: (0, 0, 0, last))
     grid_spec = pltpu.PrefetchScalarGridSpec(
         num_scalar_prefetch=1,
-        grid=(per_dev // group,),
-        in_specs=left_specs + right_specs + [left, right],
-        out_specs=out,
+        grid=(1,),
+        in_specs=[inc_first, inc_last, first, final],
+        out_specs=first,
     )
     return pl.pallas_call(
         edges_kernel,
         grid_spec=grid_spec,
         out_shape=jax.ShapeDtypeStruct((per_dev, nf, rows, LANES), noise.dtype),
-    )(position, *([incoming] * (2 * group)), noise, noise)
+    )(position, incoming, incoming, noise, noise)
 
 
 def edge_kernel(own, from_left, from_right, body, out, patch, first_buf, last_buf, sems):

time: 104 us -> 106 us (1.019)
  Pallas kernels: 19.4 us -> 21.4 us
    pallas_call x1, Pallas kernels: 3.13 us -> 5.12 us  [edge_blocks(): pl.pallas_call(edges_kernel, grid_spec=grid_spec, out_shape=jax.ShapeDtyp...]
where the time goes in v13:
time: 106 us; the launch traced here: 105 us
  waiting for transfers between devices  70.3 us (66%)
  Pallas kernels  21.4 us (20%)
  starting transfers between devices  7.79 us (7%)
  local copies, waits for them, and re-layouts  4.21 us (4%)
  other arithmetic  1.36 us (1%)
    all_to_all x1, waiting for transfers between devices, shards(): lax.all_to_all(outgoing, 'ens', split_axis=0, concat_axis=0, tiled=True)  70.3 us
    pallas_call x1, Pallas kernels, main_forecast(): pl.pallas_call(main_kernel, grid_spec=grid_spec, out_shape=jax.ShapeDtype...  12.1 us
    all_to_all x1, starting transfers between devices, shards(): lax.all_to_all(outgoing, 'ens', split_axis=0, concat_axis=0, tiled=True)  7.28 us
    pallas_call x1, Pallas kernels, edge_blocks(): pl.pallas_call(edges_kernel, grid_spec=grid_spec, out_shape=jax.ShapeDtyp...  5.12 us
    pallas_call x1, Pallas kernels, edge_fix(): pl.pallas_call(edge_kernel, in_specs=[whole, whole, whole, raw], out_spec...  4.18 us
    gather x1, local copies, waits for them, and re-layouts, shards(): outgoing = jnp.take(state, send_index, axis=0, mode='clip')  2.41 us
  transfers between devices with their start and end apart: 3, of which 1 were waited for; matrix products, arithmetic and copies ran while one was open for 1% of the time, Pallas kernels for 12%

profile of v13, /device:TPU:0, one launch (start us, length us, event | category | flops | bytes accessed | tf_op | source)
XLA Modules:
  0.0 105.1 jit_solution(3905231328033579762)
XLA Ops:
  0.0 0.0 copy-start
  0.0 0.9 reshape.117
  0.9 0.3 and_reduce_fusion
  1.3 0.3 convert_reduce_fusion
  1.6 0.2 select_reduce_fusion
  1.7 0.1 copy.5
  1.8 0.1 reshape.120
  1.9 0.0 copy-done
  1.9 2.4 %gather_fusion = f32[32,3,8,1024]{3,2,1,0:T(8,128)} fusion(f32[32,3,8,1024]{3,2,1,0:T(8,128)S(1)} %copy-done, s32[1024]{0:T(1024)S(1)} %pad_clamp_fusion), kind=kCustom, calls=%fused_computation | custom fusion | bytes 6291584 | tf_op jit(solution)/shard_map/jit(_take)/gather | solution.py:290
  4.3 7.3 %all-to-all-start = ((f32[32,3,8,1024]{3,2,1,0:T(8,128)}), f32[32,3,8,1024]{3,2,1,0:T(8,128)}, u32[]{:S(2)}, u32[]{:S(2)}) async-start(f32[32,3,8,1024]{3,2,1,0:T(8,128)} %gather_fusion), calls=%async_computation | async-start | bytes 6291456 | tf_op jit(solution)/shard_map/all_to_all | solution.py:291
  11.6 0.5 add_bitcast_fusion.pos_ref
  12.2 70.3 %all-to-all-done.inc_left.inc_right.refs_0_.refs_1_.refs_2_.refs_3_ = f32[32,3,8,1024]{3,2,1,0:T(8,128)} async-done(((f32[32,3,8,1024]{3,2,1,0:T(8,128)}), f32[32,3,8,1024]{3,2,1,0:T(8,128)}, u32[]{:S(2)}, u32[]{:S(2)}) %all-to-all-start) | async-done | bytes 3145760 | tf_op jit(solution)/shard_map/all_to_all | solution.py:291
  82.4 5.1 %shard_map.37.own = f32[32,3,8,128]{3,2,1,0:T(8,128)} custom-call(s32[32]{0:T(128)} %add_bitcast_fusion.pos_ref, f32[32,3,8,1024]{3,2,1,0:T(8,128)} %all-to-all-done.inc_left.inc_right.refs_0_.refs_1_.refs_2_.refs_3_, f32[32,3,8,1024]{3,2,1,0:T(8,128)} %all-to-all-done.inc_left.inc_right.refs_0_.refs_1_.refs_2_.refs_3_, f32[32,3,8,1024]{3,2,1,0:T(8,128)} %refs_4_.1, ...), custom_call_target="tpu_custom_call" | custom-call | tf_op jit(solution)/shard_map/pallas_call | solution.py:198
  87.6 0.0 collective-permute-start.1
  87.6 0.5 collective-permute-start
  88.1 12.1 %shard_map.38.body = f32[32,3,8,1024]{3,2,1,0:T(8,128)} custom-call(s32[32]{0:T(128)} %add_bitcast_fusion.pos_ref, f32[32,3,8,1024]{3,2,1,0:T(8,128)} %all-to-all-done.inc_left.inc_right.refs_0_.refs_1_.refs_2_.refs_3_, f32[32,3,8,1024]{3,2,1,0:T(8,128)} %all-to-all-done.inc_left.inc_right.refs_0_.refs_1_.refs_2_.refs_3_, ...), custom_call_target="tpu_custom_call" | custom-call | tf_op jit(solution)/shard_map/pallas_call | solution.py:161
  100.2 0.0 collective-permute-done.1.from_right
  100.2 0.0 copy-start.1
  100.2 0.0 collective-permute-done.from_left
  100.2 0.7 copy-done.1
  100.9 4.2 %shard_map.39 = f32[32,3,8,1024]{3,2,1,0:T(8,128)} custom-call(f32[32,3,8,128]{3,2,1,0:T(8,128)} %shard_map.37.own, f32[32,3,8,128]{3,2,1,0:T(8,128)} %collective-permute-done.from_left, f32[32,3,8,128]{3,2,1,0:T(8,128)} %copy-done.1, f32[32,3,8,1024]{3,2,1,0:T(8,128)} %shard_map.38.body), custom_call_target="tpu_custom_call", output_to_operand_aliasing={{}: (3, {})} | custom-call | tf_op jit(solution)/shard_map/pallas_call | solution.py:269
  (4 shorter events, 0.0 us)
Async XLA Ops:
  0.0 1.9 %copy-start = (f32[32,3,8,1024]{3,2,1,0:T(8,128)S(1)}, f32[32,3,8,1024]{3,2,1,0:T(8,128)}, u32[]{:S(2)}) copy-start(f32[32,3,8,1024]{3,2,1,0:T(8,128)} %param.3) | copy-start | bytes 9437188
  4.3 78.1 %all-to-all-start = ((f32[32,3,8,1024]{3,2,1,0:T(8,128)}), f32[32,3,8,1024]{3,2,1,0:T(8,128)}, u32[]{:S(2)}, u32[]{:S(2)}) async-start(f32[32,3,8,1024]{3,2,1,0:T(8,128)} %gather_fusion), calls=%async_computation | async-start | bytes 6291456 | tf_op jit(solution)/shard_map/all_to_all | solution.py:291
  87.6 12.6 %collective-permute-start.1 = (f32[32,3,8,128]{3,2,1,0:T(8,128)}, f32[32,3,8,128]{3,2,1,0:T(8,128)S(1)}, u32[]{:S(2)}, u32[]{:S(2)}) collective-permute-start(f32[32,3,8,128]{3,2,1,0:T(8,128)} %shard_map.37.own), channel_id=1, source_target_pairs={{0,3},{1,0},{2,1},{3,2},{4,7},{5,4},{6,5},{7,6},{8,11},{9,8},{10,9... | collective-permute-start | bytes 1179656 | tf_op jit(solution)/shard_map/ppermute | solution.py:295
  87.6 12.6 %collective-permute-start = (f32[32,3,8,128]{3,2,1,0:T(8,128)}, f32[32,3,8,128]{3,2,1,0:T(8,128)}, u32[]{:S(2)}, u32[]{:S(2)}) collective-permute-start(f32[32,3,8,128]{3,2,1,0:T(8,128)} %shard_map.37.own), channel_id=1, source_target_pairs={{0,1},{1,2},{2,3},{3,0},{4,5},{5,6},{6,7},{7,4},{8,9},{9,10},{10,1... | collective-permute-start | bytes 1179656 | tf_op jit(solution)/shard_map/ppermute | solution.py:294
  100.2 0.7 copy-start.1

commit v14 on v12

--- a/solution.py
+++ b/solution.py
@@ -7,7 +7,7 @@
 
 STEPS = 4
 LANES = 128
-PAIR = 4
+PAIR = 8
 EDGE_GROUP = 8
 GATHER_GROUP = 32
 
@@ -52,20 +52,20 @@
     e_yp, e_ym = yp(e), ym(e)
     u_yp, u_ym = yp(u), ym(u)
     v_yp, v_ym = yp(v), ym(v)
-    hu_xp = (1.0 + e_xp) * u_xp
-    hu_xm = (1.0 + e_xm) * u_xm
-    hv_yp = (1.0 + e_yp) * v_yp
-    hv_ym = (1.0 + e_ym) * v_ym
+    dx_u = u_xp - u_xm
+    dy_v = v_yp - v_ym
+    dx_hu = dx_u + (e_xp * u_xp - e_xm * u_xm)
+    dy_hv = dy_v + (e_yp * v_yp - e_ym * v_ym)
     half_step = 0.5 * time_step
-    new_e = 0.25 * (e_xp + e_xm + e_yp + e_ym) - half_step * ((hu_xp - hu_xm) + (hv_yp - hv_ym))
+    new_e = 0.25 * (e_xp + e_xm + e_yp + e_ym) - half_step * (dx_hu + dy_hv)
     new_u = (
         0.25 * (u_xp + u_xm + u_yp + u_ym)
-        - half_step * (u * (u_xp - u_xm) + v * (u_yp - u_ym) + gravity * (e_xp - e_xm))
+        - half_step * (u * dx_u + v * (u_yp - u_ym) + gravity * (e_xp - e_xm))
         + (time_step * coriolis) * v
     )
     new_v = (
         0.25 * (v_xp + v_xm + v_yp + v_ym)
-        - half_step * (u * (v_xp - v_xm) + v * (v_yp - v_ym) + gravity * (e_yp - e_ym))
+        - half_step * (u * (v_xp - v_xm) + v * dy_v + gravity * (e_yp - e_ym))
         - (time_step * coriolis) * u
     )
     return new_e, new_u, new_v

time: 104 us -> 104 us (level)
  transfers between devices with their start and end apart: 3 -> 3, of which waited for: 1 -> 1; matrix products, arithmetic and copies ran while one was open for 1% -> 1% of each run, Pallas kernels for 12% -> 11%
where the time goes in v14:
time: 104 us; the launch traced here: 103 us
  waiting for transfers between devices  70.3 us (68%)
  Pallas kernels  19.1 us (18%)
  starting transfers between devices  7.83 us (8%)
  local copies, waits for them, and re-layouts  4.21 us (4%)
  other arithmetic  1.36 us (1%)
    all_to_all x1, waiting for transfers between devices, shards(): lax.all_to_all(outgoing, 'ens', split_axis=0, concat_axis=0, tiled=True)  70.3 us
    pallas_call x1, Pallas kernels, main_forecast(): pl.pallas_call(main_kernel, grid_spec=grid_spec, out_shape=jax.ShapeDtype...  11.8 us
    all_to_all x1, starting transfers between devices, shards(): lax.all_to_all(outgoing, 'ens', split_axis=0, concat_axis=0, tiled=True)  7.28 us
    pallas_call x1, Pallas kernels, edge_fix(): pl.pallas_call(edge_kernel, in_specs=[whole, whole, whole, raw], out_spec...  4.18 us
    pallas_call x1, Pallas kernels, edge_blocks(): pl.pallas_call(edges_kernel, grid_spec=grid_spec, out_shape=jax.ShapeDtyp...  3.13 us
    gather x1, local copies, waits for them, and re-layouts, shards(): outgoing = jnp.take(state, send_index, axis=0, mode='clip')  2.41 us
  transfers between devices with their start and end apart: 3, of which 1 were waited for; matrix products, arithmetic and copies ran while one was open for 1% of the time, Pallas kernels for 11%

profile of v14, /device:TPU:0, one launch (start us, length us, event | category | flops | bytes accessed | tf_op | source)
XLA Modules:
  0.0 102.8 jit_solution(10833926742297773850)
XLA Ops:
  0.0 0.0 copy-start
  0.0 0.9 reshape.117
  0.9 0.3 and_reduce_fusion
  1.3 0.3 convert_reduce_fusion
  1.6 0.2 select_reduce_fusion
  1.7 0.1 copy.5
  1.8 0.1 reshape.120
  1.9 0.0 copy-done
  1.9 2.4 %gather_fusion = f32[32,3,8,1024]{3,2,1,0:T(8,128)} fusion(f32[32,3,8,1024]{3,2,1,0:T(8,128)S(1)} %copy-done, s32[1024]{0:T(1024)S(1)} %pad_clamp_fusion), kind=kCustom, calls=%fused_computation | custom fusion | bytes 6291584 | tf_op jit(solution)/shard_map/jit(_take)/gather | solution.py:293
  4.3 7.3 %all-to-all-start = ((f32[32,3,8,1024]{3,2,1,0:T(8,128)}), f32[32,3,8,1024]{3,2,1,0:T(8,128)}, u32[]{:S(2)}, u32[]{:S(2)}) async-start(f32[32,3,8,1024]{3,2,1,0:T(8,128)} %gather_fusion), calls=%async_computation | async-start | bytes 6291456 | tf_op jit(solution)/shard_map/all_to_all | solution.py:294
  11.6 0.5 add_bitcast_fusion.pos_ref
  12.2 70.3 %all-to-all-done.refs_0_.refs_1_.refs_2_.refs_3_.refs_4_.refs_5_.refs_6_.refs_7_.refs_8_.refs_9_.refs_10_.refs_11_.refs_12_.refs_13_.refs_14_.refs_15_.refs_16_.refs_17_.refs_18_.refs_19_.refs_20_.refs_21_.refs_22_.refs_23_.refs_24_.refs_25_.refs_26_.refs_27_.refs_28_.refs_29_.refs_30_.refs_31_.refs_32_.refs_33_.refs_34_.refs_35_.refs_36_.refs_37_.refs_38_.refs_39_.refs_40_.refs_41_.refs_42_.refs_43_.refs_44_.refs_45_.refs_46_.refs_47_.refs_48_.refs_49_.refs_50_.refs_51_.refs_52_.refs_53_.refs_54_.refs_55_.refs_56_.refs_57_.refs_58_.refs_59_.refs_60_.refs_61_.refs_62_.refs_63_ = f32[32,3,8,1024]{3,2,1,0:T(8,128)} async-done(((f32[32,3,8,1024]{3,2,1,0:T(8,128)}), ...) | async-done | bytes 3145760 | tf_op jit(solution)/shard_map/all_to_all | solution.py:294
  82.4 3.1 %shard_map.37.own = f32[32,3,8,128]{3,2,1,0:T(8,128)} custom-call(s32[32]{0:T(128)} %add_bitcast_fusion.pos_ref, ...), custom_call_target="tpu_custom_call" | custom-call | tf_op jit(solution)/shard_map/pallas_call | solution.py:201
  85.6 0.1 collective-permute-start.1
  85.6 0.5 collective-permute-start
  86.1 11.8 %shard_map.38.body = f32[32,3,8,1024]{3,2,1,0:T(8,128)} custom-call(s32[32]{0:T(128)} %add_bitcast_fusion.pos_ref, ...), custom_call_target="tpu_custom_call" | custom-call | tf_op jit(solution)/shard_map/pallas_call | solution.py:161
  97.9 0.0 collective-permute-done.1.from_right
  97.9 0.0 copy-start.1
  97.9 0.0 collective-permute-done.from_left
  97.9 0.7 copy-done.1
  98.6 4.2 %shard_map.39 = f32[32,3,8,1024]{3,2,1,0:T(8,128)} custom-call(f32[32,3,8,128]{3,2,1,0:T(8,128)} %shard_map.37.own, f32[32,3,8,128]{3,2,1,0:T(8,128)} %collective-permute-done.from_left, f32[32,3,8,128]{3,2,1,0:T(8,128)} %copy-done.1, f32[32,3,8,1024]{3,2,1,0:T(8,128)} %shard_map.38.body), custom_call_target="tpu_custom_call", output_to_operand_aliasing={{}: (3, {})} | custom-call | tf_op jit(solution)/shard_map/pallas_call | solution.py:272
  (4 shorter events, 0.0 us)
Async XLA Ops:
  0.0 1.9 %copy-start = (f32[32,3,8,1024]{3,2,1,0:T(8,128)S(1)}, f32[32,3,8,1024]{3,2,1,0:T(8,128)}, u32[]{:S(2)}) copy-start(f32[32,3,8,1024]{3,2,1,0:T(8,128)} %param.3) | copy-start | bytes 9437188
  4.3 78.1 %all-to-all-start = ((f32[32,3,8,1024]{3,2,1,0:T(8,128)}), f32[32,3,8,1024]{3,2,1,0:T(8,128)}, u32[]{:S(2)}, u32[]{:S(2)}) async-start(f32[32,3,8,1024]{3,2,1,0:T(8,128)} %gather_fusion), calls=%async_computation | async-start | bytes 6291456 | tf_op jit(solution)/shard_map/all_to_all | solution.py:294
  85.6 12.3 %collective-permute-start.1 = (f32[32,3,8,128]{3,2,1,0:T(8,128)}, f32[32,3,8,128]{3,2,1,0:T(8,128)S(1)}, u32[]{:S(2)}, u32[]{:S(2)}) collective-permute-start(f32[32,3,8,128]{3,2,1,0:T(8,128)} %shard_map.37.own), channel_id=1, source_target_pairs={{0,3},{1,0},{2,1},{3,2},{4,7},{5,4},{6,5},{7,6},{8,11},{9,8},{10,9... | collective-permute-start | bytes 1179656 | tf_op jit(solution)/shard_map/ppermute | solution.py:298
  85.6 12.3 %collective-permute-start = (f32[32,3,8,128]{3,2,1,0:T(8,128)}, f32[32,3,8,128]{3,2,1,0:T(8,128)}, u32[]{:S(2)}, u32[]{:S(2)}) collective-permute-start(f32[32,3,8,128]{3,2,1,0:T(8,128)} %shard_map.37.own), channel_id=1, source_target_pairs={{0,1},{1,2},{2,3},{3,0},{4,5},{5,6},{6,7},{7,4},{8,9},{9,10},{10,1... | collective-permute-start | bytes 1179656 | tf_op jit(solution)/shard_map/ppermute | solution.py:297
  97.9 0.7 copy-start.1

commit v15 on v14

--- a/solution.py
+++ b/solution.py
@@ -17,24 +17,23 @@
 
 
 def routing(parents, count, per_dev, dist, me):
-    blocks = parents.reshape(count, per_dev)
-    owner = blocks // per_dev
-    local = blocks % per_dev
-    ids = jnp.arange(per_dev, dtype=jnp.int32)
-    same = blocks[:, :, None] == blocks[:, None, :]
+    total = count * per_dev
+    ids = jnp.arange(total, dtype=jnp.int32)
+    block = ids // per_dev
+    owner = parents // per_dev
+    local = parents % per_dev
+    same_block = block[:, None] == block[None, :]
     earlier = ids[None, :] < ids[:, None]
-    first = jnp.logical_not(jnp.any(same & earlier[None], axis=2))
-    below = (
-        (owner[:, :, None] == owner[:, None, :])
-        & (blocks[:, None, :] < blocks[:, :, None])
-        & first[:, None, :]
-    )
-    slot = jnp.sum(below.astype(jnp.int32), axis=2)
-    slots = jnp.arange(dist, dtype=jnp.int32)
-    pick = (owner == me)[:, None, :] & first[:, None, :] & (slot[:, None, :] == slots[None, :, None])
-    send_index = jnp.sum(pick.astype(jnp.int32) * local[:, None, :], axis=2).reshape(-1)
-    my_owner = lax.dynamic_index_in_dim(owner, me, 0, keepdims=False)
-    my_slot = lax.dynamic_index_in_dim(slot, me, 0, keepdims=False)
+    same = parents[:, None] == parents[None, :]
+    first = jnp.logical_not(jnp.any(same_block & earlier & same, axis=1))
+    below = same_block & (owner[:, None] == owner[None, :]) & (parents[None, :] < parents[:, None]) & first[None, :]
+    slot = jnp.sum(below.astype(jnp.int32), axis=1)
+    sending = (owner == me) & first
+    key = jnp.where(sending, block * dist + slot, -1)
+    targets = jnp.arange(count * dist, dtype=jnp.int32)
+    send_index = jnp.sum(jnp.where(key[None, :] == targets[:, None], local[None, :], 0), axis=1)
+    my_owner = lax.dynamic_slice_in_dim(owner, me * per_dev, per_dev)
+    my_slot = lax.dynamic_slice_in_dim(slot, me * per_dev, per_dev)
     return send_index, my_owner * dist + my_slot
 
 
@@ -205,14 +204,22 @@
     )(position, *([incoming] * (2 * group)), noise, noise)
 
 
-def edge_kernel(own, from_left, from_right, body, out, patch, first_buf, last_buf, sems):
+def edge_kernel(own_hbm, left_hbm, right_hbm, body, out, patch, first_buf, last_buf, own, from_left, from_right, sems):
     rows = own.shape[-2]
     cols = body.shape[-1]
     lane = lax.broadcasted_iota(jnp.int32, (rows, LANES), 1)
+    staged = [
+        pltpu.make_async_copy(src, dst, sems.at[2 + n])
+        for n, (src, dst) in enumerate(((own_hbm, own), (left_hbm, from_left), (right_hbm, from_right)))
+    ]
+    for copy in staged:
+        copy.start()
     first_in = pltpu.make_async_copy(body.at[:, :, :, pl.ds(0, LANES)], first_buf, sems.at[0])
     last_in = pltpu.make_async_copy(body.at[:, :, :, pl.ds(cols - LANES, LANES)], last_buf, sems.at[1])
     first_in.start()
     last_in.start()
+    for copy in staged:
+        copy.wait()
 
     slot = 16
     per_vreg = LANES // (2 * slot)
@@ -267,18 +274,20 @@
 
 
 def edge_fix(own, from_left, from_right, body):
-    whole = pl.BlockSpec(memory_space=pltpu.VMEM)
     raw = pl.BlockSpec(memory_space=pl.ANY)
     return pl.pallas_call(
         edge_kernel,
-        in_specs=[whole, whole, whole, raw],
+        in_specs=[raw, raw, raw, raw],
         out_specs=raw,
         out_shape=jax.ShapeDtypeStruct(body.shape, body.dtype),
         scratch_shapes=[
             pltpu.VMEM((own.shape[0] // 4,) + own.shape[1:], jnp.float32),
             pltpu.VMEM(own.shape, jnp.float32),
             pltpu.VMEM(own.shape, jnp.float32),
-            pltpu.SemaphoreType.DMA((2,)),
+            pltpu.VMEM(own.shape, jnp.float32),
+            pltpu.VMEM(own.shape, jnp.float32),
+            pltpu.VMEM(own.shape, jnp.float32),
+            pltpu.SemaphoreType.DMA((5,)),
         ],
         input_output_aliases={3: 0},
     )(own, from_left, from_right, body)

time: 104 us -> 105 us (level)
  other arithmetic: 1.36 us -> 3.62 us
  local copies, waits for them, and re-layouts: 4.21 us -> 3.14 us
where the time goes in v15:
time: 105 us; the launch traced here: 104 us
  waiting for transfers between devices  70.2 us (67%)
  Pallas kernels  19.1 us (18%)
  starting transfers between devices  7.83 us (7%)
  other arithmetic  3.62 us (3%)
  local copies, waits for them, and re-layouts  3.14 us (3%)
    all_to_all x1, waiting for transfers between devices, shards(): lax.all_to_all(outgoing, 'ens', split_axis=0, concat_axis=0, tiled=True)  70.2 us
    pallas_call x1, Pallas kernels, main_forecast(): pl.pallas_call(main_kernel, grid_spec=grid_spec, out_shape=jax.ShapeDtype...  11.8 us
    all_to_all x1, starting transfers between devices, shards(): lax.all_to_all(outgoing, 'ens', split_axis=0, concat_axis=0, tiled=True)  7.28 us
    pallas_call x1, Pallas kernels, edge_fix(): pl.pallas_call(edge_kernel, in_specs=[raw, raw, raw, raw], out_specs=raw,...  4.21 us
    pallas_call x1, Pallas kernels, edge_blocks(): pl.pallas_call(edges_kernel, grid_spec=grid_spec, out_shape=jax.ShapeDtyp...  3.13 us
    gather x1, local copies, waits for them, and re-layouts, shards(): outgoing = jnp.take(state, send_index, axis=0, mode='clip')  2.41 us
  transfers between devices with their start and end apart: 3, of which 1 were waited for; matrix products, arithmetic and copies ran while one was open for 1% of the time, Pallas kernels for 11%

profile of v15, /device:TPU:0, one launch (start us, length us, event | category | flops | bytes accessed | tf_op | source)
XLA Modules:
  0.0 104.0 jit_solution(14055152113299770323)
XLA Ops:
  0.0 0.0 copy-start
  0.0 0.8 and_select_fusion
  0.8 1.0 fusion.3
  1.9 1.0 convert_reduce_fusion
  2.9 0.1 select_reduce_fusion
  3.0 0.0 copy-done
  3.0 2.4 %gather_fusion = f32[32,3,8,1024]{3,2,1,0:T(8,128)} fusion(f32[32,3,8,1024]{3,2,1,0:T(8,128)S(1)} %copy-done, s32[1024]{0:T(1024)S(1)} %pad_clamp_fusion), kind=kCustom, calls=%fused_computation | custom fusion | bytes 6291584 | tf_op jit(solution)/shard_map/jit(_take)/gather | solution.py:302
  5.5 7.3 %all-to-all-start = ((f32[32,3,8,1024]{3,2,1,0:T(8,128)}), f32[32,3,8,1024]{3,2,1,0:T(8,128)}, u32[]{:S(2)}, u32[]{:S(2)}) async-start(f32[32,3,8,1024]{3,2,1,0:T(8,128)} %gather_fusion), calls=%async_computation | async-start | bytes 6291456 | tf_op jit(solution)/shard_map/all_to_all | solution.py:303
  12.7 0.6 dynamic-slice_add_fusion.pos_ref
  13.3 70.2 %all-to-all-done.refs_0_.refs_1_.refs_2_.refs_3_.refs_4_.refs_5_.refs_6_.refs_7_.refs_8_.refs_9_.refs_10_.refs_11_.refs_12_.refs_13_.refs_14_.refs_15_.refs_16_.refs_17_.refs_18_.refs_19_.refs_20_.refs_21_.refs_22_.refs_23_.refs_24_.refs_25_.refs_26_.refs_27_.refs_28_.refs_29_.refs_30_.refs_31_.refs_32_.refs_33_.refs_34_.refs_35_.refs_36_.refs_37_.refs_38_.refs_39_.refs_40_.refs_41_.refs_42_.refs_43_.refs_44_.refs_45_.refs_46_.refs_47_.refs_48_.refs_49_.refs_50_.refs_51_.refs_52_.refs_53_.refs_54_.refs_55_.refs_56_.refs_57_.refs_58_.refs_59_.refs_60_.refs_61_.refs_62_.refs_63_ = f32[32,3,8,1024]{3,2,1,0:T(8,128)} async-done(((f32[32,3,8,1024]{3,2,1,0:T(8,128)}), ...) | async-done | bytes 3145760 | tf_op jit(solution)/shard_map/all_to_all | solution.py:303
  83.6 3.1 %shard_map.37.own_hbm = f32[32,3,8,128]{3,2,1,0:T(8,128)} custom-call(s32[32]{0:T(128)} %dynamic-slice_add_fusion.pos_ref, ...), custom_call_target="tpu_custom_call" | custom-call | tf_op jit(solution)/shard_map/pallas_call | solution.py:200
  86.7 0.1 collective-permute-start.1
  86.8 0.5 collective-permute-start
  87.3 11.8 %shard_map.38.body = f32[32,3,8,1024]{3,2,1,0:T(8,128)} custom-call(s32[32]{0:T(128)} %dynamic-slice_add_fusion.pos_ref, ...), custom_call_target="tpu_custom_call" | custom-call | tf_op jit(solution)/shard_map/pallas_call | solution.py:160
  99.0 0.0 collective-permute-done.1.right_hbm
  99.0 0.0 copy-start.1
  99.0 0.0 collective-permute-done.left_hbm
  99.0 0.7 copy-done.1
  99.7 4.2 %shard_map.39 = f32[32,3,8,1024]{3,2,1,0:T(8,128)} custom-call(f32[32,3,8,128]{3,2,1,0:T(8,128)} %shard_map.37.own_hbm, f32[32,3,8,128]{3,2,1,0:T(8,128)} %collective-permute-done.left_hbm, f32[32,3,8,128]{3,2,1,0:T(8,128)} %copy-done.1, f32[32,3,8,1024]{3,2,1,0:T(8,128)} %shard_map.38.body), custom_call_target="tpu_custom_call", output_to_operand_aliasing={{}: (3, {})} | custom-call | tf_op jit(solution)/shard_map/pallas_call | solution.py:278
  (3 shorter events, 0.0 us)
Async XLA Ops:
  0.0 3.0 %copy-start = (f32[32,3,8,1024]{3,2,1,0:T(8,128)S(1)}, f32[32,3,8,1024]{3,2,1,0:T(8,128)}, u32[]{:S(2)}) copy-start(f32[32,3,8,1024]{3,2,1,0:T(8,128)} %param.3) | copy-start | bytes 9437188
  5.5 78.1 %all-to-all-start = ((f32[32,3,8,1024]{3,2,1,0:T(8,128)}), f32[32,3,8,1024]{3,2,1,0:T(8,128)}, u32[]{:S(2)}, u32[]{:S(2)}) async-start(f32[32,3,8,1024]{3,2,1,0:T(8,128)} %gather_fusion), calls=%async_computation | async-start | bytes 6291456 | tf_op jit(solution)/shard_map/all_to_all | solution.py:303
  86.7 12.3 %collective-permute-start.1 = (f32[32,3,8,128]{3,2,1,0:T(8,128)}, f32[32,3,8,128]{3,2,1,0:T(8,128)S(1)}, u32[]{:S(2)}, u32[]{:S(2)}) collective-permute-start(f32[32,3,8,128]{3,2,1,0:T(8,128)} %shard_map.37.own_hbm), channel_id=1, source_target_pairs={{0,3},{1,0},{2,1},{3,2},{4,7},{5,4},{6,5},{7,6},{8,11},{9,8},{10,9... | collective-permute-start | bytes 1179656 | tf_op jit(solution)/shard_map/ppermute | solution.py:307
  86.8 12.3 %collective-permute-start = (f32[32,3,8,128]{3,2,1,0:T(8,128)}, f32[32,3,8,128]{3,2,1,0:T(8,128)}, u32[]{:S(2)}, u32[]{:S(2)}) collective-permute-start(f32[32,3,8,128]{3,2,1,0:T(8,128)} %shard_map.37.own_hbm), channel_id=1, source_target_pairs={{0,1},{1,2},{2,3},{3,0},{4,5},{5,6},{6,7},{7,4},{8,9},{9,10},{10,1... | collective-permute-start | bytes 1179656 | tf_op jit(solution)/shard_map/ppermute | solution.py:306
  99.0 0.7 copy-start.1

commit v16 on v14

--- a/solution.py
+++ b/solution.py
@@ -290,8 +290,16 @@
     per_dev = state.shape[0]
     dist = max(1, -(-per_dev // count))
     send_index, position = routing(parents, count, per_dev, dist, me)
-    outgoing = jnp.take(state, send_index, axis=0, mode="clip")
-    incoming = lax.all_to_all(outgoing, "ens", split_axis=0, concat_axis=0, tiled=True)
+    shifts = jnp.arange(count * dist, dtype=jnp.int32)
+    by_shift = ((shifts // dist + me) % count) * dist + shifts % dist
+    outgoing = jnp.take(state, jnp.take(send_index, by_shift), axis=0, mode="clip")
+    chunks = [outgoing[:dist]]
+    for k in range(1, count):
+        pairs = [(i, (i + k) % count) for i in range(count)]
+        chunks.append(lax.ppermute(outgoing[k * dist:(k + 1) * dist], "ens", pairs))
+    incoming = jnp.concatenate(chunks, axis=0)
+    owner = position // dist
+    position = ((me - owner) % count) * dist + position % dist
     own = edge_blocks(position, incoming, noise)
     ring = lax.axis_size("col")
     from_left = lax.ppermute(own, "col", [(i, (i + 1) % ring) for i in range(ring)])

time: 104 us -> 106 us (1.019)
  the two profiles are of different devices: /device:TPU:0 before, /device:TPU:29 now
where the time goes in v16:
time: 106 us; the launch traced here: 105 us
  waiting for transfers between devices  58 us (55%)
  Pallas kernels  19.1 us (18%)
  local copies, waits for them, and re-layouts  18.8 us (18%)
  starting transfers between devices  7.94 us (7%)
  other arithmetic  1.47 us (1%)
    ppermute x7, waiting for transfers between devices, shards(): chunks.append(lax.ppermute(outgoing[k * dist:(k + 1) * dist], 'ens', pairs))  58 us
    pallas_call x1, Pallas kernels, main_forecast(): pl.pallas_call(main_kernel, grid_spec=grid_spec, out_shape=jax.ShapeDtype...  11.8 us
    unnamed x10, local copies, waits for them, and re-layouts  9.44 us
    ppermute x7, starting transfers between devices, shards(): chunks.append(lax.ppermute(outgoing[k * dist:(k + 1) * dist], 'ens', pairs))  5.18 us
    pallas_call x1, Pallas kernels, edge_fix(): pl.pallas_call(edge_kernel, in_specs=[whole, whole, whole, raw], out_spec...  4.18 us
    slice x1, local copies, waits for them, and re-layouts, shards(): chunks.append(lax.ppermute(outgoing[k * dist:(k + 1) * dist], 'ens', pairs))  3.39 us
    pallas_call x1, Pallas kernels, edge_blocks(): pl.pallas_call(edges_kernel, grid_spec=grid_spec, out_shape=jax.ShapeDtyp...  3.13 us
    gather x1, local copies, waits for them, and re-layouts, shards(): jnp.take(state, jnp.take(send_index, by_shift), axis=0, mode='clip')  2.41 us
  transfers between devices with their start and end apart: 9, of which 4 were waited for; matrix products, arithmetic and copies ran while one was open for 9% of the time, Pallas kernels for 11%

profile of v16, /device:TPU:29, one launch (start us, length us, event | category | flops | bytes accessed | tf_op | source)
XLA Modules:
  0.0 105.4 jit_solution(5484022740577670437)
XLA Ops:
  0.1 0.9 reshape.240
  2.7 2.4 %gather_fusion.1 = f32[32,3,8,1024]{3,2,1,0:T(8,128)} fusion(f32[32,3,8,1024]{3,2,1,0:T(8,128)S(1)} %copy-done, s32[1024]{0:T(1024)S(1)} %pad_clamp_fusion), kind=kCustom, calls=%fused_computation.1 | custom fusion | bytes 6291584 | tf_op jit(solution)/shard_map/jit(_take)/gather | solution.py:295
  5.1 3.4 %fusion.12 = (f32[4,3,8,1024]{3,2,1,0:T(8,128)S(1)}, f32[4,3,8,1024]{3,2,1,0:T(8,128)}, f32[4,3,8,1024]{3,2,1,0:T(8,128)}, f32[4,3,8,1024]{3,2,1,0:T(8,128)}, f3...) fusion(f32[32,3,8,1024]{3,2,1,0:T(8,128)} %gather_fusion.1), kind=kLoop, calls=%fused_computation.55 | loop fusion | bytes 6291456 | tf_op jit(solution)/shard_map/slice | solution.py:299
  8.5 1.2 %collective-permute-start.1 = (f32[4,3,8,1024]{3,2,1,0:T(8,128)}, f32[4,3,8,1024]{3,2,1,0:T(8,128)}, u32[]{:S(2)}, u32[]{:S(2)}) collective-permute-start(f32[4,3,8,1024]{3,2,1,0:T(8,128)} %get-tuple-element.12), channel_id=1, source_target_pairs={{0,8},{4,12},{8,16},{12,20},{16,24},{20,28},{24,0},{28,4},{1,9},{5... | collective-permute-start | bytes 1179656 | tf_op jit(solution)/shard_map/ppermute | solution.py:299
  9.7 1.4 %collective-permute-start.2 = (f32[4,3,8,1024]{3,2,1,0:T(8,128)}, f32[4,3,8,1024]{3,2,1,0:T(8,128)}, u32[]{:S(2)}, u32[]{:S(2)}) collective-permute-start(f32[4,3,8,1024]{3,2,1,0:T(8,128)} %get-tuple-element.11), channel_id=1, source_target_pairs={{0,12},{4,16},{8,20},{12,24},{16,28},{20,0},{24,4},{28,8},{1,13},{... | collective-permute-start | bytes 1179656 | tf_op jit(solution)/shard_map/ppermute | solution.py:299
  11.0 1.1 %collective-permute-start.6 = (f32[4,3,8,1024]{3,2,1,0:T(8,128)S(1)}, f32[4,3,8,1024]{3,2,1,0:T(8,128)}, u32[]{:S(2)}, u32[]{:S(2)}) collective-permute-start(f32[4,3,8,1024]{3,2,1,0:T(8,128)S(1)} %get-tuple-element.7), channel_id=1, source_target_pairs={{0,28},{4,0},{8,4},{12,8},{16,12},{20,16},{24,20},{28,24},{1,29},{... | collective-permute-start | bytes 1179656 | tf_op jit(solution)/shard_map/ppermute | solution.py:299
  13.0 5.8 %collective-permute-done = f32[4,3,8,1024]{3,2,1,0:T(8,128)} collective-permute-done((f32[4,3,8,1024]{3,2,1,0:T(8,128)}, f32[4,3,8,1024]{3,2,1,0:T(8,128)}, u32[]{:S(2)}, u32[]{:S(2)}) %collective-permute-start) | collective-permute-done | bytes 393248 | tf_op jit(solution)/shard_map/ppermute | solution.py:299
  18.8 1.1 %collective-permute-start.4 = (f32[4,3,8,1024]{3,2,1,0:T(8,128)}, f32[4,3,8,1024]{3,2,1,0:T(8,128)S(1)}, u32[]{:S(2)}, u32[]{:S(2)}) collective-permute-start(f32[4,3,8,1024]{3,2,1,0:T(8,128)} %get-tuple-element.9), channel_id=1, source_target_pairs={{0,20},{4,24},{8,28},{12,0},{16,4},{20,8},{24,12},{28,16},{1,21},{... | collective-permute-start | bytes 1179656 | tf_op jit(solution)/shard_map/ppermute | solution.py:299
  19.9 1.8 %constant_dynamic-update-slice_fusion.6 = f32[32,3,8,1024]{3,2,1,0:T(8,128)} fusion(f32[32,3,8,1024]{3,2,1,0:T(8,128)} %get-tuple-element.14, f32[4,3,8,1024]{3,2,1,0:T(8,128)} %collective-permute-done), kind=kLoop, calls=%fused_computation.11 | loop fusion | bytes 786432
  21.6 5.6 %collective-permute-done.1 = f32[4,3,8,1024]{3,2,1,0:T(8,128)} collective-permute-done((f32[4,3,8,1024]{3,2,1,0:T(8,128)}, f32[4,3,8,1024]{3,2,1,0:T(8,128)}, u32[]{:S(2)}, u32[]{:S(2)}) %collective-permute-start.1) | collective-permute-done | bytes 393248 | tf_op jit(solution)/shard_map/ppermute | solution.py:299
  27.5 1.8 %constant_dynamic-update-slice_fusion.5 = f32[32,3,8,1024]{3,2,1,0:T(8,128)} fusion(f32[32,3,8,1024]{3,2,1,0:T(8,128)} %constant_dynamic-update-slice_fusion.6, f32[4,3,8,1024]{3,2,1,0:T(8,128)} %collective-permute-done.1), kind=kLoop, calls=%fused_computation.10 | loop fusion | bytes 786432
  29.3 4.6 %collective-permute-done.2 = f32[4,3,8,1024]{3,2,1,0:T(8,128)} collective-permute-done((f32[4,3,8,1024]{3,2,1,0:T(8,128)}, f32[4,3,8,1024]{3,2,1,0:T(8,128)}, u32[]{:S(2)}, u32[]{:S(2)}) %collective-permute-start.2) | collective-permute-done | bytes 393248 | tf_op jit(solution)/shard_map/ppermute | solution.py:299
  33.9 1.8 %constant_dynamic-update-slice_fusion.4 = f32[32,3,8,1024]{3,2,1,0:T(8,128)} fusion(f32[32,3,8,1024]{3,2,1,0:T(8,128)} %constant_dynamic-update-slice_fusion.5, f32[4,3,8,1024]{3,2,1,0:T(8,128)} %collective-permute-done.2), kind=kLoop, calls=%fused_computation.9 | loop fusion | bytes 786432
  35.7 42.0 %collective-permute-done.3 = f32[4,3,8,1024]{3,2,1,0:T(8,128)} collective-permute-done((f32[4,3,8,1024]{3,2,1,0:T(8,128)}, f32[4,3,8,1024]{3,2,1,0:T(8,128)}, u32[]{:S(2)}, u32[]{:S(2)}) %collective-permute-start.3) | collective-permute-done | bytes 393248 | tf_op jit(solution)/shard_map/ppermute | solution.py:299
  77.7 1.8 %constant_dynamic-update-slice_fusion.3 = f32[32,3,8,1024]{3,2,1,0:T(8,128)} fusion(f32[32,3,8,1024]{3,2,1,0:T(8,128)} %constant_dynamic-update-slice_fusion.4, f32[4,3,8,1024]{3,2,1,0:T(8,128)} %collective-permute-done.3), kind=kLoop, calls=%fused_computation.8 | loop fusion | bytes 786432
  79.4 0.8 constant_dynamic-update-slice_fusion.2
  80.3 0.8 constant_dynamic-update-slice_fusion.1
  81.0 1.8 %constant_dynamic-update-slice_fusion.refs_0_.refs_1_.refs_2_.refs_3_.refs_4_.refs_5_.refs_6_.refs_7_.refs_8_.refs_9_.refs_10_.refs_11_.refs_12_.refs_13_.refs_14_.refs_15_.refs_16_.refs_17_.refs_18_.refs_19_.refs_20_.refs_21_.refs_22_.refs_23_.refs_24_.refs_25_.refs_26_.refs_27_.refs_28_.refs_29_.refs_30_.refs_31_.refs_32_.refs_33_.refs_34_.refs_35_.refs_36_.refs_37_.refs_38_.refs_39_.refs_40_.refs_41_.refs_42_.refs_43_.refs_44_.refs_45_.refs_46_.refs_47_.refs_48_.refs_49_.refs_50_.refs_51_.refs_52_.refs_53_.refs_54_.refs_55_.refs_56_.refs_57_.refs_58_.refs_59_.refs_60_.refs_61_.refs_62_.refs_63_ = f32[32,3,8,1024]{3,2,1,0:T(8,128)} fusion(f32[32,3,8,1024]{3,2,1,0:T(8,128)} %constant_dynamic-upd, ...), kind=kLoop, calls=%fused_computation.5 | loop fusion | bytes 786432 | tf_op jit(solution)/shard_map/concatenate | solution.py:300
  82.8 3.1 %shard_map.37.own = f32[32,3,8,128]{3,2,1,0:T(8,128)} custom-call(s32[32]{0:T(128)} %fusion.4.pos_ref, ...), custom_call_target="tpu_custom_call" | custom-call | tf_op jit(solution)/shard_map/pallas_call | solution.py:201
  86.0 1.6 %collective-permute-start.8 = (f32[32,3,8,128]{3,2,1,0:T(8,128)}, f32[32,3,8,128]{3,2,1,0:T(8,128)S(1)}, u32[]{:S(2)}, u32[]{:S(2)}) collective-permute-start(f32[32,3,8,128]{3,2,1,0:T(8,128)} %shard_map.37.own), channel_id=1, source_target_pairs={{0,3},{1,0},{2,1},{3,2},{4,7},{5,4},{6,5},{7,6},{8,11},{9,8},{10,9... | collective-permute-start | bytes 1179656 | tf_op jit(solution)/shard_map/ppermute | solution.py:306
  87.6 1.2 %collective-permute-start.7 = (f32[32,3,8,128]{3,2,1,0:T(8,128)}, f32[32,3,8,128]{3,2,1,0:T(8,128)}, u32[]{:S(2)}, u32[]{:S(2)}) collective-permute-start(f32[32,3,8,128]{3,2,1,0:T(8,128)} %shard_map.37.own), channel_id=1, source_target_pairs={{0,1},{1,2},{2,3},{3,0},{4,5},{5,6},{6,7},{7,4},{8,9},{9,10},{10,1... | collective-permute-start | bytes 1179656 | tf_op jit(solution)/shard_map/ppermute | solution.py:305
  88.7 11.8 %shard_map.38.body = f32[32,3,8,1024]{3,2,1,0:T(8,128)} custom-call(s32[32]{0:T(128)} %fusion.4.pos_ref, ...), custom_call_target="tpu_custom_call" | custom-call | tf_op jit(solution)/shard_map/pallas_call | solution.py:161
  100.5 0.7 copy-done.1
  101.2 4.2 %shard_map.39 = f32[32,3,8,1024]{3,2,1,0:T(8,128)} custom-call(f32[32,3,8,128]{3,2,1,0:T(8,128)} %shard_map.37.own, f32[32,3,8,128]{3,2,1,0:T(8,128)} %collective-permute-done.7.from_left, f32[32,3,8,128]{3,2,1,0:T(8,128)} %copy-done.1, f32[32,3,8,1024]{3,2,1,0:T(8,128)} %shard_map.38.body), custom_call_target="tpu_custom_call", output_to_operand_aliasing={{}: (3, {})} | custom-call | tf_op jit(solution)/shard_map/pallas_call | solution.py:272
  (25 shorter events, 2.8 us)
Async XLA Ops:
  0.0 2.7 %copy-start = (f32[32,3,8,1024]{3,2,1,0:T(8,128)S(1)}, f32[32,3,8,1024]{3,2,1,0:T(8,128)}, u32[]{:S(2)}) copy-start(f32[32,3,8,1024]{3,2,1,0:T(8,128)} %param.3) | copy-start | bytes 9437188
  8.5 10.3 %collective-permute-start = (f32[4,3,8,1024]{3,2,1,0:T(8,128)}, f32[4,3,8,1024]{3,2,1,0:T(8,128)}, u32[]{:S(2)}, u32[]{:S(2)}) collective-permute-start(f32[4,3,8,1024]{3,2,1,0:T(8,128)} %get-tuple-element.13), channel_id=1, source_target_pairs={{0,4},{4,8},{8,12},{12,16},{16,20},{20,24},{24,28},{28,0},{1,5},{5... | collective-permute-start | bytes 1179656 | tf_op jit(solution)/shard_map/ppermute | solution.py:299
  8.5 18.7 %collective-permute-start.1 = (f32[4,3,8,1024]{3,2,1,0:T(8,128)}, f32[4,3,8,1024]{3,2,1,0:T(8,128)}, u32[]{:S(2)}, u32[]{:S(2)}) collective-permute-start(f32[4,3,8,1024]{3,2,1,0:T(8,128)} %get-tuple-element.12), channel_id=1, source_target_pairs={{0,8},{4,12},{8,16},{12,20},{16,24},{20,28},{24,0},{28,4},{1,9},{5... | collective-permute-start | bytes 1179656 | tf_op jit(solution)/shard_map/ppermute | solution.py:299
  9.7 24.2 %collective-permute-start.2 = (f32[4,3,8,1024]{3,2,1,0:T(8,128)}, f32[4,3,8,1024]{3,2,1,0:T(8,128)}, u32[]{:S(2)}, u32[]{:S(2)}) collective-permute-start(f32[4,3,8,1024]{3,2,1,0:T(8,128)} %get-tuple-element.11), channel_id=1, source_target_pairs={{0,12},{4,16},{8,20},{12,24},{16,28},{20,0},{24,4},{28,8},{1,13},{... | collective-permute-start | bytes 1179656 | tf_op jit(solution)/shard_map/ppermute | solution.py:299
  11.0 70.0 %collective-permute-start.6 = (f32[4,3,8,1024]{3,2,1,0:T(8,128)S(1)}, f32[4,3,8,1024]{3,2,1,0:T(8,128)}, u32[]{:S(2)}, u32[]{:S(2)}) collective-permute-start(f32[4,3,8,1024]{3,2,1,0:T(8,128)S(1)} %get-tuple-element.7), channel_id=1, source_target_pairs={{0,28},{4,0},{8,4},{12,8},{16,12},{20,16},{24,20},{28,24},{1,29},{... | collective-permute-start | bytes 1179656 | tf_op jit(solution)/shard_map/ppermute | solution.py:299
  12.2 65.5 %collective-permute-start.3 = (f32[4,3,8,1024]{3,2,1,0:T(8,128)}, f32[4,3,8,1024]{3,2,1,0:T(8,128)}, u32[]{:S(2)}, u32[]{:S(2)}) collective-permute-start(f32[4,3,8,1024]{3,2,1,0:T(8,128)} %get-tuple-element.10), channel_id=1, source_target_pairs={{0,16},{4,20},{8,24},{12,28},{16,0},{20,4},{24,8},{28,12},{1,17},{... | collective-permute-start | bytes 1179656 | tf_op jit(solution)/shard_map/ppermute | solution.py:299
  18.8 60.6 %collective-permute-start.4 = (f32[4,3,8,1024]{3,2,1,0:T(8,128)}, f32[4,3,8,1024]{3,2,1,0:T(8,128)S(1)}, u32[]{:S(2)}, u32[]{:S(2)}) collective-permute-start(f32[4,3,8,1024]{3,2,1,0:T(8,128)} %get-tuple-element.9), channel_id=1, source_target_pairs={{0,20},{4,24},{8,28},{12,0},{16,4},{20,8},{24,12},{28,16},{1,21},{... | collective-permute-start | bytes 1179656 | tf_op jit(solution)/shard_map/ppermute | solution.py:299
  27.2 53.0 %collective-permute-start.5 = (f32[4,3,8,1024]{3,2,1,0:T(8,128)}, f32[4,3,8,1024]{3,2,1,0:T(8,128)S(1)}, u32[]{:S(2)}, u32[]{:S(2)}) collective-permute-start(f32[4,3,8,1024]{3,2,1,0:T(8,128)} %get-tuple-element.8), channel_id=1, source_target_pairs={{0,24},{4,28},{8,0},{12,4},{16,8},{20,12},{24,16},{28,20},{1,25},{... | collective-permute-start | bytes 1179656 | tf_op jit(solution)/shard_map/ppermute | solution.py:299
  86.0 14.5 %collective-permute-start.8 = (f32[32,3,8,128]{3,2,1,0:T(8,128)}, f32[32,3,8,128]{3,2,1,0:T(8,128)S(1)}, u32[]{:S(2)}, u32[]{:S(2)}) collective-permute-start(f32[32,3,8,128]{3,2,1,0:T(8,128)} %shard_map.37.own), channel_id=1, source_target_pairs={{0,3},{1,0},{2,1},{3,2},{4,7},{5,4},{6,5},{7,6},{8,11},{9,8},{10,9... | collective-permute-start | bytes 1179656 | tf_op jit(solution)/shard_map/ppermute | solution.py:306
  87.6 12.9 %collective-permute-start.7 = (f32[32,3,8,128]{3,2,1,0:T(8,128)}, f32[32,3,8,128]{3,2,1,0:T(8,128)}, u32[]{:S(2)}, u32[]{:S(2)}) collective-permute-start(f32[32,3,8,128]{3,2,1,0:T(8,128)} %shard_map.37.own), channel_id=1, source_target_pairs={{0,1},{1,2},{2,3},{3,0},{4,5},{5,6},{6,7},{7,4},{8,9},{9,10},{10,1... | collective-permute-start | bytes 1179656 | tf_op jit(solution)/shard_map/ppermute | solution.py:305
  100.5 0.7 copy-start.1

commit v17 on v14

--- a/solution.py
+++ b/solution.py
@@ -165,44 +165,36 @@
     )(position, *([incoming] * group), noise)
 
 
-def edges_kernel(pos_ref, *refs):
-    group = (len(refs) - 3) // 2
-    left_rows, right_rows = refs[:group], refs[group:2 * group]
-    noise_left, noise_right, own = refs[2 * group:]
+def edges_kernel(pos_ref, inc, noise_left, noise_right, own):
     rows = own.shape[-2]
+    cols = inc.shape[-1]
     lane = lax.broadcasted_iota(jnp.int32, (rows, LANES), 1)
     keep_left = (lane < 2 * STEPS) | (lane >= LANES - STEPS)
-    for k in range(group):
+    for k in range(own.shape[0]):
+        row = pos_ref[k]
         for f in range(3):
-            left = left_rows[k][0, f] + noise_left[k, f]
-            right = pltpu.roll(right_rows[k][0, f] + noise_right[k, f], LANES // 2, 1)
-            own[k, f] = jnp.where(keep_left, left, right)
+            left = inc[row, f, :, pl.ds(0, LANES)] + noise_left[k, f]
+            right = inc[row, f, :, pl.ds(cols - LANES, LANES)] + noise_right[k, f]
+            own[k, f] = jnp.where(keep_left, left, pltpu.roll(right, LANES // 2, 1))
 
 
 def edge_blocks(position, incoming, noise):
     per_dev, nf, rows, cols = noise.shape
     last = cols // LANES - 1
-    group = GATHER_GROUP if per_dev % GATHER_GROUP == 0 else 1
-
-    def row_map(k, col):
-        return lambda i, pos: (pos[i * group + k], 0, 0, col)
-
-    left_specs = [pl.BlockSpec((1, nf, rows, LANES), row_map(k, 0)) for k in range(group)]
-    right_specs = [pl.BlockSpec((1, nf, rows, LANES), row_map(k, last)) for k in range(group)]
-    left = pl.BlockSpec((group, nf, rows, LANES), lambda i, pos: (i, 0, 0, 0))
-    right = pl.BlockSpec((group, nf, rows, LANES), lambda i, pos: (i, 0, 0, last))
-    out = pl.BlockSpec((group, nf, rows, LANES), lambda i, pos: (i, 0, 0, 0))
+    whole = pl.BlockSpec(incoming.shape, lambda i, pos: (0, 0, 0, 0))
+    left = pl.BlockSpec((per_dev, nf, rows, LANES), lambda i, pos: (0, 0, 0, 0))
+    right = pl.BlockSpec((per_dev, nf, rows, LANES), lambda i, pos: (0, 0, 0, last))
     grid_spec = pltpu.PrefetchScalarGridSpec(
         num_scalar_prefetch=1,
-        grid=(per_dev // group,),
-        in_specs=left_specs + right_specs + [left, right],
-        out_specs=out,
+        grid=(1,),
+        in_specs=[whole, left, right],
+        out_specs=left,
     )
     return pl.pallas_call(
         edges_kernel,
         grid_spec=grid_spec,
         out_shape=jax.ShapeDtypeStruct((per_dev, nf, rows, LANES), noise.dtype),
-    )(position, *([incoming] * (2 * group)), noise, noise)
+    )(position, incoming, noise, noise)
 
 
 def edge_kernel(own, from_left, from_right, body, out, patch, first_buf, last_buf, sems):

time: 104 us -> 104 us (level)
  no operation moved by 1% of the time
where the time goes in v17:
time: 104 us; the launch traced here: 103 us
  waiting for transfers between devices  70.3 us (68%)
  Pallas kernels  19.6 us (19%)
  starting transfers between devices  7.79 us (7%)
  local copies, waits for them, and re-layouts  4.21 us (4%)
  other arithmetic  1.36 us (1%)
    all_to_all x1, waiting for transfers between devices, shards(): lax.all_to_all(outgoing, 'ens', split_axis=0, concat_axis=0, tiled=True)  70.3 us
    pallas_call x1, Pallas kernels, main_forecast(): pl.pallas_call(main_kernel, grid_spec=grid_spec, out_shape=jax.ShapeDtype...  11.8 us
    all_to_all x1, starting transfers between devices, shards(): lax.all_to_all(outgoing, 'ens', split_axis=0, concat_axis=0, tiled=True)  7.28 us
    pallas_call x1, Pallas kernels, edge_fix(): pl.pallas_call(edge_kernel, in_specs=[whole, whole, whole, raw], out_spec...  4.18 us
    pallas_call x1, Pallas kernels, edge_blocks(): pl.pallas_call(edges_kernel, grid_spec=grid_spec, out_shape=jax.ShapeDtyp...  3.64 us
    gather x1, local copies, waits for them, and re-layouts, shards(): outgoing = jnp.take(state, send_index, axis=0, mode='clip')  2.41 us
  transfers between devices with their start and end apart: 3, of which 1 were waited for; matrix products, arithmetic and copies ran while one was open for 1% of the time, Pallas kernels for 11%

profile of v17, /device:TPU:0, one launch (start us, length us, event | category | flops | bytes accessed | tf_op | source)
XLA Modules:
  0.0 103.3 jit_solution(12765591577093710791)
XLA Ops:
  0.0 0.0 copy-start
  0.0 0.9 reshape.117
  0.9 0.3 and_reduce_fusion
  1.3 0.3 convert_reduce_fusion
  1.6 0.2 select_reduce_fusion
  1.7 0.1 copy.5
  1.8 0.1 reshape.120
  1.9 0.0 copy-done
  1.9 2.4 %gather_fusion = f32[32,3,8,1024]{3,2,1,0:T(8,128)} fusion(f32[32,3,8,1024]{3,2,1,0:T(8,128)S(1)} %copy-done, s32[1024]{0:T(1024)S(1)} %pad_clamp_fusion), kind=kCustom, calls=%fused_computation | custom fusion | bytes 6291584 | tf_op jit(solution)/shard_map/jit(_take)/gather | solution.py:285
  4.3 7.3 %all-to-all-start = ((f32[32,3,8,1024]{3,2,1,0:T(8,128)}), f32[32,3,8,1024]{3,2,1,0:T(8,128)}, u32[]{:S(2)}, u32[]{:S(2)}) async-start(f32[32,3,8,1024]{3,2,1,0:T(8,128)} %gather_fusion), calls=%async_computation | async-start | bytes 6291456 | tf_op jit(solution)/shard_map/all_to_all | solution.py:286
  11.6 0.5 add_bitcast_fusion.pos_ref
  12.2 70.3 %all-to-all-done.inc.refs_0_.refs_1_.refs_2_.refs_3_.refs_4_.refs_5_.refs_6_.refs_7_ = f32[32,3,8,1024]{3,2,1,0:T(8,128)} async-done(((f32[32,3,8,1024]{3,2,1,0:T(8,128)}), f32[32,3,8,1024]{3,2,1,0:T(8,128)}, u32[]{:S(2)}, u32[]{:S(2)}) %all-to-all-start) | async-done | bytes 3145760 | tf_op jit(solution)/shard_map/all_to_all | solution.py:286
  82.4 3.6 %shard_map.37.own = f32[32,3,8,128]{3,2,1,0:T(8,128)} custom-call(s32[32]{0:T(128)} %add_bitcast_fusion.pos_ref, f32[32,3,8,1024]{3,2,1,0:T(8,128)} %all-to-all-done.inc.refs_0_.refs_1_.refs_2_.refs_3_.refs_4_.refs_5_.refs_6_.refs_7_, f32[32,3,8,1024]{3,2,1,0:T(8,128)} %refs_8_.1, f32[32,3,8,1024]{3,2,1,0:T(8,128)} %refs_8_.1), custom_call_target="tpu_custom_call" | custom-call | tf_op jit(solution)/shard_map/pallas_call | solution.py:193
  86.1 0.0 collective-permute-start.1
  86.1 0.5 collective-permute-start
  86.6 11.8 %shard_map.38.body = f32[32,3,8,1024]{3,2,1,0:T(8,128)} custom-call(s32[32]{0:T(128)} %add_bitcast_fusion.pos_ref, f32[32,3,8,1024]{3,2,1,0:T(8,128)} %all-to-all-done.inc.refs_0_.refs_1_.refs_2_.refs_3_.refs_4_.refs_5_.refs_6_.refs_7_, f32[32,3,8,1024]{3,2,1,0:T(8,128)} %all-to-all-done.inc.refs_0_.refs_1_.refs_2_.refs_3_.refs_4_.refs_5_.refs_6_.refs_7_, ...), custom_call_target="tpu_custom_call" | custom-call | tf_op jit(solution)/shard_map/pallas_call | solution.py:161
  98.4 0.0 collective-permute-done.1.from_right
  98.4 0.0 copy-start.1
  98.4 0.0 collective-permute-done.from_left
  98.4 0.7 copy-done.1
  99.1 4.2 %shard_map.39 = f32[32,3,8,1024]{3,2,1,0:T(8,128)} custom-call(f32[32,3,8,128]{3,2,1,0:T(8,128)} %shard_map.37.own, f32[32,3,8,128]{3,2,1,0:T(8,128)} %collective-permute-done.from_left, f32[32,3,8,128]{3,2,1,0:T(8,128)} %copy-done.1, f32[32,3,8,1024]{3,2,1,0:T(8,128)} %shard_map.38.body), custom_call_target="tpu_custom_call", output_to_operand_aliasing={{}: (3, {})} | custom-call | tf_op jit(solution)/shard_map/pallas_call | solution.py:264
  (4 shorter events, 0.0 us)
Async XLA Ops:
  0.0 1.9 %copy-start = (f32[32,3,8,1024]{3,2,1,0:T(8,128)S(1)}, f32[32,3,8,1024]{3,2,1,0:T(8,128)}, u32[]{:S(2)}) copy-start(f32[32,3,8,1024]{3,2,1,0:T(8,128)} %param.3) | copy-start | bytes 9437188
  4.3 78.1 %all-to-all-start = ((f32[32,3,8,1024]{3,2,1,0:T(8,128)}), f32[32,3,8,1024]{3,2,1,0:T(8,128)}, u32[]{:S(2)}, u32[]{:S(2)}) async-start(f32[32,3,8,1024]{3,2,1,0:T(8,128)} %gather_fusion), calls=%async_computation | async-start | bytes 6291456 | tf_op jit(solution)/shard_map/all_to_all | solution.py:286
  86.1 12.3 %collective-permute-start.1 = (f32[32,3,8,128]{3,2,1,0:T(8,128)}, f32[32,3,8,128]{3,2,1,0:T(8,128)S(1)}, u32[]{:S(2)}, u32[]{:S(2)}) collective-permute-start(f32[32,3,8,128]{3,2,1,0:T(8,128)} %shard_map.37.own), channel_id=1, source_target_pairs={{0,3},{1,0},{2,1},{3,2},{4,7},{5,4},{6,5},{7,6},{8,11},{9,8},{10,9... | collective-permute-start | bytes 1179656 | tf_op jit(solution)/shard_map/ppermute | solution.py:290
  86.1 12.3 %collective-permute-start = (f32[32,3,8,128]{3,2,1,0:T(8,128)}, f32[32,3,8,128]{3,2,1,0:T(8,128)}, u32[]{:S(2)}, u32[]{:S(2)}) collective-permute-start(f32[32,3,8,128]{3,2,1,0:T(8,128)} %shard_map.37.own), channel_id=1, source_target_pairs={{0,1},{1,2},{2,3},{3,0},{4,5},{5,6},{6,7},{7,4},{8,9},{9,10},{10,1... | collective-permute-start | bytes 1179656 | tf_op jit(solution)/shard_map/ppermute | solution.py:289
  98.4 0.7 copy-start.1

commit v18 on v14

--- a/solution.py
+++ b/solution.py
@@ -166,22 +166,21 @@
 
 
 def edges_kernel(pos_ref, *refs):
-    group = (len(refs) - 3) // 2
+    group = (len(refs) - 2) // 2
     left_rows, right_rows = refs[:group], refs[group:2 * group]
-    noise_left, noise_right, own = refs[2 * group:]
+    noise_packed, own = refs[2 * group:]
     rows = own.shape[-2]
     lane = lax.broadcasted_iota(jnp.int32, (rows, LANES), 1)
     keep_left = (lane < 2 * STEPS) | (lane >= LANES - STEPS)
     for k in range(group):
         for f in range(3):
-            left = left_rows[k][0, f] + noise_left[k, f]
-            right = pltpu.roll(right_rows[k][0, f] + noise_right[k, f], LANES // 2, 1)
-            own[k, f] = jnp.where(keep_left, left, right)
-
-
-def edge_blocks(position, incoming, noise):
-    per_dev, nf, rows, cols = noise.shape
-    last = cols // LANES - 1
+            right = pltpu.roll(right_rows[k][0, f], LANES // 2, 1)
+            own[k, f] = jnp.where(keep_left, left_rows[k][0, f], right) + noise_packed[k, f]
+
+
+def edge_blocks(position, incoming, noise_packed):
+    per_dev, nf, rows, _ = noise_packed.shape
+    last = incoming.shape[-1] // LANES - 1
     group = GATHER_GROUP if per_dev % GATHER_GROUP == 0 else 1
 
     def row_map(k, col):
@@ -189,20 +188,24 @@
 
     left_specs = [pl.BlockSpec((1, nf, rows, LANES), row_map(k, 0)) for k in range(group)]
     right_specs = [pl.BlockSpec((1, nf, rows, LANES), row_map(k, last)) for k in range(group)]
-    left = pl.BlockSpec((group, nf, rows, LANES), lambda i, pos: (i, 0, 0, 0))
-    right = pl.BlockSpec((group, nf, rows, LANES), lambda i, pos: (i, 0, 0, last))
-    out = pl.BlockSpec((group, nf, rows, LANES), lambda i, pos: (i, 0, 0, 0))
+    packed = pl.BlockSpec((group, nf, rows, LANES), lambda i, pos: (i, 0, 0, 0))
     grid_spec = pltpu.PrefetchScalarGridSpec(
         num_scalar_prefetch=1,
         grid=(per_dev // group,),
-        in_specs=left_specs + right_specs + [left, right],
-        out_specs=out,
+        in_specs=left_specs + right_specs + [packed],
+        out_specs=packed,
     )
     return pl.pallas_call(
         edges_kernel,
         grid_spec=grid_spec,
-        out_shape=jax.ShapeDtypeStruct((per_dev, nf, rows, LANES), noise.dtype),
-    )(position, *([incoming] * (2 * group)), noise, noise)
+        out_shape=jax.ShapeDtypeStruct(noise_packed.shape, noise_packed.dtype),
+    )(position, *([incoming] * (2 * group)), noise_packed)
+
+
+def pack_edges(a):
+    lane = lax.broadcasted_iota(jnp.int32, a.shape[:-1] + (LANES,), a.ndim - 1)
+    keep_left = (lane < 2 * STEPS) | (lane >= LANES - STEPS)
+    return jnp.where(keep_left, a[..., :LANES], jnp.roll(a[..., -LANES:], LANES // 2, axis=-1))
 
 
 def edge_kernel(own, from_left, from_right, body, out, patch, first_buf, last_buf, sems):
@@ -292,7 +295,7 @@
     send_index, position = routing(parents, count, per_dev, dist, me)
     outgoing = jnp.take(state, send_index, axis=0, mode="clip")
     incoming = lax.all_to_all(outgoing, "ens", split_axis=0, concat_axis=0, tiled=True)
-    own = edge_blocks(position, incoming, noise)
+    own = edge_blocks(position, incoming, pack_edges(noise))
     ring = lax.axis_size("col")
     from_left = lax.ppermute(own, "col", [(i, (i + 1) % ring) for i in range(ring)])
     from_right = lax.ppermute(own, "col", [(i, (i - 1) % ring) for i in range(ring)])

time: 104 us -> 104 us (level)
  waiting for transfers between devices: 70.3 us -> 67.1 us
  other arithmetic: 1.36 us -> 3.29 us
  local copies, waits for them, and re-layouts: 4.21 us -> 5.5 us
    all_to_all x1, waiting for transfers between devices: 70.3 us -> 67 us  [shards(): lax.all_to_all(outgoing, 'ens', split_axis=0, concat_axis=0, tiled=True)]
    select_n x0 -> x1, other arithmetic: none -> 1.92 us  [pack_edges(): jnp.where(keep_left, a[..., :LANES], jnp.roll(a[..., -LANES:], LANES // 2...]
    slice x0 -> x1, local copies, waits for them, and re-layouts: none -> 1.29 us  [pack_edges(): jnp.roll(a[..., -LANES:], LANES // 2, axis=-1)]
  transfers between devices with their start and end apart: 3 -> 3, of which waited for: 1 -> 1; matrix products, arithmetic and copies ran while one was open for 1% -> 4% of each run, Pallas kernels for 11% -> 11%
where the time goes in v18:
time: 104 us; the launch traced here: 103 us
  waiting for transfers between devices  67.1 us (65%)
  Pallas kernels  18.9 us (18%)
  starting transfers between devices  7.83 us (8%)
  local copies, waits for them, and re-layouts  5.5 us (5%)
  other arithmetic  3.29 us (3%)
    all_to_all x1, waiting for transfers between devices, shards(): lax.all_to_all(outgoing, 'ens', split_axis=0, concat_axis=0, tiled=True)  67 us
    pallas_call x1, Pallas kernels, main_forecast(): pl.pallas_call(main_kernel, grid_spec=grid_spec, out_shape=jax.ShapeDtype...  11.8 us
    all_to_all x1, starting transfers between devices, shards(): lax.all_to_all(outgoing, 'ens', split_axis=0, concat_axis=0, tiled=True)  7.28 us
    pallas_call x1, Pallas kernels, edge_fix(): pl.pallas_call(edge_kernel, in_specs=[whole, whole, whole, raw], out_spec...  4.18 us
    pallas_call x1, Pallas kernels, edge_blocks(): pl.pallas_call(edges_kernel, grid_spec=grid_spec, out_shape=jax.ShapeDtyp...  3 us
    gather x1, local copies, waits for them, and re-layouts, shards(): outgoing = jnp.take(state, send_index, axis=0, mode='clip')  2.41 us
  transfers between devices with their start and end apart: 3, of which 1 were waited for; matrix products, arithmetic and copies ran while one was open for 4% of the time, Pallas kernels for 11%

profile of v18, /device:TPU:0, one launch (start us, length us, event | category | flops | bytes accessed | tf_op | source)
XLA Modules:
  0.0 102.7 jit_solution(1784051878744646963)
XLA Ops:
  0.0 0.0 copy-start
  0.0 0.9 reshape.117
  0.9 0.3 and_reduce_fusion
  1.3 0.3 convert_reduce_fusion
  1.6 0.2 select_reduce_fusion
  1.7 0.1 copy.5
  1.8 0.1 reshape.120
  1.9 0.0 copy-done
  1.9 2.4 %gather_fusion = f32[32,3,8,1024]{3,2,1,0:T(8,128)} fusion(f32[32,3,8,1024]{3,2,1,0:T(8,128)S(1)} %copy-done, s32[1024]{0:T(1024)S(1)} %pad_clamp_fusion), kind=kCustom, calls=%fused_computation | custom fusion | bytes 6291584 | tf_op jit(solution)/shard_map/jit(_take)/gather | solution.py:296
  4.3 7.3 %all-to-all-start = ((f32[32,3,8,1024]{3,2,1,0:T(8,128)}), f32[32,3,8,1024]{3,2,1,0:T(8,128)}, u32[]{:S(2)}, u32[]{:S(2)}) async-start(f32[32,3,8,1024]{3,2,1,0:T(8,128)} %gather_fusion), calls=%async_computation | async-start | bytes 6291456 | tf_op jit(solution)/shard_map/all_to_all | solution.py:297
  11.6 0.5 add_bitcast_fusion.pos_ref
  12.2 1.3 %fusion.3 = (f32[32,3,8,64]{3,2,1,0:T(8,128)S(1)}, f32[32,3,8,64]{3,2,1,0:T(8,128)S(1)}) fusion(f32[32,3,8,1024]{3,2,1,0:T(8,128)} %refs_8_.1), kind=kLoop, calls=%fused_computation.20 | loop fusion | bytes 786432 | tf_op jit(solution)/shard_map/jit(_roll_static)/slice | solution.py:208
  13.5 1.9 %maximum_select_fusion.refs_64_ = f32[32,3,8,128]{3,2,1,0:T(8,128)} fusion(f32[32,3,8,64]{3,2,1,0:T(8,128)S(1)} %get-tuple-element.8, f32[32,3,8,64]{3,2,1,0:T(8,128)S(1)} %get-tuple-element.7, f32[32,3,8,1024]{3,2,1,0:T(8,128)} %refs_8_.1, pred[128]{0:T(512)(128)(4,1)S(1)} %compare_or_fusion), kind=kLoop, calls=%fused_computation.1 | loop fusion | flops 196608 | bytes 1179776 | tf_op jit(solution)/shard_map/jit(_where)/select_n | solution.py:208
  15.4 67.0 %all-to-all-done.refs_0_.refs_1_.refs_2_.refs_3_.refs_4_.refs_5_.refs_6_.refs_7_.refs_8_.refs_9_.refs_10_.refs_11_.refs_12_.refs_13_.refs_14_.refs_15_.refs_16_.refs_17_.refs_18_.refs_19_.refs_20_.refs_21_.refs_22_.refs_23_.refs_24_.refs_25_.refs_26_.refs_27_.refs_28_.refs_29_.refs_30_.refs_31_.refs_32_.refs_33_.refs_34_.refs_35_.refs_36_.refs_37_.refs_38_.refs_39_.refs_40_.refs_41_.refs_42_.refs_43_.refs_44_.refs_45_.refs_46_.refs_47_.refs_48_.refs_49_.refs_50_.refs_51_.refs_52_.refs_53_.refs_54_.refs_55_.refs_56_.refs_57_.refs_58_.refs_59_.refs_60_.refs_61_.refs_62_.refs_63_ = f32[32,3,8,1024]{3,2,1,0:T(8,128)} async-done(((f32[32,3,8,1024]{3,2,1,0:T(8,128)}), ...) | async-done | bytes 3145760 | tf_op jit(solution)/shard_map/all_to_all | solution.py:297
  82.4 3.0 %shard_map.37.own = f32[32,3,8,128]{3,2,1,0:T(8,128)} custom-call(s32[32]{0:T(128)} %add_bitcast_fusion.pos_ref, ...), custom_call_target="tpu_custom_call" | custom-call | tf_op jit(solution)/shard_map/pallas_call | solution.py:198
  85.5 0.1 collective-permute-start.1
  85.5 0.5 collective-permute-start
  86.0 11.8 %shard_map.38.body = f32[32,3,8,1024]{3,2,1,0:T(8,128)} custom-call(s32[32]{0:T(128)} %add_bitcast_fusion.pos_ref, ...), custom_call_target="tpu_custom_call" | custom-call | tf_op jit(solution)/shard_map/pallas_call | solution.py:161
  97.8 0.0 collective-permute-done.1.from_right
  97.8 0.0 copy-start.1
  97.8 0.0 collective-permute-done.from_left
  97.8 0.7 copy-done.1
  98.5 4.2 %shard_map.39 = f32[32,3,8,1024]{3,2,1,0:T(8,128)} custom-call(f32[32,3,8,128]{3,2,1,0:T(8,128)} %shard_map.37.own, f32[32,3,8,128]{3,2,1,0:T(8,128)} %collective-permute-done.from_left, f32[32,3,8,128]{3,2,1,0:T(8,128)} %copy-done.1, f32[32,3,8,1024]{3,2,1,0:T(8,128)} %shard_map.38.body), custom_call_target="tpu_custom_call", output_to_operand_aliasing={{}: (3, {})} | custom-call | tf_op jit(solution)/shard_map/pallas_call | solution.py:275
  (5 shorter events, 0.1 us)
Async XLA Ops:
  0.0 1.9 %copy-start = (f32[32,3,8,1024]{3,2,1,0:T(8,128)S(1)}, f32[32,3,8,1024]{3,2,1,0:T(8,128)}, u32[]{:S(2)}) copy-start(f32[32,3,8,1024]{3,2,1,0:T(8,128)} %param.3) | copy-start | bytes 9437188
  4.3 78.1 %all-to-all-start = ((f32[32,3,8,1024]{3,2,1,0:T(8,128)}), f32[32,3,8,1024]{3,2,1,0:T(8,128)}, u32[]{:S(2)}, u32[]{:S(2)}) async-start(f32[32,3,8,1024]{3,2,1,0:T(8,128)} %gather_fusion), calls=%async_computation | async-start | bytes 6291456 | tf_op jit(solution)/shard_map/all_to_all | solution.py:297
  85.5 12.3 %collective-permute-start.1 = (f32[32,3,8,128]{3,2,1,0:T(8,128)}, f32[32,3,8,128]{3,2,1,0:T(8,128)S(1)}, u32[]{:S(2)}, u32[]{:S(2)}) collective-permute-start(f32[32,3,8,128]{3,2,1,0:T(8,128)} %shard_map.37.own), channel_id=1, source_target_pairs={{0,3},{1,0},{2,1},{3,2},{4,7},{5,4},{6,5},{7,6},{8,11},{9,8},{10,9... | collective-permute-start | bytes 1179656 | tf_op jit(solution)/shard_map/ppermute | solution.py:301
  85.5 12.3 %collective-permute-start = (f32[32,3,8,128]{3,2,1,0:T(8,128)}, f32[32,3,8,128]{3,2,1,0:T(8,128)}, u32[]{:S(2)}, u32[]{:S(2)}) collective-permute-start(f32[32,3,8,128]{3,2,1,0:T(8,128)} %shard_map.37.own), channel_id=1, source_target_pairs={{0,1},{1,2},{2,3},{3,0},{4,5},{5,6},{6,7},{7,4},{8,9},{9,10},{10,1... | collective-permute-start | bytes 1179656 | tf_op jit(solution)/shard_map/ppermute | solution.py:300
  97.8 0.7 copy-start.1

commit v19 on v18

--- a/solution.py
+++ b/solution.py
@@ -35,7 +35,14 @@
     send_index = jnp.sum(pick.astype(jnp.int32) * local[:, None, :], axis=2).reshape(-1)
     my_owner = lax.dynamic_index_in_dim(owner, me, 0, keepdims=False)
     my_slot = lax.dynamic_index_in_dim(slot, me, 0, keepdims=False)
-    return send_index, my_owner * dist + my_slot
+    my_first = lax.dynamic_index_in_dim(first, me, 0, keepdims=False)
+    position = my_owner * dist + my_slot
+    order = jnp.cumsum(my_first.astype(jnp.int32)) - 1
+    matches = (position[:, None] == position[None, :]) & my_first[None, :]
+    which = jnp.sum(jnp.where(matches, order[None, :], 0), axis=1)
+    distinct = jnp.arange(per_dev // 2, dtype=jnp.int32)
+    unique = jnp.sum(jnp.where(my_first[None, :] & (order[None, :] == distinct[:, None]), position[None, :], 0), axis=1)
+    return send_index, position, unique, which
 
 
 def update(e, u, v, xp, xm):
@@ -165,41 +172,46 @@
     )(position, *([incoming] * group), noise)
 
 
-def edges_kernel(pos_ref, *refs):
-    group = (len(refs) - 2) // 2
-    left_rows, right_rows = refs[:group], refs[group:2 * group]
-    noise_packed, own = refs[2 * group:]
+def edges_kernel(unique_ref, which_ref, *refs):
+    count = (len(refs) - 3) // 2
+    left_rows, right_rows = refs[:count], refs[count:2 * count]
+    noise_packed, own, stage = refs[2 * count:]
     rows = own.shape[-2]
     lane = lax.broadcasted_iota(jnp.int32, (rows, LANES), 1)
     keep_left = (lane < 2 * STEPS) | (lane >= LANES - STEPS)
-    for k in range(group):
+    for j in range(count):
         for f in range(3):
-            right = pltpu.roll(right_rows[k][0, f], LANES // 2, 1)
-            own[k, f] = jnp.where(keep_left, left_rows[k][0, f], right) + noise_packed[k, f]
-
-
-def edge_blocks(position, incoming, noise_packed):
+            right = pltpu.roll(right_rows[j][0, f], LANES // 2, 1)
+            stage[j, f] = jnp.where(keep_left, left_rows[j][0, f], right)
+    for k in range(own.shape[0]):
+        row = which_ref[k]
+        for f in range(3):
+            own[k, f] = stage[row, f] + noise_packed[k, f]
+
+
+def edge_blocks(unique, which, incoming, noise_packed):
     per_dev, nf, rows, _ = noise_packed.shape
     last = incoming.shape[-1] // LANES - 1
-    group = GATHER_GROUP if per_dev % GATHER_GROUP == 0 else 1
-
-    def row_map(k, col):
-        return lambda i, pos: (pos[i * group + k], 0, 0, col)
-
-    left_specs = [pl.BlockSpec((1, nf, rows, LANES), row_map(k, 0)) for k in range(group)]
-    right_specs = [pl.BlockSpec((1, nf, rows, LANES), row_map(k, last)) for k in range(group)]
-    packed = pl.BlockSpec((group, nf, rows, LANES), lambda i, pos: (i, 0, 0, 0))
+    count = unique.shape[0]
+
+    def row_map(j, col):
+        return lambda i, uniq, wh: (uniq[j], 0, 0, col)
+
+    left_specs = [pl.BlockSpec((1, nf, rows, LANES), row_map(j, 0)) for j in range(count)]
+    right_specs = [pl.BlockSpec((1, nf, rows, LANES), row_map(j, last)) for j in range(count)]
+    packed = pl.BlockSpec((per_dev, nf, rows, LANES), lambda i, uniq, wh: (0, 0, 0, 0))
     grid_spec = pltpu.PrefetchScalarGridSpec(
-        num_scalar_prefetch=1,
-        grid=(per_dev // group,),
+        num_scalar_prefetch=2,
+        grid=(1,),
         in_specs=left_specs + right_specs + [packed],
         out_specs=packed,
+        scratch_shapes=[pltpu.VMEM((count, nf, rows, LANES), jnp.float32)],
     )
     return pl.pallas_call(
         edges_kernel,
         grid_spec=grid_spec,
         out_shape=jax.ShapeDtypeStruct(noise_packed.shape, noise_packed.dtype),
-    )(position, *([incoming] * (2 * group)), noise_packed)
+    )(unique, which, *([incoming] * (2 * count)), noise_packed)
 
 
 def pack_edges(a):
@@ -292,10 +304,10 @@
     me = lax.axis_index("ens")
     per_dev = state.shape[0]
     dist = max(1, -(-per_dev // count))
-    send_index, position = routing(parents, count, per_dev, dist, me)
+    send_index, position, unique, which = routing(parents, count, per_dev, dist, me)
     outgoing = jnp.take(state, send_index, axis=0, mode="clip")
     incoming = lax.all_to_all(outgoing, "ens", split_axis=0, concat_axis=0, tiled=True)
-    own = edge_blocks(position, incoming, pack_edges(noise))
+    own = edge_blocks(unique, which, incoming, pack_edges(noise))
     ring = lax.axis_size("col")
     from_left = lax.ppermute(own, "col", [(i, (i + 1) % ring) for i in range(ring)])
     from_right = lax.ppermute(own, "col", [(i, (i - 1) % ring) for i in range(ring)])

time: 104 us -> 104 us (level)
  waiting for transfers between devices: 67.1 us -> 65.9 us
    reduce_sum x0 -> x2, other arithmetic: none -> 1.39 us  [the longest x1 0.72 us: routing(): which = jnp.sum(jnp.where(matches, order[None, :], 0), axis=1)]
    all_to_all x1, waiting for transfers between devices: 67 us -> 65.9 us  [shards(): lax.all_to_all(outgoing, 'ens', split_axis=0, concat_axis=0, tiled=True)]
  transfers between devices with their start and end apart: 3 -> 3, of which waited for: 1 -> 1; matrix products, arithmetic and copies ran while one was open for 4% -> 5% of each run, Pallas kernels for 11% -> 11%
where the time goes in v19:
time: 104 us; the launch traced here: 103 us
  waiting for transfers between devices  65.9 us (63%)
  Pallas kernels  18.8 us (18%)
  starting transfers between devices  7.83 us (8%)
  local copies, waits for them, and re-layouts  5.6 us (5%)
  other arithmetic  4.31 us (4%)
    all_to_all x1, waiting for transfers between devices, shards(): lax.all_to_all(outgoing, 'ens', split_axis=0, concat_axis=0, tiled=True)  65.9 us
    pallas_call x1, Pallas kernels, main_forecast(): pl.pallas_call(main_kernel, grid_spec=grid_spec, out_shape=jax.ShapeDtype...  11.8 us
    all_to_all x1, starting transfers between devices, shards(): lax.all_to_all(outgoing, 'ens', split_axis=0, concat_axis=0, tiled=True)  7.28 us
    pallas_call x1, Pallas kernels, edge_fix(): pl.pallas_call(edge_kernel, in_specs=[whole, whole, whole, raw], out_spec...  4.18 us
    pallas_call x1, Pallas kernels, edge_blocks(): pl.pallas_call(edges_kernel, grid_spec=grid_spec, out_shape=jax.ShapeDtyp...  2.84 us
    gather x1, local copies, waits for them, and re-layouts, shards(): outgoing = jnp.take(state, send_index, axis=0, mode='clip')  2.41 us
  transfers between devices with their start and end apart: 3, of which 1 were waited for; matrix products, arithmetic and copies ran while one was open for 5% of the time, Pallas kernels for 11%

profile of v19, /device:TPU:0, one launch (start us, length us, event | category | flops | bytes accessed | tf_op | source)
XLA Modules:
  0.0 102.5 jit_solution(17597373923620816407)
XLA Ops:
  0.0 0.9 eq.79
  0.9 0.3 and_reduce_fusion
  1.3 0.3 convert_reduce_fusion
  1.6 0.2 select_reduce_fusion
  1.7 0.1 copy.8
  1.8 0.1 reshape.159
  1.9 2.4 %gather_fusion = f32[32,3,8,1024]{3,2,1,0:T(8,128)} fusion(f32[32,3,8,1024]{3,2,1,0:T(8,128)S(1)} %copy-done, s32[1024]{0:T(1024)S(1)} %pad_clamp_fusion), kind=kCustom, calls=%fused_computation | custom fusion | bytes 6291584 | tf_op jit(solution)/shard_map/jit(_take)/gather | solution.py:308
  4.3 7.3 %all-to-all-start = ((f32[32,3,8,1024]{3,2,1,0:T(8,128)}), f32[32,3,8,1024]{3,2,1,0:T(8,128)}, u32[]{:S(2)}, u32[]{:S(2)}) async-start(f32[32,3,8,1024]{3,2,1,0:T(8,128)} %gather_fusion), calls=%async_computation | async-start | bytes 6291456 | tf_op jit(solution)/shard_map/all_to_all | solution.py:309
  11.6 0.1 copy.7
  11.7 0.1 reduce-window.8
  11.8 0.1 add_reduce_fusion
  11.9 0.7 select_reduce_fusion.2.unique_ref
  12.6 0.7 select_reduce_fusion.1.which_ref
  13.3 1.3 %fusion.8 = (f32[32,3,8,64]{3,2,1,0:T(8,128)S(1)}, f32[32,3,8,64]{3,2,1,0:T(8,128)S(1)}) fusion(f32[32,3,8,1024]{3,2,1,0:T(8,128)} %refs_8_.1), kind=kLoop, calls=%fused_computation.32 | loop fusion | bytes 786432 | tf_op jit(solution)/shard_map/jit(_roll_static)/slice | solution.py:220
  14.6 1.9 %maximum_select_fusion.refs_32_ = f32[32,3,8,128]{3,2,1,0:T(8,128)} fusion(f32[32,3,8,64]{3,2,1,0:T(8,128)S(1)} %get-tuple-element.8, f32[32,3,8,64]{3,2,1,0:T(8,128)S(1)} %get-tuple-element.7, f32[32,3,8,1024]{3,2,1,0:T(8,128)} %refs_8_.1, pred[128]{0:T(512)(128)(4,1)S(1)} %compare_or_fusion), kind=kLoop, calls=%fused_computation.1 | loop fusion | flops 196608 | bytes 1179776 | tf_op jit(solution)/shard_map/jit(_where)/select_n | solution.py:220
  16.5 65.9 %all-to-all-done.refs_0_.refs_1_.refs_2_.refs_3_.refs_4_.refs_5_.refs_6_.refs_7_.refs_8_.refs_9_.refs_10_.refs_11_.refs_12_.refs_13_.refs_14_.refs_15_.refs_16_.refs_17_.refs_18_.refs_19_.refs_20_.refs_21_.refs_22_.refs_23_.refs_24_.refs_25_.refs_26_.refs_27_.refs_28_.refs_29_.refs_30_.refs_31_ = f32[32,3,8,1024]{3,2,1,0:T(8,128)} async-done(((f32[32,3,8,1024]{3,2,1,0:T(8,128)}), ...) | async-done | bytes 3145760 | tf_op jit(solution)/shard_map/all_to_all | solution.py:309
  82.4 2.8 %shard_map.37.own = f32[32,3,8,128]{3,2,1,0:T(8,128)} custom-call(s32[16]{0:T(128)} %select_reduce_fusion.2.unique_ref, s32[32]{0:T(128)} %select_reduce_fusion.1.which_ref, ...), custom_call_target="tpu_custom_call" | custom-call | tf_op jit(solution)/shard_map/pallas_call | solution.py:210
  85.3 0.1 collective-permute-start.1
  85.4 0.5 collective-permute-start
  85.9 11.8 %shard_map.38.body = f32[32,3,8,1024]{3,2,1,0:T(8,128)} custom-call(s32[32]{0:T(128)} %copy-done.2, ...), custom_call_target="tpu_custom_call" | custom-call | tf_op jit(solution)/shard_map/pallas_call | solution.py:168
  97.6 0.0 collective-permute-done.1.from_right
  97.6 0.0 collective-permute-done.from_left
  97.6 0.7 copy-done.1
  98.4 4.2 %shard_map.39 = f32[32,3,8,1024]{3,2,1,0:T(8,128)} custom-call(f32[32,3,8,128]{3,2,1,0:T(8,128)} %shard_map.37.own, f32[32,3,8,128]{3,2,1,0:T(8,128)} %collective-permute-done.from_left, f32[32,3,8,128]{3,2,1,0:T(8,128)} %copy-done.1, f32[32,3,8,1024]{3,2,1,0:T(8,128)} %shard_map.38.body), custom_call_target="tpu_custom_call", output_to_operand_aliasing={{}: (3, {})} | custom-call | tf_op jit(solution)/shard_map/pallas_call | solution.py:287
  (12 shorter events, 0.1 us)
Async XLA Ops:
  0.0 1.9 %copy-start = (f32[32,3,8,1024]{3,2,1,0:T(8,128)S(1)}, f32[32,3,8,1024]{3,2,1,0:T(8,128)}, u32[]{:S(2)}) copy-start(f32[32,3,8,1024]{3,2,1,0:T(8,128)} %param.3) | copy-start | bytes 9437188
  4.3 78.1 %all-to-all-start = ((f32[32,3,8,1024]{3,2,1,0:T(8,128)}), f32[32,3,8,1024]{3,2,1,0:T(8,128)}, u32[]{:S(2)}, u32[]{:S(2)}) async-start(f32[32,3,8,1024]{3,2,1,0:T(8,128)} %gather_fusion), calls=%async_computation | async-start | bytes 6291456 | tf_op jit(solution)/shard_map/all_to_all | solution.py:309
  11.8 73.5 %copy-start.2 = (s32[32]{0:T(128)}, s32[32]{0:T(128)S(1)}, u32[]{:S(2)}) copy-start(s32[32]{0:T(128)S(1)} %fusion.6.pos_ref) | copy-start | bytes 388
  85.3 12.3 %collective-permute-start.1 = (f32[32,3,8,128]{3,2,1,0:T(8,128)}, f32[32,3,8,128]{3,2,1,0:T(8,128)S(1)}, u32[]{:S(2)}, u32[]{:S(2)}) collective-permute-start(f32[32,3,8,128]{3,2,1,0:T(8,128)} %shard_map.37.own), channel_id=1, source_target_pairs={{0,3},{1,0},{2,1},{3,2},{4,7},{5,4},{6,5},{7,6},{8,11},{9,8},{10,9... | collective-permute-start | bytes 1179656 | tf_op jit(solution)/shard_map/ppermute | solution.py:313
  85.4 12.3 %collective-permute-start = (f32[32,3,8,128]{3,2,1,0:T(8,128)}, f32[32,3,8,128]{3,2,1,0:T(8,128)}, u32[]{:S(2)}, u32[]{:S(2)}) collective-permute-start(f32[32,3,8,128]{3,2,1,0:T(8,128)} %shard_map.37.own), channel_id=1, source_target_pairs={{0,1},{1,2},{2,3},{3,0},{4,5},{5,6},{6,7},{7,4},{8,9},{9,10},{10,1... | collective-permute-start | bytes 1179656 | tf_op jit(solution)/shard_map/ppermute | solution.py:312
  97.6 0.7 copy-start.1
